TPU v7x, 512 devices: a whole 4x8x8 slice. The times are simulated.
512 devices in a mesh: seq: 128 (over z, y, core), head: 4 (over x).
Axes of the slice: x: 4, y: 8, z: 8, core: 2. Of those that a mesh axis runs over, the one named last changes fastest.
Arguments:
- tokens: bfloat16 [16384, 4096], P('seq', 'head'), may hold values from -120 to 120
- shared_weight: bfloat16 [4096, 512], P(None, 'head'), may hold values from -0.75 to 0.75
- value_weight: bfloat16 [4096, 512], P(None, 'head'), may hold values from -0.09375 to 0.09375
- head_grad: bfloat16 [16384, 512], P('seq', 'head'), may hold values from -0.75 to 0.75
- sorted_slot: int32 [4, 16384], P('head', 'seq'), may hold values from 0 to 16383, as said below
Outputs:
- shared_grad: float32 [4096, 512], P('seq', 'head')
- value_grad: float32 [4096, 512], P('seq', 'head')
Inputs may be any that keep to these rules, and one draw needn't show every extreme that they name: For each head, sorted_slot[h] is a permutation of the positions. Of the 128 positions of one device (positions r * 128 to (r+1) * 128 - 1), at most 2 have sorted indices in the range s * 128 to (s+1) * 128 - 1 of one device s, for every head, and in every head some pair r, s reaches 2.
All inputs are finite; a program needn't handle non-finite values.
Results may differ from a plain program's by a relative error of at most 0.006.
The roundings to bfloat16 on the way count: a program that leaves them out, or rounds other values in their place, can miss the bound.
Values may be sent and summed in bfloat16 or wider, within the bound.
No kernel may reach another device: no remote copies, remote signals or barrier semaphores. Data moves between devices by JAX's collectives and lax.ppermute only.
A program may use at most 64 MiB of HBM per device.

v0:
```python
import math

import jax
import jax.numpy as jnp
from jax import lax
from jax.sharding import PartitionSpec as P

GROUP = 64


eps_norm = 1e-06
masked_score = -1000000000.0


def shifted(value, axis, steps):
    count = lax.axis_size(axis)
    pairs = [(source, (source + steps) % count) for source in range(count)]
    return lax.ppermute(value, axis, pairs)


def unit_keys(block):
    block_float = block.astype(jnp.float32)
    norm_rows = jnp.sqrt(jnp.sum(block_float * block_float, axis=1, keepdims=True) + eps_norm)
    return (block_float / norm_rows).astype(jnp.bfloat16)


def per_device(tokens, shared_weight, value_weight, head_grad, sorted_slot):
    whole = lax.all_gather(tokens, "head", axis=1, tiled=True)
    tok_count = whole.shape[0]
    head_width = shared_weight.shape[1]
    peer_count = lax.axis_size("seq")
    capacity = 2 * tok_count // peer_count
    group_count = tok_count // GROUP
    tail_start = tok_count - GROUP
    scale_factor = 1.0 / math.sqrt(head_width)
    query = jnp.dot(whole, shared_weight, preferred_element_type=jnp.float32).astype(jnp.bfloat16)
    values = jnp.dot(whole, value_weight, preferred_element_type=jnp.float32).astype(jnp.bfloat16)
    slot_ids = sorted_slot[0]
    target = slot_ids // tok_count
    local_slot = slot_ids - target * tok_count
    peer_ids = jnp.arange(peer_count, dtype=jnp.int32)
    row_ids = jnp.arange(tok_count, dtype=jnp.int32)
    earlier_rows = (row_ids[:, None] > row_ids[None, :]).astype(jnp.bfloat16)
    every_row = jnp.ones((tok_count,), dtype=bool)
    one_hot = ((target[:, None] == peer_ids[None, :]) & every_row[:, None]).astype(jnp.bfloat16)
    before = jnp.dot(earlier_rows, one_hot, preferred_element_type=jnp.float32)
    buffer_index = target * capacity + jnp.sum(before * one_hot.astype(jnp.float32), axis=1).astype(
        jnp.int32
    )
    payload = jnp.concatenate([query, values, head_grad], axis=1)
    send_rows = (
        jnp.zeros((peer_count * capacity, 3 * head_width), jnp.bfloat16)
        .at[buffer_index]
        .set(payload)
    )
    send_slots = (
        jnp.full((peer_count * capacity,), tok_count, jnp.int32).at[buffer_index].set(local_slot)
    )
    recv_rows, recv_slots = (
        lax.all_to_all(send_rows, "seq", split_axis=0, concat_axis=0, tiled=True),
        lax.all_to_all(send_slots, "seq", split_axis=0, concat_axis=0, tiled=True),
    )
    sorted_rows = (
        jnp.zeros((tok_count, 3 * head_width), jnp.bfloat16)
        .at[recv_slots]
        .set(recv_rows, mode="drop")
    )
    halo_rows = shifted(sorted_rows[tail_start:, : 2 * head_width], "seq", 1)
    sorted_query = sorted_rows[:, :head_width]
    own_keys = unit_keys(sorted_query).reshape(group_count, GROUP, head_width)
    halo_keys = unit_keys(halo_rows[:, :head_width])
    q_blocks = sorted_query.reshape(group_count, GROUP, head_width)
    v_blocks = sorted_rows[:, head_width : 2 * head_width].reshape(group_count, GROUP, head_width)
    g_blocks = sorted_rows[:, 2 * head_width :].reshape(group_count, GROUP, head_width)
    prev_keys = jnp.concatenate([halo_keys[None], own_keys[:-1]], axis=0)
    prev_values = jnp.concatenate([halo_rows[None, :, head_width:], v_blocks[:-1]], axis=0)
    key_window = jnp.concatenate([own_keys, prev_keys], axis=1)
    value_window = jnp.concatenate([v_blocks, prev_values], axis=1)
    scores = (
        jnp.einsum("cqd,ckd->cqk", q_blocks, key_window, preferred_element_type=jnp.float32)
        * scale_factor
    )
    self_mask = jnp.arange(GROUP)[:, None] == jnp.arange(2 * GROUP)[None, :]
    scores = jnp.where(self_mask[None], masked_score, scores)
    probs = jax.nn.softmax(scores, axis=-1)
    dprob = jnp.einsum("cqd,ckd->cqk", g_blocks, value_window, preferred_element_type=jnp.float32)
    dscore = probs * (dprob - jnp.sum(probs * dprob, axis=-1, keepdims=True))
    probs_low = probs.astype(jnp.bfloat16)
    dscore_low = dscore.astype(jnp.bfloat16)
    dquery = (
        jnp.einsum("cqk,ckd->cqd", dscore_low, key_window, preferred_element_type=jnp.float32)
        * scale_factor
    )
    dkey_window = (
        jnp.einsum("cqk,cqd->ckd", dscore_low, q_blocks, preferred_element_type=jnp.float32)
        * scale_factor
    )
    dvalue_window = jnp.einsum(
        "cqk,cqd->ckd", probs_low, g_blocks, preferred_element_type=jnp.float32
    )
    grad_window = jnp.concatenate([dkey_window, dvalue_window], axis=-1)
    own_part = grad_window[:, :GROUP]
    later_part = grad_window[1:, GROUP:]
    outgoing = grad_window[0, GROUP:]
    incoming = shifted(outgoing, "seq", -1)
    key_value = own_part + jnp.concatenate([later_part, incoming[None]], axis=0)
    sorted_grads = jnp.concatenate(
        [dquery.reshape(tok_count, head_width), key_value.reshape(tok_count, 2 * head_width)],
        axis=1,
    )
    return_rows = sorted_grads[jnp.minimum(recv_slots, tok_count - 1)]
    back_rows = lax.all_to_all(return_rows, "seq", split_axis=0, concat_axis=0, tiled=True)
    owned = back_rows[buffer_index]
    dquery_p = owned[:, :head_width]
    dkey_p = owned[:, head_width : 2 * head_width]
    dvalue_p = owned[:, 2 * head_width :]
    query_float = query.astype(jnp.float32)
    norm_pos = jnp.sqrt(jnp.sum(query_float * query_float, axis=1, keepdims=True) + eps_norm)
    along = jnp.sum(query_float * dkey_p, axis=1, keepdims=True)
    dshared = dquery_p + dkey_p / norm_pos - query_float * (along / norm_pos**3)
    combined = jnp.concatenate(
        [dshared.astype(jnp.bfloat16), dvalue_p.astype(jnp.bfloat16)], axis=1
    )
    grads = lax.psum_scatter(
        lax.dot_general(
            whole, combined, (((0,), (0,)), ((), ())), preferred_element_type=jnp.float32
        ),
        "seq",
        scatter_dimension=0,
        tiled=True,
    )
    return (grads[:, :head_width], grads[:, head_width:])


def solution(mesh):
    in_specs = (
        P("seq", "head"),
        P(None, "head"),
        P(None, "head"),
        P("seq", "head"),
        P("head", "seq"),
    )
    out_specs = (P("seq", "head"), P("seq", "head"))
    return jax.shard_map(
        per_device, mesh=mesh, in_specs=in_specs, out_specs=out_specs, check_vma=False
    )
```

profile of v0, /device:TPU:6, one launch (start us, length us, event | category | flops | bytes accessed | tf_op | source)
XLA Modules:
  0.0 334.7 jit_solution(2812549587791526192)
XLA Ops:
  9.4 1.0 scatter_custom_fusion
  11.2 17.8 %all-to-all-start = ((s32[128,2,1]{1,2,0:T(1,128)}), s32[128,2,1]{1,2,0:T(1,128)S(1)}, u32[]{:S(2)}, u32[]{:S(2)}) async-start(s32[128,2,1]{1,2,0:T(1,128)} %bitcast.4), calls=%async_computation | async-start | bytes 131072 | tf_op jit(solution)/shard_map/all_to_all | solution.py:61
  29.0 0.9 copy.22
  29.9 12.8 %all-gather.2.cloned.1.call-done = bf16[128,4096]{1,0:T(8,128)(2,1)} async-done(((bf16[128,1024]{1,0:T(8,128)(2,1)}), bf16[128,4096]{1,0:T(8,128)(2,1)}) %all-gather.2.cloned.1.call-update) | async-done | bytes 1048592 | tf_op jit(solution)/shard_map/all_gather | solution.py:28
  42.6 1.7 convolution_convert_fusion.1
  44.4 2.1 convolution_convert_fusion
  46.6 1.1 scatter_custom_fusion.1
  48.5 14.9 %all-to-all-start.1 = ((bf16[128,2,384]{2,1,0:T(2,128)(2,1)}), bf16[128,2,384]{2,1,0:T(2,128)(2,1)S(1)}, u32[]{:S(2)}, u32[]{:S(2)}) async-start(bf16[128,2,384]{2,1,0:T(2,128)(2,1)} %all_to_all.27), calls=%async_computation.1 | async-start | bytes 393216 | tf_op jit(solution)/shard_map/all_to_all | solution.py:60
  63.9 0.8 reduce.3
  64.8 11.9 %all-to-all-done.1 = bf16[128,2,384]{2,1,0:T(2,128)(2,1)S(1)} async-done(((bf16[128,2,384]{2,1,0:T(2,128)(2,1)}), bf16[128,2,384]{2,1,0:T(2,128)(2,1)S(1)}, u32[]{:S(2)}, u32[]{:S(2)}) %all-to-all-start.1) | async-done | bytes 196640 | tf_op jit(solution)/shard_map/all_to_all | solution.py:60
  76.9 1.5 scatter_custom_fusion.2
  78.6 2.0 collective-permute-start
  80.7 6.5 %collective-permute-done = bf16[64,256]{1,0:T(8,128)(2,1)S(1)} collective-permute-done((bf16[64,256]{1,0:T(8,128)(2,1)S(1)}, bf16[64,256]{1,0:T(8,128)(2,1)S(1)}, u32[]{:S(2)}, u32[]{:S(2)}) %collective-permute-start) | collective-permute-done | bytes 32800 | tf_op jit(solution)/shard_map/ppermute | solution.py:18
  88.9 1.9 collective-permute-start.1
  90.9 2.4 collective-permute-done.1
  93.5 1.0 gather_fusion
  94.5 1.0 all_to_all.30
  95.4 8.7 %all-to-all-start.2 = ((f32[128,2,384]{2,1,0:T(2,128)}), f32[128,2,384]{2,1,0:T(2,128)S(1)}, u32[]{:S(2)}, u32[]{:S(2)}) async-start(f32[128,2,384]{2,1,0:T(2,128)} %all_to_all.30), calls=%async_computation.2 | async-start | bytes 786432 | tf_op jit(solution)/shard_map/all_to_all | solution.py:112
  104.2 17.2 %all-to-all-done.2 = f32[128,2,384]{2,1,0:T(2,128)S(1)} async-done(((f32[128,2,384]{2,1,0:T(2,128)}), f32[128,2,384]{2,1,0:T(2,128)S(1)}, u32[]{:S(2)}, u32[]{:S(2)}) %all-to-all-start.2) | async-done | bytes 393248 | tf_op jit(solution)/shard_map/all_to_all | solution.py:112
  121.7 0.8 gather_fusion.1
  122.9 2.7 convolution_bitcast_fusion
  125.6 5.6 %copy.30 = f32[4096,256]{1,0:T(8,128)} copy(f32[4096,256]{0,1:T(8,128)} %convolution_bitcast_fusion) | data formatting | bytes 8388608
  131.2 195.3 %reduce-scatter.4.cloned.1.call-done = f32[32,256]{1,0:T(8,128)} async-done(((f32[4096,256]{1,0:T(8,128)}), f32[32,256]{1,0:T(8,128)}) %reduce-scatter.4.cloned.1.call-update) | async-done | bytes 32784
  326.5 1.3 fusion.50
  (53 shorter events, 7.5 us)
Async XLA Ops:
  7.2 35.5 %copy-start = (bf16[4096,128]{1,0:T(8,128)(2,1)S(1)}, bf16[4096,128]{1,0:T(8,128)(2,1)}, u32[]{:S(2)}) copy-start(bf16[4096,128]{1,0:T(8,128)(2,1)} %param.6) | copy-start | bytes 3145732
  7.2 35.4 %all-gather.2.cloned.1.call-start = ((), (), s32[]{:S(2)}) async-start(), calls=%async_computation.4 | async-start | bytes 1310720 | tf_op jit(solution)/shard_map/all_gather | solution.py:28
  11.2 37.3 %all-to-all-start = ((s32[128,2,1]{1,2,0:T(1,128)}), s32[128,2,1]{1,2,0:T(1,128)S(1)}, u32[]{:S(2)}, u32[]{:S(2)}) async-start(s32[128,2,1]{1,2,0:T(1,128)} %bitcast.4), calls=%async_computation | async-start | bytes 131072 | tf_op jit(solution)/shard_map/all_to_all | solution.py:61
  48.5 28.3 %all-to-all-start.1 = ((bf16[128,2,384]{2,1,0:T(2,128)(2,1)}), bf16[128,2,384]{2,1,0:T(2,128)(2,1)S(1)}, u32[]{:S(2)}, u32[]{:S(2)}) async-start(bf16[128,2,384]{2,1,0:T(2,128)(2,1)} %all_to_all.27), calls=%async_computation.1 | async-start | bytes 393216 | tf_op jit(solution)/shard_map/all_to_all | solution.py:60
  78.6 8.6 %collective-permute-start = (bf16[64,256]{1,0:T(8,128)(2,1)S(1)}, bf16[64,256]{1,0:T(8,128)(2,1)S(1)}, u32[]{:S(2)}, u32[]{:S(2)}) collective-permute-start(bf16[64,256]{1,0:T(8,128)(2,1)S(1)} %slice.79), channel_id=1, source_target_pairs={{0,4},{4,8},{8,12},{12,16},{16,20},{20,24},{24,28},{28,32},{32,36}... | collective-permute-start | bytes 98312 | tf_op jit(solution)/shard_map/ppermute | solution.py:18
  88.9 4.4 %collective-permute-start.1 = (f32[64,256]{0,1:T(8,128)S(1)}, f32[64,256]{0,1:T(8,128)S(1)}, u32[]{:S(2)}, u32[]{:S(2)}) collective-permute-start(f32[64,256]{0,1:T(8,128)S(1)} %get-tuple-element.13), channel_id=1, source_target_pairs={{0,508},{4,0},{8,4},{12,8},{16,12},{20,16},{24,20},{28,24},{32,28}... | collective-permute-start | bytes 196616 | tf_op jit(solution)/shard_map/ppermute | solution.py:18
  93.5 29.4 %copy-start.1 = (bf16[128,4096]{1,0:T(8,128)(2,1)S(1)}, bf16[128,4096]{1,0:T(8,128)(2,1)}, u32[]{:S(2)}) copy-start(bf16[128,4096]{1,0:T(8,128)(2,1)} %all-gather.2.cloned.1.call-done) | copy-start | bytes 3145732
  95.4 26.0 %all-to-all-start.2 = ((f32[128,2,384]{2,1,0:T(2,128)}), f32[128,2,384]{2,1,0:T(2,128)S(1)}, u32[]{:S(2)}, u32[]{:S(2)}) async-start(f32[128,2,384]{2,1,0:T(2,128)} %all_to_all.30), calls=%async_computation.2 | async-start | bytes 786432 | tf_op jit(solution)/shard_map/all_to_all | solution.py:112
  104.2 222.4 %reduce-scatter.4.cloned.1.call-start = ((), (), s32[]{:S(2)}) async-start(), calls=%async_computation.5 | async-start | bytes 4227072
Sparse Core Ops, SparseCore 0:
  10.1 32.4 all-gather.1
  131.3 195.1 reduce-scatter.3
where the time goes:
time: 335 us
  waiting for transfers between devices  247 us (74%)
  starting transfers between devices  45.4 us (14%)
  local copies, waits for them, and re-layouts  17.2 us (5%)
  between operations  14.4 us (4%)
  matrix products  7.98 us (2%)
    unnamed x3, waiting for transfers between devices  196 us
    all_to_all x1, starting transfers between devices, per_device(): lax.all_to_all(send_slots, 'seq', split_axis=0, concat_axis=0, tiled=True)  17.8 us
    all_to_all x1, waiting for transfers between devices, per_device(): lax.all_to_all(return_rows, 'seq', split_axis=0, concat_axis=0, tiled=True)  17.2 us
    all_to_all x1, starting transfers between devices, per_device(): lax.all_to_all(send_rows, 'seq', split_axis=0, concat_axis=0, tiled=True)  14.9 us
    all_gather x1, waiting for transfers between devices, per_device(): whole = lax.all_gather(tokens, 'head', axis=1, tiled=True)  12.8 us
    all_to_all x1, waiting for transfers between devices, per_device(): lax.all_to_all(send_rows, 'seq', split_axis=0, concat_axis=0, tiled=True)  11.9 us
    ppermute x2, waiting for transfers between devices, shifted(): return lax.ppermute(value, axis, pairs)  8.87 us
    all_to_all x1, starting transfers between devices, per_device(): lax.all_to_all(return_rows, 'seq', split_axis=0, concat_axis=0, tiled=True)  8.7 us
  transfers between devices with their start and end apart: 7, of which 6 were waited for; matrix products, arithmetic and copies ran while one was open for 3% of the time, Pallas kernels for 0%

commit v1 on v0

--- a/solution.py
+++ b/solution.py
@@ -3,9 +3,12 @@
 import jax
 import jax.numpy as jnp
 from jax import lax
+from jax.sharding import Mesh
 from jax.sharding import PartitionSpec as P
 
 GROUP = 64
+
+SEQ = ("z", "y", "c")
 
 
 eps_norm = 1e-06
@@ -27,8 +30,9 @@
 def per_device(tokens, shared_weight, value_weight, head_grad, sorted_slot):
     whole = lax.all_gather(tokens, "head", axis=1, tiled=True)
     tok_count = whole.shape[0]
+    feat_count = whole.shape[1]
     head_width = shared_weight.shape[1]
-    peer_count = lax.axis_size("seq")
+    peer_count = lax.axis_size(SEQ)
     capacity = 2 * tok_count // peer_count
     group_count = tok_count // GROUP
     tail_start = tok_count - GROUP
@@ -57,15 +61,15 @@
         jnp.full((peer_count * capacity,), tok_count, jnp.int32).at[buffer_index].set(local_slot)
     )
     recv_rows, recv_slots = (
-        lax.all_to_all(send_rows, "seq", split_axis=0, concat_axis=0, tiled=True),
-        lax.all_to_all(send_slots, "seq", split_axis=0, concat_axis=0, tiled=True),
+        lax.all_to_all(send_rows, SEQ, split_axis=0, concat_axis=0, tiled=True),
+        lax.all_to_all(send_slots, SEQ, split_axis=0, concat_axis=0, tiled=True),
     )
     sorted_rows = (
         jnp.zeros((tok_count, 3 * head_width), jnp.bfloat16)
         .at[recv_slots]
         .set(recv_rows, mode="drop")
     )
-    halo_rows = shifted(sorted_rows[tail_start:, : 2 * head_width], "seq", 1)
+    halo_rows = shifted(sorted_rows[tail_start:, : 2 * head_width], SEQ, 1)
     sorted_query = sorted_rows[:, :head_width]
     own_keys = unit_keys(sorted_query).reshape(group_count, GROUP, head_width)
     halo_keys = unit_keys(halo_rows[:, :head_width])
@@ -102,45 +106,61 @@
     own_part = grad_window[:, :GROUP]
     later_part = grad_window[1:, GROUP:]
     outgoing = grad_window[0, GROUP:]
-    incoming = shifted(outgoing, "seq", -1)
-    key_value = own_part + jnp.concatenate([later_part, incoming[None]], axis=0)
+    incoming = shifted(outgoing, SEQ, -1)
+    key_value = (own_part + jnp.concatenate([later_part, incoming[None]], axis=0)).reshape(
+        tok_count, 2 * head_width
+    )
+    dquery_s = dquery.reshape(tok_count, head_width)
+    dkey_s = key_value[:, :head_width]
+    dvalue_s = key_value[:, head_width:]
+    query_float = sorted_query.astype(jnp.float32)
+    norm_s = jnp.sqrt(jnp.sum(query_float * query_float, axis=1, keepdims=True) + eps_norm)
+    along = jnp.sum(query_float * dkey_s, axis=1, keepdims=True)
+    dshared_s = dquery_s + dkey_s / norm_s - query_float * (along / norm_s**3)
     sorted_grads = jnp.concatenate(
-        [dquery.reshape(tok_count, head_width), key_value.reshape(tok_count, 2 * head_width)],
-        axis=1,
+        [dshared_s.astype(jnp.bfloat16), dvalue_s.astype(jnp.bfloat16)], axis=1
     )
     return_rows = sorted_grads[jnp.minimum(recv_slots, tok_count - 1)]
-    back_rows = lax.all_to_all(return_rows, "seq", split_axis=0, concat_axis=0, tiled=True)
-    owned = back_rows[buffer_index]
-    dquery_p = owned[:, :head_width]
-    dkey_p = owned[:, head_width : 2 * head_width]
-    dvalue_p = owned[:, 2 * head_width :]
-    query_float = query.astype(jnp.float32)
-    norm_pos = jnp.sqrt(jnp.sum(query_float * query_float, axis=1, keepdims=True) + eps_norm)
-    along = jnp.sum(query_float * dkey_p, axis=1, keepdims=True)
-    dshared = dquery_p + dkey_p / norm_pos - query_float * (along / norm_pos**3)
-    combined = jnp.concatenate(
-        [dshared.astype(jnp.bfloat16), dvalue_p.astype(jnp.bfloat16)], axis=1
-    )
-    grads = lax.psum_scatter(
-        lax.dot_general(
-            whole, combined, (((0,), (0,)), ((), ())), preferred_element_type=jnp.float32
-        ),
-        "seq",
-        scatter_dimension=0,
-        tiled=True,
-    )
+    back_rows = lax.all_to_all(return_rows, SEQ, split_axis=0, concat_axis=0, tiled=True)
+    combined = back_rows[buffer_index]
+    nz, ny, nc = (lax.axis_size(a) for a in SEQ)
+    blocks = whole.reshape(tok_count, nz, ny, nc, feat_count // (nz * ny * nc))
+    partial = jnp.einsum(
+        "pzyck,ph->cyzkh", blocks, combined, preferred_element_type=jnp.float32
+    ).reshape(feat_count, 2 * head_width)
+    grads = partial
+    for axis in ("c", "y", "z"):
+        grads = lax.psum_scatter(grads, axis, scatter_dimension=0, tiled=True)
     return (grads[:, :head_width], grads[:, head_width:])
 
 
+def split_mesh(mesh):
+    devices = mesh.devices
+    seq_n, head_n = devices.shape
+    column = devices[:, 0]
+    cores = sorted({d.core_on_chip for d in column})
+    ys = sorted({d.coords[1] for d in column})
+    nc, ny = len(cores), len(ys)
+    nz = seq_n // (nc * ny)
+    grid = devices.reshape(nz, ny, nc, head_n)
+    for z in range(nz):
+        for y in range(ny):
+            for c in range(nc):
+                d = grid[z, y, c, 0]
+                assert d.core_on_chip == cores[c] and d.coords[1] == ys[y]
+    return Mesh(grid, SEQ + ("head",))
+
+
 def solution(mesh):
+    fine = split_mesh(mesh)
     in_specs = (
-        P("seq", "head"),
+        P(SEQ, "head"),
         P(None, "head"),
         P(None, "head"),
-        P("seq", "head"),
-        P("head", "seq"),
+        P(SEQ, "head"),
+        P("head", SEQ),
     )
-    out_specs = (P("seq", "head"), P("seq", "head"))
+    out_specs = (P(SEQ, "head"), P(SEQ, "head"))
     return jax.shard_map(
-        per_device, mesh=mesh, in_specs=in_specs, out_specs=out_specs, check_vma=False
+        per_device, mesh=fine, in_specs=in_specs, out_specs=out_specs, check_vma=False
     )

time: 335 us -> 233 us (0.70)
  waiting for transfers between devices: 247 us -> 151 us
  local copies, waits for them, and re-layouts: 17.2 us -> 13.3 us
    unnamed x3 -> x4, waiting for transfers between devices: 196 us -> 0.73 us
    reduce_scatter x0 -> x3, waiting for transfers between devices: none -> 104 us  [per_device(): grads = lax.psum_scatter(grads, axis, scatter_dimension=0, tiled=True)]
    unnamed x9 -> x5, local copies, waits for them, and re-layouts: 6.77 us -> 0.88 us
    all_to_all x3, waiting for transfers between devices: 29.1 us -> 24.1 us  [the longest x1 12.1 us: per_device(): lax.all_to_all(return_rows, SEQ, split_axis=0, concat_axis=0, tiled=True)]
  transfers between devices with their start and end apart: 7 -> 9, of which waited for: 6 -> 8; matrix products, arithmetic and copies ran while one was open for 3% -> 4% of each run, Pallas kernels for 0% -> 0%
where the time goes in v1:
time: 233 us
  waiting for transfers between devices  151 us (65%)
  starting transfers between devices  45.5 us (20%)
  between operations  14.1 us (6%)
  local copies, waits for them, and re-layouts  13.3 us (6%)
  matrix products  6.05 us (3%)
  other arithmetic  3.1 us (1%)
    reduce_scatter x3, waiting for transfers between devices, per_device(): grads = lax.psum_scatter(grads, axis, scatter_dimension=0, tiled=True)  104 us
    all_to_all x1, starting transfers between devices, per_device(): lax.all_to_all(send_slots, SEQ, split_axis=0, concat_axis=0, tiled=True)  17.8 us
    all_to_all x1, starting transfers between devices, per_device(): lax.all_to_all(send_rows, SEQ, split_axis=0, concat_axis=0, tiled=True)  14.9 us
    all_gather x1, waiting for transfers between devices, per_device(): whole = lax.all_gather(tokens, 'head', axis=1, tiled=True)  12.8 us
    all_to_all x1, waiting for transfers between devices, per_device(): lax.all_to_all(return_rows, SEQ, split_axis=0, concat_axis=0, tiled=True)  12.1 us
    all_to_all x1, waiting for transfers between devices, per_device(): lax.all_to_all(send_rows, SEQ, split_axis=0, concat_axis=0, tiled=True)  11.9 us
    ppermute x2, waiting for transfers between devices, shifted(): return lax.ppermute(value, axis, pairs)  8.87 us
    all_to_all x1, starting transfers between devices, per_device(): lax.all_to_all(return_rows, SEQ, split_axis=0, concat_axis=0, tiled=True)  8.7 us
  transfers between devices with their start and end apart: 9, of which 8 were waited for; matrix products, arithmetic and copies ran while one was open for 4% of the time, Pallas kernels for 0%

profile of v1, /device:TPU:6, one launch (start us, length us, event | category | flops | bytes accessed | tf_op | source)
XLA Modules:
  0.0 232.8 jit_solution(7353964962916671930)
XLA Ops:
  9.4 1.0 scatter_custom_fusion
  11.2 17.8 %all-to-all-start = ((s32[128,2,1]{1,2,0:T(1,128)}), s32[128,2,1]{1,2,0:T(1,128)S(1)}, u32[]{:S(2)}, u32[]{:S(2)}) async-start(s32[128,2,1]{1,2,0:T(1,128)} %bitcast.4), calls=%async_computation | async-start | bytes 131072 | tf_op jit(solution)/shard_map/all_to_all | solution.py:65
  29.0 0.9 copy.16
  29.9 12.8 %all-gather.2.cloned.1.call-done = bf16[128,4096]{1,0:T(8,128)(2,1)} async-done(((bf16[128,1024]{1,0:T(8,128)(2,1)}), bf16[128,4096]{1,0:T(8,128)(2,1)}) %all-gather.2.cloned.1.call-update) | async-done | bytes 1048592 | tf_op jit(solution)/shard_map/all_gather | solution.py:31
  42.6 1.7 convolution_convert_fusion
  44.4 2.1 convolution_convert_fusion.1
  46.6 1.1 scatter_custom_fusion.1
  48.5 14.9 %all-to-all-start.1 = ((bf16[128,2,384]{2,1,0:T(2,128)(2,1)}), bf16[128,2,384]{2,1,0:T(2,128)(2,1)S(1)}, u32[]{:S(2)}, u32[]{:S(2)}) async-start(bf16[128,2,384]{2,1,0:T(2,128)(2,1)} %all_to_all.27), calls=%async_computation.1 | async-start | bytes 393216 | tf_op jit(solution)/shard_map/all_to_all | solution.py:64
  63.9 0.8 reduce.3
  64.8 11.9 %all-to-all-done.1 = bf16[128,2,384]{2,1,0:T(2,128)(2,1)S(1)} async-done(((bf16[128,2,384]{2,1,0:T(2,128)(2,1)}), bf16[128,2,384]{2,1,0:T(2,128)(2,1)S(1)}, u32[]{:S(2)}, u32[]{:S(2)}) %all-to-all-start.1) | async-done | bytes 196640 | tf_op jit(solution)/shard_map/all_to_all | solution.py:64
  76.9 1.5 scatter_custom_fusion.2
  78.6 2.0 collective-permute-start
  80.7 6.5 %collective-permute-done = bf16[64,256]{1,0:T(8,128)(2,1)S(1)} collective-permute-done((bf16[64,256]{1,0:T(8,128)(2,1)S(1)}, bf16[64,256]{1,0:T(8,128)(2,1)S(1)}, u32[]{:S(2)}, u32[]{:S(2)}) %collective-permute-start) | collective-permute-done | bytes 32800 | tf_op jit(solution)/shard_map/ppermute | solution.py:21
  88.9 1.9 collective-permute-start.1
  90.9 2.4 %collective-permute-done.1 = f32[64,256]{0,1:T(8,128)S(1)} collective-permute-done((f32[64,256]{0,1:T(8,128)S(1)}, f32[64,256]{0,1:T(8,128)S(1)}, u32[]{:S(2)}, u32[]{:S(2)}) %collective-permute-start.1) | collective-permute-done | bytes 65568 | tf_op jit(solution)/shard_map/ppermute | solution.py:21
  93.7 1.2 gather_fusion
  95.6 8.7 %all-to-all-start.2 = ((bf16[128,2,256]{2,1,0:T(2,128)(2,1)}), bf16[128,2,256]{2,1,0:T(2,128)(2,1)S(1)}, u32[]{:S(2)}, u32[]{:S(2)}) async-start(bf16[128,2,256]{2,1,0:T(2,128)(2,1)} %all_to_all.30), calls=%async_computation.2 | async-start | bytes 262144 | tf_op jit(solution)/shard_map/all_to_all | solution.py:124
  104.4 12.1 %all-to-all-done.2 = bf16[128,2,256]{2,1,0:T(2,128)(2,1)S(1)} async-done(((bf16[128,2,256]{2,1,0:T(2,128)(2,1)}), bf16[128,2,256]{2,1,0:T(2,128)(2,1)S(1)}, u32[]{:S(2)}, u32[]{:S(2)}) %all-to-all-start.2) | async-done | bytes 131104 | tf_op jit(solution)/shard_map/all_to_all | solution.py:124
  116.6 0.8 gather_fusion.1
  118.2 2.2 copy.20
  120.5 12.8 %reduce-scatter.4.cloned.1.call-done = f32[2048,256]{1,0:T(8,128)} async-done(((f32[4096,256]{1,0:T(8,128)}), f32[2048,256]{1,0:T(8,128)}) %reduce-scatter.4.cloned.1.call-update) | async-done | bytes 2097168 | tf_op jit(solution)/shard_map/reduce_scatter | solution.py:133
  133.4 49.3 %reduce-scatter.6.cloned.1.call-done = f32[256,256]{1,0:T(8,128)} async-done(((f32[2048,256]{1,0:T(8,128)}), f32[256,256]{1,0:T(8,128)}) %reduce-scatter.6.cloned.1.call-update) | async-done | bytes 262160 | tf_op jit(solution)/shard_map/reduce_scatter | solution.py:133
  182.7 42.3 %reduce-scatter.8.cloned.1.call-done = f32[32,256]{1,0:T(8,128)} async-done(((f32[256,256]{1,0:T(8,128)}), f32[32,256]{1,0:T(8,128)}) %reduce-scatter.8.cloned.1.call-update) | async-done | bytes 32784 | tf_op jit(solution)/shard_map/reduce_scatter | solution.py:133
  225.0 1.3 fusion.44
  (55 shorter events, 8.7 us)
Async XLA Ops:
  7.2 35.5 %copy-start = (bf16[4096,128]{1,0:T(8,128)(2,1)S(1)}, bf16[4096,128]{1,0:T(8,128)(2,1)}, u32[]{:S(2)}) copy-start(bf16[4096,128]{1,0:T(8,128)(2,1)} %param.7) | copy-start | bytes 3145732
  7.2 35.4 %all-gather.2.cloned.1.call-start = ((), (), s32[]{:S(2)}) async-start(), calls=%async_computation.6 | async-start | bytes 1310720 | tf_op jit(solution)/shard_map/all_gather | solution.py:31
  11.2 37.3 %all-to-all-start = ((s32[128,2,1]{1,2,0:T(1,128)}), s32[128,2,1]{1,2,0:T(1,128)S(1)}, u32[]{:S(2)}, u32[]{:S(2)}) async-start(s32[128,2,1]{1,2,0:T(1,128)} %bitcast.4), calls=%async_computation | async-start | bytes 131072 | tf_op jit(solution)/shard_map/all_to_all | solution.py:65
  47.7 69.7 %copy-start.1 = (bf16[128,4096]{1,0:T(8,128)(2,1)S(1)}, bf16[128,4096]{1,0:T(8,128)(2,1)}, u32[]{:S(2)}) copy-start(bf16[128,4096]{1,0:T(8,128)(2,1)} %all-gather.2.cloned.1.call-done) | copy-start | bytes 3145732
  48.5 28.3 %all-to-all-start.1 = ((bf16[128,2,384]{2,1,0:T(2,128)(2,1)}), bf16[128,2,384]{2,1,0:T(2,128)(2,1)S(1)}, u32[]{:S(2)}, u32[]{:S(2)}) async-start(bf16[128,2,384]{2,1,0:T(2,128)(2,1)} %all_to_all.27), calls=%async_computation.1 | async-start | bytes 393216 | tf_op jit(solution)/shard_map/all_to_all | solution.py:64
  78.6 8.6 %collective-permute-start = (bf16[64,256]{1,0:T(8,128)(2,1)S(1)}, bf16[64,256]{1,0:T(8,128)(2,1)S(1)}, u32[]{:S(2)}, u32[]{:S(2)}) collective-permute-start(bf16[64,256]{1,0:T(8,128)(2,1)S(1)} %slice.75), channel_id=1, source_target_pairs={{0,4},{4,8},{8,12},{12,16},{16,20},{20,24},{24,28},{28,32},{32,36}... | collective-permute-start | bytes 98312 | tf_op jit(solution)/shard_map/ppermute | solution.py:21
  88.9 4.4 %collective-permute-start.1 = (f32[64,256]{0,1:T(8,128)S(1)}, f32[64,256]{0,1:T(8,128)S(1)}, u32[]{:S(2)}, u32[]{:S(2)}) collective-permute-start(f32[64,256]{0,1:T(8,128)S(1)} %get-tuple-element.5), channel_id=1, source_target_pairs={{0,508},{4,0},{8,4},{12,8},{16,12},{20,16},{24,20},{28,24},{32,28}... | collective-permute-start | bytes 196616 | tf_op jit(solution)/shard_map/ppermute | solution.py:21
  95.6 20.9 %all-to-all-start.2 = ((bf16[128,2,256]{2,1,0:T(2,128)(2,1)}), bf16[128,2,256]{2,1,0:T(2,128)(2,1)S(1)}, u32[]{:S(2)}, u32[]{:S(2)}) async-start(bf16[128,2,256]{2,1,0:T(2,128)(2,1)} %all_to_all.30), calls=%async_computation.2 | async-start | bytes 262144 | tf_op jit(solution)/shard_map/all_to_all | solution.py:124
  104.3 29.0 %reduce-scatter.4.cloned.1.call-start = ((), (), s32[]{:S(2)}) async-start(), calls=%async_computation.7 | async-start | bytes 6291456 | tf_op jit(solution)/shard_map/reduce_scatter | solution.py:133
  120.4 62.2 %reduce-scatter.6.cloned.1.call-start = ((), (), s32[]{:S(2)}) async-start(), calls=%async_computation.8 | async-start | bytes 2359296 | tf_op jit(solution)/shard_map/reduce_scatter | solution.py:133
  133.3 91.6 %reduce-scatter.8.cloned.1.call-start = ((), (), s32[]{:S(2)}) async-start(), calls=%async_computation.9 | async-start | bytes 294912 | tf_op jit(solution)/shard_map/reduce_scatter | solution.py:133
Sparse Core Ops, SparseCore 0:
  10.1 32.4 all-gather.1
  120.6 12.7 reduce-scatter.3
  136.2 46.4 reduce-scatter.5
  185.3 39.6 reduce-scatter.7

commit v2 on v1

--- a/solution.py
+++ b/solution.py
@@ -28,8 +28,11 @@
 
 
 def per_device(tokens, shared_weight, value_weight, head_grad, sorted_slot):
-    whole = lax.all_gather(tokens, "head", axis=1, tiled=True)
-    tok_count = whole.shape[0]
+    tok_count = tokens.shape[0]
+    head_n = lax.axis_size("head")
+    spread = jnp.broadcast_to(tokens[None], (head_n,) + tokens.shape)
+    gathered = lax.all_to_all(spread, "head", 0, 0, tiled=True)
+    whole = gathered.transpose(1, 0, 2).reshape(tok_count, head_n * tokens.shape[1])
     feat_count = whole.shape[1]
     head_width = shared_weight.shape[1]
     peer_count = lax.axis_size(SEQ)
@@ -124,13 +127,23 @@
     back_rows = lax.all_to_all(return_rows, SEQ, split_axis=0, concat_axis=0, tiled=True)
     combined = back_rows[buffer_index]
     nz, ny, nc = (lax.axis_size(a) for a in SEQ)
-    blocks = whole.reshape(tok_count, nz, ny, nc, feat_count // (nz * ny * nc))
-    partial = jnp.einsum(
-        "pzyck,ph->cyzkh", blocks, combined, preferred_element_type=jnp.float32
-    ).reshape(feat_count, 2 * head_width)
-    grads = partial
-    for axis in ("c", "y", "z"):
-        grads = lax.psum_scatter(grads, axis, scatter_dimension=0, tiled=True)
+    rows = feat_count // (nz * ny * nc)
+    blocks = whole.reshape(tok_count, nz, ny, nc, rows)
+    first = jnp.einsum(
+        "pzyck,ph->cyzkh", blocks[..., : rows // 2], combined, preferred_element_type=jnp.float32
+    )
+    second = jnp.einsum(
+        "pzyck,ph->czykh", blocks[..., rows // 2 :], combined, preferred_element_type=jnp.float32
+    )
+    partial = jnp.stack([first, second], axis=1)
+
+    def reduce_over(value, axis):
+        return jnp.sum(lax.all_to_all(value, axis, 0, 0, tiled=True), axis=0)
+
+    halves = reduce_over(partial, "c")
+    first = reduce_over(reduce_over(halves[0], "y"), "z")
+    second = reduce_over(reduce_over(halves[1], "z"), "y")
+    grads = jnp.concatenate([first, second], axis=0)
     return (grads[:, :head_width], grads[:, head_width:])
 
 

time: 233 us -> 219 us (0.940)
  waiting for transfers between devices: 151 us -> 122 us
  starting transfers between devices: 45.5 us -> 59.8 us
  between operations: 14.1 us -> 1.08 us
  blocking collectives: 0 us -> 8.17 us
  other arithmetic: 3.1 us -> 7.57 us
  matrix products: 6.05 us -> 3.3 us
    reduce_scatter x3 -> x0, waiting for transfers between devices: 104 us -> none  [per_device(): grads = lax.psum_scatter(grads, axis, scatter_dimension=0, tiled=True)]
    all_to_all x0 -> x5, waiting for transfers between devices: none -> 81 us  [the longest x4 74.3 us: reduce_over(): return jnp.sum(lax.all_to_all(value, axis, 0, 0, tiled=True), axis=0)]
    all_to_all x0 -> x5, starting transfers between devices: none -> 23.3 us  [the longest x4 13.9 us: reduce_over(): return jnp.sum(lax.all_to_all(value, axis, 0, 0, tiled=True), axis=0)]
    all_gather x1 -> x0, waiting for transfers between devices: 12.8 us -> none  [per_device(): whole = lax.all_gather(tokens, 'head', axis=1, tiled=True)]
    all_to_all x1, starting transfers between devices: 14.9 us -> 6.17 us  [per_device(): lax.all_to_all(send_rows, SEQ, split_axis=0, concat_axis=0, tiled=True)]
    all_to_all x0 -> x1, blocking collectives: none -> 8.17 us  [reduce_over(): return jnp.sum(lax.all_to_all(value, axis, 0, 0, tiled=True), axis=0)]
    all_to_all x1, waiting for transfers between devices: 0.01 us -> 8.16 us  [per_device(): lax.all_to_all(send_slots, SEQ, split_axis=0, concat_axis=0, tiled=True)]
    reduce_sum x0 -> x5, other arithmetic: none -> 4.34 us  [reduce_over(): return jnp.sum(lax.all_to_all(value, axis, 0, 0, tiled=True), axis=0)]
  transfers between devices with their start and end apart: 9 -> 10, of which waited for: 8 -> 10; matrix products, arithmetic and copies ran while one was open for 4% -> 4% of each run, Pallas kernels for 0% -> 0%
where the time goes in v2:
time: 219 us; the launch traced here: 217 us
  waiting for transfers between devices  122 us (56%)
  starting transfers between devices  59.8 us (27%)
  local copies, waits for them, and re-layouts  15.6 us (7%)
  blocking collectives  8.17 us (4%)
  other arithmetic  7.57 us (3%)
  matrix products  3.3 us (2%)
    all_to_all x4, waiting for transfers between devices, reduce_over(): return jnp.sum(lax.all_to_all(value, axis, 0, 0, tiled=True), axis=0)  74.3 us
    all_to_all x1, starting transfers between devices, per_device(): lax.all_to_all(send_slots, SEQ, split_axis=0, concat_axis=0, tiled=True)  17.5 us
    all_to_all x4, starting transfers between devices, reduce_over(): return jnp.sum(lax.all_to_all(value, axis, 0, 0, tiled=True), axis=0)  13.9 us
    all_to_all x1, waiting for transfers between devices, per_device(): lax.all_to_all(send_rows, SEQ, split_axis=0, concat_axis=0, tiled=True)  12 us
    all_to_all x1, waiting for transfers between devices, per_device(): lax.all_to_all(return_rows, SEQ, split_axis=0, concat_axis=0, tiled=True)  11.8 us
    all_to_all x1, starting transfers between devices, per_device(): gathered = lax.all_to_all(spread, 'head', 0, 0, tiled=True)  9.44 us
    all_to_all x1, starting transfers between devices, per_device(): lax.all_to_all(return_rows, SEQ, split_axis=0, concat_axis=0, tiled=True)  8.88 us
    ppermute x2, waiting for transfers between devices, shifted(): return lax.ppermute(value, axis, pairs)  8.87 us
  transfers between devices with their start and end apart: 10, of which 10 were waited for; matrix products, arithmetic and copies ran while one was open for 4% of the time, Pallas kernels for 0%

profile of v2, /device:TPU:6, one launch (start us, length us, event | category | flops | bytes accessed | tf_op | source)
XLA Modules:
  0.0 217.3 jit_solution(8707869608622428291)
XLA Ops:
  3.0 9.4 %all-to-all-start.1 = ((bf16[4,128,1024]{1,2,0:T(8,128)(2,1)}), bf16[4,128,1024]{1,2,0:T(8,128)(2,1)S(1)}, u32[]{:S(2)}, u32[]{:S(2)}) async-start(bf16[4,128,1024]{1,2,0:T(8,128)(2,1)} %broadcast_in_dim.28), calls=%async_computation.1 | async-start | bytes 2097152 | tf_op jit(solution)/shard_map/all_to_all | solution.py:34
  14.5 6.7 %all-to-all-done.1 = bf16[4,128,1024]{1,2,0:T(8,128)(2,1)S(1)} async-done(((bf16[4,128,1024]{1,2,0:T(8,128)(2,1)}), bf16[4,128,1024]{1,2,0:T(8,128)(2,1)S(1)}, u32[]{:S(2)}, u32[]{:S(2)}) %all-to-all-start.1) | async-done | bytes 1048608 | tf_op jit(solution)/shard_map/all_to_all | solution.py:34
  21.3 17.5 %all-to-all-start = ((s32[128,2,1]{1,2,0:T(1,128)}), s32[128,2,1]{1,2,0:T(1,128)S(1)}, u32[]{:S(2)}, u32[]{:S(2)}) async-start(s32[128,2,1]{1,2,0:T(1,128)} %bitcast.4), calls=%async_computation | async-start | bytes 131072 | tf_op jit(solution)/shard_map/all_to_all | solution.py:68
  41.8 8.2 %all-to-all-done = s32[128,2,1]{1,2,0:T(1,128)S(1)} async-done(((s32[128,2,1]{1,2,0:T(1,128)}), s32[128,2,1]{1,2,0:T(1,128)S(1)}, u32[]{:S(2)}, u32[]{:S(2)}) %all-to-all-start) | async-done | bytes 1056 | tf_op jit(solution)/shard_map/all_to_all | solution.py:68
  49.9 6.2 %all-to-all-start.2 = ((bf16[128,2,384]{2,1,0:T(2,128)(2,1)}), bf16[128,2,384]{2,1,0:T(2,128)(2,1)S(1)}, u32[]{:S(2)}, u32[]{:S(2)}) async-start(bf16[128,2,384]{2,1,0:T(2,128)(2,1)} %all_to_all.46), calls=%async_computation.2 | async-start | bytes 393216 | tf_op jit(solution)/shard_map/all_to_all | solution.py:67
  57.6 12.0 %all-to-all-done.2 = bf16[128,2,384]{2,1,0:T(2,128)(2,1)S(1)} async-done(((bf16[128,2,384]{2,1,0:T(2,128)(2,1)}), bf16[128,2,384]{2,1,0:T(2,128)(2,1)S(1)}, u32[]{:S(2)}, u32[]{:S(2)}) %all-to-all-start.2) | async-done | bytes 196640 | tf_op jit(solution)/shard_map/all_to_all | solution.py:67
  69.6 1.5 scatter_custom_fusion.2
  71.4 2.0 collective-permute-start
  73.4 6.5 %collective-permute-done = bf16[64,256]{1,0:T(8,128)(2,1)S(1)} collective-permute-done((bf16[64,256]{1,0:T(8,128)(2,1)S(1)}, bf16[64,256]{1,0:T(8,128)(2,1)S(1)}, u32[]{:S(2)}, u32[]{:S(2)}) %collective-permute-start) | collective-permute-done | bytes 32800 | tf_op jit(solution)/shard_map/ppermute | solution.py:21
  81.6 1.9 collective-permute-start.1
  83.7 2.4 %collective-permute-done.1 = f32[64,256]{0,1:T(8,128)S(1)} collective-permute-done((f32[64,256]{0,1:T(8,128)S(1)}, f32[64,256]{0,1:T(8,128)S(1)}, u32[]{:S(2)}, u32[]{:S(2)}) %collective-permute-start.1) | collective-permute-done | bytes 65568 | tf_op jit(solution)/shard_map/ppermute | solution.py:21
  88.3 8.9 %all-to-all-start.3 = ((bf16[128,2,256]{2,1,0:T(2,128)(2,1)}), bf16[128,2,256]{2,1,0:T(2,128)(2,1)S(1)}, u32[]{:S(2)}, u32[]{:S(2)}) async-start(bf16[128,2,256]{2,1,0:T(2,128)(2,1)} %all_to_all.49), calls=%async_computation.3 | async-start | bytes 262144 | tf_op jit(solution)/shard_map/all_to_all | solution.py:127
  97.5 11.8 %all-to-all-done.3 = bf16[128,2,256]{2,1,0:T(2,128)(2,1)S(1)} async-done(((bf16[128,2,256]{2,1,0:T(2,128)(2,1)}), bf16[128,2,256]{2,1,0:T(2,128)(2,1)S(1)}, u32[]{:S(2)}, u32[]{:S(2)}) %all-to-all-start.3) | async-done | bytes 131104 | tf_op jit(solution)/shard_map/all_to_all | solution.py:127
  112.5 8.2 %all_to_all.66 = f32[2,2,8,8,16,256]{5,4,2,3,1,0:T(8,128)} all-to-all(f32[2,2,8,8,16,256]{5,4,2,3,1,0:T(8,128)S(1)} %copy.40), channel_id=1, replica_groups=mesh['z'=8,'y'=8,'c'=2,'head'=4] {'c'}, dimensions={0} | all-to-all | bytes 8388608 | tf_op jit(solution)/shard_map/all_to_all | solution.py:141
  120.7 2.9 %reduce_sum.109 = f32[2,8,8,16,256]{4,3,1,2,0:T(8,128)S(1)} reduce(f32[2,2,8,8,16,256]{5,4,2,3,1,0:T(8,128)} %all_to_all.66, f32[]{:T(128)} %constant.11.clone.1), dimensions={0}, to_apply=%region_10.11 | reduce | flops 524288 | bytes 6291460 | tf_op jit(solution)/shard_map/reduce_sum | solution.py:141
  123.5 1.3 slice_bitcast_fusion
  125.9 3.6 %all-to-all-start.7 = ((f32[8,8,16,256]{3,2,1,0:T(8,128)}), f32[8,8,16,256]{3,2,1,0:T(8,128)S(1)}, u32[]{:S(2)}, u32[]{:S(2)}) async-start(f32[8,8,16,256]{3,2,1,0:T(8,128)} %copy.43), calls=%async_computation.7 | async-start | bytes 2097152 | tf_op jit(solution)/shard_map/all_to_all | solution.py:141
  130.6 28.2 %all-to-all-done.7 = f32[8,8,16,256]{3,2,1,0:T(8,128)S(1)} async-done(((f32[8,8,16,256]{3,2,1,0:T(8,128)}), f32[8,8,16,256]{3,2,1,0:T(8,128)S(1)}, u32[]{:S(2)}, u32[]{:S(2)}) %all-to-all-start.7) | async-done | bytes 1048608 | tf_op jit(solution)/shard_map/all_to_all | solution.py:141
  158.8 3.6 %all-to-all-start.5 = ((f32[8,8,16,256]{3,2,1,0:T(8,128)}), f32[8,8,16,256]{3,2,1,0:T(8,128)S(1)}, u32[]{:S(2)}, u32[]{:S(2)}) async-start(f32[8,8,16,256]{3,2,1,0:T(8,128)} %copy.42), calls=%async_computation.5 | async-start | bytes 2097152 | tf_op jit(solution)/shard_map/all_to_all | solution.py:141
  163.0 28.5 %all-to-all-done.5 = f32[8,8,16,256]{3,2,1,0:T(8,128)S(1)} async-done(((f32[8,8,16,256]{3,2,1,0:T(8,128)}), f32[8,8,16,256]{3,2,1,0:T(8,128)S(1)}, u32[]{:S(2)}, u32[]{:S(2)}) %all-to-all-start.5) | async-done | bytes 1048608 | tf_op jit(solution)/shard_map/all_to_all | solution.py:141
  191.5 3.4 %all-to-all-start.8 = ((f32[8,16,256]{2,1,0:T(8,128)}), f32[8,16,256]{2,1,0:T(8,128)S(1)}, u32[]{:S(2)}, u32[]{:S(2)}) async-start(f32[8,16,256]{2,1,0:T(8,128)} %reduce_sum.112), calls=%async_computation.8 | async-start | bytes 262144 | tf_op jit(solution)/shard_map/all_to_all | solution.py:141
  195.6 8.7 %all-to-all-done.8 = f32[8,16,256]{2,1,0:T(8,128)S(1)} async-done(((f32[8,16,256]{2,1,0:T(8,128)}), f32[8,16,256]{2,1,0:T(8,128)S(1)}, u32[]{:S(2)}, u32[]{:S(2)}) %all-to-all-start.8) | async-done | bytes 131104 | tf_op jit(solution)/shard_map/all_to_all | solution.py:141
  204.3 3.4 %all-to-all-start.6 = ((f32[8,16,256]{2,1,0:T(8,128)}), f32[8,16,256]{2,1,0:T(8,128)S(1)}, u32[]{:S(2)}, u32[]{:S(2)}) async-start(f32[8,16,256]{2,1,0:T(8,128)} %reduce_sum.110), calls=%async_computation.6 | async-start | bytes 262144 | tf_op jit(solution)/shard_map/all_to_all | solution.py:141
  207.7 9.0 %all-to-all-done.6 = f32[8,16,256]{2,1,0:T(8,128)S(1)} async-done(((f32[8,16,256]{2,1,0:T(8,128)}), f32[8,16,256]{2,1,0:T(8,128)S(1)}, u32[]{:S(2)}, u32[]{:S(2)}) %all-to-all-start.6) | async-done | bytes 131104 | tf_op jit(solution)/shard_map/all_to_all | solution.py:141
  (73 shorter events, 20.9 us)
Async XLA Ops:
  0.6 38.1 %copy-start = (bf16[4096,128]{1,0:T(8,128)(2,1)S(1)}, bf16[4096,128]{1,0:T(8,128)(2,1)}, u32[]{:S(2)}) copy-start(bf16[4096,128]{1,0:T(8,128)(2,1)} %param.7) | copy-start | bytes 3145732
  0.6 11.8 %copy-start.3 = (bf16[128,128]{1,0:T(8,128)(2,1)S(1)}, bf16[128,128]{1,0:T(8,128)(2,1)}, u32[]{:S(2)}) copy-start(bf16[128,128]{1,0:T(8,128)(2,1)} %param.8) | copy-start | bytes 98308
  0.7 11.9 %copy-start.4 = (s32[1,128]{1,0:T(1,128)S(1)}, s32[1,128]{1,0:T(1,128)}, u32[]{:S(2)}) copy-start(s32[1,128]{1,0:T(1,128)} %param.9) | copy-start | bytes 1540
  3.0 36.2 %copy-start.2 = (bf16[4096,128]{1,0:T(8,128)(2,1)S(1)}, bf16[4096,128]{1,0:T(8,128)(2,1)}, u32[]{:S(2)}) copy-start(bf16[4096,128]{1,0:T(8,128)(2,1)} %param.6) | copy-start | bytes 3145732
  3.0 18.3 %all-to-all-start.1 = ((bf16[4,128,1024]{1,2,0:T(8,128)(2,1)}), bf16[4,128,1024]{1,2,0:T(8,128)(2,1)S(1)}, u32[]{:S(2)}, u32[]{:S(2)}) async-start(bf16[4,128,1024]{1,2,0:T(8,128)(2,1)} %broadcast_in_dim.28), calls=%async_computation.1 | async-start | bytes 2097152 | tf_op jit(solution)/shard_map/all_to_all | solution.py:34
  21.3 28.6 %all-to-all-start = ((s32[128,2,1]{1,2,0:T(1,128)}), s32[128,2,1]{1,2,0:T(1,128)S(1)}, u32[]{:S(2)}, u32[]{:S(2)}) async-start(s32[128,2,1]{1,2,0:T(1,128)} %bitcast.4), calls=%async_computation | async-start | bytes 131072 | tf_op jit(solution)/shard_map/all_to_all | solution.py:68
  49.9 19.6 %all-to-all-start.2 = ((bf16[128,2,384]{2,1,0:T(2,128)(2,1)}), bf16[128,2,384]{2,1,0:T(2,128)(2,1)S(1)}, u32[]{:S(2)}, u32[]{:S(2)}) async-start(bf16[128,2,384]{2,1,0:T(2,128)(2,1)} %all_to_all.46), calls=%async_computation.2 | async-start | bytes 393216 | tf_op jit(solution)/shard_map/all_to_all | solution.py:67
  71.4 8.6 %collective-permute-start = (bf16[64,256]{1,0:T(8,128)(2,1)S(1)}, bf16[64,256]{1,0:T(8,128)(2,1)S(1)}, u32[]{:S(2)}, u32[]{:S(2)}) collective-permute-start(bf16[64,256]{1,0:T(8,128)(2,1)S(1)} %slice.92), channel_id=1, source_target_pairs={{0,4},{4,8},{8,12},{12,16},{16,20},{20,24},{24,28},{28,32},{32,36}... | collective-permute-start | bytes 98312 | tf_op jit(solution)/shard_map/ppermute | solution.py:21
  81.6 4.4 %collective-permute-start.1 = (f32[64,256]{0,1:T(8,128)S(1)}, f32[64,256]{0,1:T(8,128)S(1)}, u32[]{:S(2)}, u32[]{:S(2)}) collective-permute-start(f32[64,256]{0,1:T(8,128)S(1)} %get-tuple-element.9), channel_id=1, source_target_pairs={{0,508},{4,0},{8,4},{12,8},{16,12},{20,16},{24,20},{28,24},{32,28}... | collective-permute-start | bytes 196616 | tf_op jit(solution)/shard_map/ppermute | solution.py:21
  88.3 20.9 %all-to-all-start.3 = ((bf16[128,2,256]{2,1,0:T(2,128)(2,1)}), bf16[128,2,256]{2,1,0:T(2,128)(2,1)S(1)}, u32[]{:S(2)}, u32[]{:S(2)}) async-start(bf16[128,2,256]{2,1,0:T(2,128)(2,1)} %all_to_all.49), calls=%async_computation.3 | async-start | bytes 262144 | tf_op jit(solution)/shard_map/all_to_all | solution.py:127
  124.8 4.6 %copy-start.1 = (f32[8,8,16,256]{3,2,0,1:T(8,128)S(1)}, f32[8,8,16,256]{3,2,0,1:T(8,128)}, u32[]{:S(2)}) copy-start(f32[8,8,16,256]{3,2,0,1:T(8,128)} %get-tuple-element.5) | copy-start | bytes 3145732
  125.9 32.9 %all-to-all-start.7 = ((f32[8,8,16,256]{3,2,1,0:T(8,128)}), f32[8,8,16,256]{3,2,1,0:T(8,128)S(1)}, u32[]{:S(2)}, u32[]{:S(2)}) async-start(f32[8,8,16,256]{3,2,1,0:T(8,128)} %copy.43), calls=%async_computation.7 | async-start | bytes 2097152 | tf_op jit(solution)/shard_map/all_to_all | solution.py:141
  158.8 32.7 %all-to-all-start.5 = ((f32[8,8,16,256]{3,2,1,0:T(8,128)}), f32[8,8,16,256]{3,2,1,0:T(8,128)S(1)}, u32[]{:S(2)}, u32[]{:S(2)}) async-start(f32[8,8,16,256]{3,2,1,0:T(8,128)} %copy.42), calls=%async_computation.5 | async-start | bytes 2097152 | tf_op jit(solution)/shard_map/all_to_all | solution.py:141
  191.5 12.8 %all-to-all-start.8 = ((f32[8,16,256]{2,1,0:T(8,128)}), f32[8,16,256]{2,1,0:T(8,128)S(1)}, u32[]{:S(2)}, u32[]{:S(2)}) async-start(f32[8,16,256]{2,1,0:T(8,128)} %reduce_sum.112), calls=%async_computation.8 | async-start | bytes 262144 | tf_op jit(solution)/shard_map/all_to_all | solution.py:141
  204.3 12.4 %all-to-all-start.6 = ((f32[8,16,256]{2,1,0:T(8,128)}), f32[8,16,256]{2,1,0:T(8,128)S(1)}, u32[]{:S(2)}, u32[]{:S(2)}) async-start(f32[8,16,256]{2,1,0:T(8,128)} %reduce_sum.110), calls=%async_computation.6 | async-start | bytes 262144 | tf_op jit(solution)/shard_map/all_to_all | solution.py:141

commit v3 on v2

--- a/solution.py
+++ b/solution.py
@@ -54,24 +54,28 @@
     buffer_index = target * capacity + jnp.sum(before * one_hot.astype(jnp.float32), axis=1).astype(
         jnp.int32
     )
-    payload = jnp.concatenate([query, values, head_grad], axis=1)
-    send_rows = (
-        jnp.zeros((peer_count * capacity, 3 * head_width), jnp.bfloat16)
-        .at[buffer_index]
-        .set(payload)
+    slot_block = jnp.zeros((tok_count, head_width), jnp.bfloat16).at[:, 0].set(
+        local_slot.astype(jnp.bfloat16)
     )
-    send_slots = (
-        jnp.full((peer_count * capacity,), tok_count, jnp.int32).at[buffer_index].set(local_slot)
+    payload = jnp.concatenate([query, values, head_grad, slot_block], axis=1)
+    buffer_ids = jnp.arange(peer_count * capacity, dtype=jnp.int32)
+    to_buffer = (buffer_ids[:, None] == buffer_index[None, :]).astype(jnp.bfloat16)
+    send_rows = jnp.dot(to_buffer, payload, preferred_element_type=jnp.float32).astype(jnp.bfloat16)
+    empty = (buffer_ids[:, None] * 0 + jnp.arange(head_width)[None, :]) == 0
+    used = jnp.sum(to_buffer.astype(jnp.float32), axis=1) > 0
+    send_rows = send_rows.at[:, 3 * head_width :].set(
+        jnp.where(
+            empty & ~used[:, None],
+            jnp.bfloat16(tok_count),
+            send_rows[:, 3 * head_width :],
+        )
     )
-    recv_rows, recv_slots = (
-        lax.all_to_all(send_rows, SEQ, split_axis=0, concat_axis=0, tiled=True),
-        lax.all_to_all(send_slots, SEQ, split_axis=0, concat_axis=0, tiled=True),
-    )
-    sorted_rows = (
-        jnp.zeros((tok_count, 3 * head_width), jnp.bfloat16)
-        .at[recv_slots]
-        .set(recv_rows, mode="drop")
-    )
+    recv_rows = lax.all_to_all(send_rows, SEQ, split_axis=0, concat_axis=0, tiled=True)
+    recv_slots = recv_rows[:, 3 * head_width].astype(jnp.int32)
+    to_sorted = (row_ids[:, None] == recv_slots[None, :]).astype(jnp.bfloat16)
+    sorted_rows = jnp.dot(
+        to_sorted, recv_rows[:, : 3 * head_width], preferred_element_type=jnp.float32
+    ).astype(jnp.bfloat16)
     halo_rows = shifted(sorted_rows[tail_start:, : 2 * head_width], SEQ, 1)
     sorted_query = sorted_rows[:, :head_width]
     own_keys = unit_keys(sorted_query).reshape(group_count, GROUP, head_width)
@@ -123,27 +127,20 @@
     sorted_grads = jnp.concatenate(
         [dshared_s.astype(jnp.bfloat16), dvalue_s.astype(jnp.bfloat16)], axis=1
     )
-    return_rows = sorted_grads[jnp.minimum(recv_slots, tok_count - 1)]
+    return_rows = lax.dot_general(
+        to_sorted, sorted_grads, (((0,), (0,)), ((), ())), preferred_element_type=jnp.float32
+    ).astype(jnp.bfloat16)
     back_rows = lax.all_to_all(return_rows, SEQ, split_axis=0, concat_axis=0, tiled=True)
-    combined = back_rows[buffer_index]
+    combined = lax.dot_general(
+        to_buffer, back_rows, (((0,), (0,)), ((), ())), preferred_element_type=jnp.float32
+    ).astype(jnp.bfloat16)
     nz, ny, nc = (lax.axis_size(a) for a in SEQ)
     rows = feat_count // (nz * ny * nc)
     blocks = whole.reshape(tok_count, nz, ny, nc, rows)
-    first = jnp.einsum(
-        "pzyck,ph->cyzkh", blocks[..., : rows // 2], combined, preferred_element_type=jnp.float32
-    )
-    second = jnp.einsum(
-        "pzyck,ph->czykh", blocks[..., rows // 2 :], combined, preferred_element_type=jnp.float32
-    )
-    partial = jnp.stack([first, second], axis=1)
-
-    def reduce_over(value, axis):
-        return jnp.sum(lax.all_to_all(value, axis, 0, 0, tiled=True), axis=0)
-
-    halves = reduce_over(partial, "c")
-    first = reduce_over(reduce_over(halves[0], "y"), "z")
-    second = reduce_over(reduce_over(halves[1], "z"), "y")
-    grads = jnp.concatenate([first, second], axis=0)
+    grads = jnp.einsum("pzyck,ph->cyzkh", blocks, combined, preferred_element_type=jnp.float32)
+    for axis in ("c", "y", "z"):
+        grads = jnp.sum(lax.all_to_all(grads, axis, 0, 0, tiled=True), axis=0)
+    grads = grads.reshape(rows, 2 * head_width)
     return (grads[:, :head_width], grads[:, head_width:])
 
 

time: 219 us -> 180 us (0.82)
  waiting for transfers between devices: 122 us -> 27.9 us
  blocking collectives: 8.17 us -> 97.8 us
  starting transfers between devices: 59.8 us -> 30.7 us
  local copies, waits for them, and re-layouts: 15.6 us -> 7.69 us
  matrix products: 3.3 us -> 5.97 us
    all_to_all x6 -> x0, waiting for transfers between devices: 94.2 us -> none  [the longest x4 74.3 us: reduce_over(): return jnp.sum(lax.all_to_all(value, axis, 0, 0, tiled=True), axis=0)]
    all_to_all x1 -> x4, blocking collectives: 8.17 us -> 97.8 us  [the longest x3 77.1 us: per_device(): grads = jnp.sum(lax.all_to_all(grads, axis, 0, 0, tiled=True), axis=0)]
    all_to_all x6 -> x0, starting transfers between devices: 40.2 us -> none  [the longest x1 17.5 us: per_device(): lax.all_to_all(send_slots, SEQ, split_axis=0, concat_axis=0, tiled=True)]
    all_to_all x1, starting transfers between devices: 6.17 us -> 17.5 us  [per_device(): lax.all_to_all(send_rows, SEQ, split_axis=0, concat_axis=0, tiled=True)]
    scatter x3 -> x0, local copies, waits for them, and re-layouts: 3.57 us -> none  [the longest x1 1.49 us: per_device(): sorted_rows = jnp.zeros((tok_count, 3 * head_width), jnp.bfloat16).at[rec...]
    squeeze x3 -> x0, local copies, waits for them, and re-layouts: 3.45 us -> none  [the longest x2 2.32 us: per_device(): second = reduce_over(reduce_over(halves[1], 'z'), 'y')]
    all_to_all x1, waiting for transfers between devices: 12 us -> 14.7 us  [per_device(): lax.all_to_all(send_rows, SEQ, split_axis=0, concat_axis=0, tiled=True)]
    transpose x0 -> x1, local copies, waits for them, and re-layouts: none -> 2.5 us  [per_device(): jnp.einsum('pzyck,ph->cyzkh', blocks, combined, preferred_element_type=jn...]
  transfers between devices with their start and end apart: 10 -> 4, of which waited for: 10 -> 4; matrix products, arithmetic and copies ran while one was open for 4% -> 3% of each run, Pallas kernels for 0% -> 0%
where the time goes in v3:
time: 180 us; the launch traced here: 179 us
  blocking collectives  97.8 us (54%)
  starting transfers between devices  30.7 us (17%)
  waiting for transfers between devices  27.9 us (16%)
  local copies, waits for them, and re-layouts  7.69 us (4%)
  other arithmetic  7.58 us (4%)
  matrix products  5.97 us (3%)
    all_to_all x3, blocking collectives, per_device(): grads = jnp.sum(lax.all_to_all(grads, axis, 0, 0, tiled=True), axis=0)  77.1 us
    all_to_all x1, blocking collectives, per_device(): lax.all_to_all(return_rows, SEQ, split_axis=0, concat_axis=0, tiled=True)  20.7 us
    all_to_all x1, starting transfers between devices, per_device(): lax.all_to_all(send_rows, SEQ, split_axis=0, concat_axis=0, tiled=True)  17.5 us
    all_to_all x1, waiting for transfers between devices, per_device(): lax.all_to_all(send_rows, SEQ, split_axis=0, concat_axis=0, tiled=True)  14.7 us
    all_to_all x1, starting transfers between devices, per_device(): gathered = lax.all_to_all(spread, 'head', 0, 0, tiled=True)  9.31 us
    ppermute x2, waiting for transfers between devices, shifted(): return lax.ppermute(value, axis, pairs)  8.86 us
    all_to_all x1, waiting for transfers between devices, per_device(): gathered = lax.all_to_all(spread, 'head', 0, 0, tiled=True)  4.33 us
    ppermute x2, starting transfers between devices, shifted(): return lax.ppermute(value, axis, pairs)  3.96 us
  transfers between devices with their start and end apart: 4, of which 4 were waited for; matrix products, arithmetic and copies ran while one was open for 3% of the time, Pallas kernels for 0%

profile of v3, /device:TPU:6, one launch (start us, length us, event | category | flops | bytes accessed | tf_op | source)
XLA Modules:
  0.0 178.6 jit_solution(17016612068828001655)
XLA Ops:
  0.7 1.3 copy.28
  1.9 1.1 broadcast_in_dim.20
  3.1 9.3 %all-to-all-start = ((bf16[4,128,1024]{1,2,0:T(8,128)(2,1)}), bf16[4,128,1024]{1,2,0:T(8,128)(2,1)S(1)}, u32[]{:S(2)}, u32[]{:S(2)}) async-start(bf16[4,128,1024]{1,2,0:T(8,128)(2,1)} %broadcast_in_dim.20), calls=%async_computation | async-start | bytes 2097152 | tf_op jit(solution)/shard_map/all_to_all | solution.py:34
  12.4 0.7 and_select_fusion.2
  13.2 0.9 copy.29
  14.1 0.7 compare_reduce_fusion
  14.7 0.7 fusion.52
  15.5 1.3 broadcast_select_fusion
  16.9 4.3 %all-to-all-done = bf16[4,128,1024]{1,2,0:T(8,128)(2,1)S(1)} async-done(((bf16[4,128,1024]{1,2,0:T(8,128)(2,1)}), bf16[4,128,1024]{1,2,0:T(8,128)(2,1)S(1)}, u32[]{:S(2)}, u32[]{:S(2)}) %all-to-all-start) | async-done | bytes 1048608 | tf_op jit(solution)/shard_map/all_to_all | solution.py:34
  22.6 0.8 all_to_all.29
  23.4 17.5 %all-to-all-start.1 = ((bf16[128,2,512]{2,1,0:T(2,128)(2,1)}), bf16[128,2,512]{2,1,0:T(2,128)(2,1)S(1)}, u32[]{:S(2)}, u32[]{:S(2)}) async-start(bf16[128,2,512]{2,1,0:T(2,128)(2,1)} %all_to_all.29), calls=%async_computation.1 | async-start | bytes 524288 | tf_op jit(solution)/shard_map/all_to_all | solution.py:73
  40.9 14.7 %all-to-all-done.1 = bf16[128,2,512]{2,1,0:T(2,128)(2,1)S(1)} async-done(((bf16[128,2,512]{2,1,0:T(2,128)(2,1)}), bf16[128,2,512]{2,1,0:T(2,128)(2,1)S(1)}, u32[]{:S(2)}, u32[]{:S(2)}) %all-to-all-start.1) | async-done | bytes 262176 | tf_op jit(solution)/shard_map/all_to_all | solution.py:73
  56.3 2.0 %collective-permute-start = (bf16[64,256]{1,0:T(8,128)(2,1)S(1)}, bf16[64,256]{1,0:T(8,128)(2,1)S(1)}, u32[]{:S(2)}, u32[]{:S(2)}) collective-permute-start(bf16[64,256]{1,0:T(8,128)(2,1)S(1)} %slice.117), channel_id=1, source_target_pairs={{0,4},{4,8},{8,12},{12,16},{16,20},{20,24},{24,28},{28,32},{32,36}... | collective-permute-start | bytes 98312 | tf_op jit(solution)/shard_map/ppermute | solution.py:21
  58.3 6.5 %collective-permute-done = bf16[64,256]{1,0:T(8,128)(2,1)S(1)} collective-permute-done((bf16[64,256]{1,0:T(8,128)(2,1)S(1)}, bf16[64,256]{1,0:T(8,128)(2,1)S(1)}, u32[]{:S(2)}, u32[]{:S(2)}) %collective-permute-start) | collective-permute-done | bytes 32800 | tf_op jit(solution)/shard_map/ppermute | solution.py:21
  66.5 1.9 %collective-permute-start.1 = (f32[64,256]{0,1:T(8,128)S(1)}, f32[64,256]{0,1:T(8,128)S(1)}, u32[]{:S(2)}, u32[]{:S(2)}) collective-permute-start(f32[64,256]{0,1:T(8,128)S(1)} %get-tuple-element.27), channel_id=1, source_target_pairs={{0,508},{4,0},{8,4},{12,8},{16,12},{20,16},{24,20},{28,24},{32,28}... | collective-permute-start | bytes 196616 | tf_op jit(solution)/shard_map/ppermute | solution.py:21
  68.6 2.4 %collective-permute-done.1 = f32[64,256]{0,1:T(8,128)S(1)} collective-permute-done((f32[64,256]{0,1:T(8,128)S(1)}, f32[64,256]{0,1:T(8,128)S(1)}, u32[]{:S(2)}, u32[]{:S(2)}) %collective-permute-start.1) | collective-permute-done | bytes 65568 | tf_op jit(solution)/shard_map/ppermute | solution.py:21
  71.6 20.7 %all_to_all.44 = bf16[128,2,256]{2,1,0:T(2,128)(2,1)S(1)} all-to-all(bf16[128,2,256]{2,1,0:T(2,128)(2,1)S(1)} %all_to_all.32), channel_id=1, replica_groups=mesh['z'=8,'y'=8,'c'=2,'head'=4] {'z','y','c'}, dimensions={0} | all-to-all | bytes 262144 | tf_op jit(solution)/shard_map/all_to_all | solution.py:133
  92.4 2.8 %fusion.2 = f32[256,4096]{0,1} fusion(bf16[128,4096]{0,1:T(8,128)(2,1)S(1)} %bitcast.75, bf16[256,256]{1,0:T(8,128)(2,1)S(1)} %all_to_all.34, s32[128]{0:T(128)S(1)} %fusion.52), kind=kOutput, calls=%fused_computation.7 | convolution fusion | flops 285278208 | bytes 5374464
  95.2 2.5 %copy.31 = f32[2,8,8,32,256]{4,3,1,2,0:T(8,128)S(1)} copy(f32[2,8,8,32,256]{4,3,0,1,2:T(8,128)} %bitcast.72) | data formatting | bytes 8388608 | tf_op jit(solution)/shard_map/pzyck,ph->cyzkh/transpose | solution.py:140
  97.8 8.2 %all_to_all.45 = f32[2,8,8,32,256]{4,3,1,2,0:T(8,128)} all-to-all(f32[2,8,8,32,256]{4,3,1,2,0:T(8,128)S(1)} %copy.31), channel_id=1, replica_groups=mesh['z'=8,'y'=8,'c'=2,'head'=4] {'c'}, dimensions={0} | all-to-all | bytes 8388608 | tf_op jit(solution)/shard_map/all_to_all | solution.py:142
  105.9 2.8 %reduce_sum.101 = f32[8,8,32,256]{3,2,0,1:T(8,128)S(1)} reduce(f32[2,8,8,32,256]{4,3,1,2,0:T(8,128)} %all_to_all.45, f32[]{:T(128)} %constant.84.clone.1), dimensions={0}, to_apply=%region_9.10 | reduce | flops 524288 | bytes 6291460 | tf_op jit(solution)/shard_map/reduce_sum | solution.py:142
  108.9 54.2 %all_to_all.46 = f32[8,8,32,256]{3,2,1,0:T(8,128)S(1)} all-to-all(f32[8,8,32,256]{3,2,1,0:T(8,128)S(1)} %copy.33), channel_id=1, replica_groups=mesh['z'=8,'y'=8,'c'=2,'head'=4] {'y'}, dimensions={0} | all-to-all | bytes 4194304 | tf_op jit(solution)/shard_map/all_to_all | solution.py:142
  163.3 14.7 %all_to_all.47 = f32[8,32,256]{2,1,0:T(8,128)S(1)} all-to-all(f32[8,32,256]{2,1,0:T(8,128)S(1)} %reduce_sum.102), channel_id=1, replica_groups=mesh['z'=8,'y'=8,'c'=2,'head'=4] {'z'}, dimensions={0} | all-to-all | bytes 524288 | tf_op jit(solution)/shard_map/all_to_all | solution.py:142
  178.0 0.6 fusion.66
  (46 shorter events, 5.1 us)
Async XLA Ops:
  0.6 20.6 %copy-start = (bf16[4096,128]{1,0:T(8,128)(2,1)S(1)}, bf16[4096,128]{1,0:T(8,128)(2,1)}, u32[]{:S(2)}) copy-start(bf16[4096,128]{1,0:T(8,128)(2,1)} %param.11) | copy-start | bytes 3145732
  0.6 21.0 %copy-start.1 = (bf16[4096,128]{1,0:T(8,128)(2,1)S(1)}, bf16[4096,128]{1,0:T(8,128)(2,1)}, u32[]{:S(2)}) copy-start(bf16[4096,128]{1,0:T(8,128)(2,1)} %param.10) | copy-start | bytes 3145732
  3.1 18.1 %all-to-all-start = ((bf16[4,128,1024]{1,2,0:T(8,128)(2,1)}), bf16[4,128,1024]{1,2,0:T(8,128)(2,1)S(1)}, u32[]{:S(2)}, u32[]{:S(2)}) async-start(bf16[4,128,1024]{1,2,0:T(8,128)(2,1)} %broadcast_in_dim.20), calls=%async_computation | async-start | bytes 2097152 | tf_op jit(solution)/shard_map/all_to_all | solution.py:34
  23.4 32.2 %all-to-all-start.1 = ((bf16[128,2,512]{2,1,0:T(2,128)(2,1)}), bf16[128,2,512]{2,1,0:T(2,128)(2,1)S(1)}, u32[]{:S(2)}, u32[]{:S(2)}) async-start(bf16[128,2,512]{2,1,0:T(2,128)(2,1)} %all_to_all.29), calls=%async_computation.1 | async-start | bytes 524288 | tf_op jit(solution)/shard_map/all_to_all | solution.py:73
  56.3 8.6 %collective-permute-start = (bf16[64,256]{1,0:T(8,128)(2,1)S(1)}, bf16[64,256]{1,0:T(8,128)(2,1)S(1)}, u32[]{:S(2)}, u32[]{:S(2)}) collective-permute-start(bf16[64,256]{1,0:T(8,128)(2,1)S(1)} %slice.117), channel_id=1, source_target_pairs={{0,4},{4,8},{8,12},{12,16},{16,20},{20,24},{24,28},{28,32},{32,36}... | collective-permute-start | bytes 98312 | tf_op jit(solution)/shard_map/ppermute | solution.py:21
  66.5 4.4 %collective-permute-start.1 = (f32[64,256]{0,1:T(8,128)S(1)}, f32[64,256]{0,1:T(8,128)S(1)}, u32[]{:S(2)}, u32[]{:S(2)}) collective-permute-start(f32[64,256]{0,1:T(8,128)S(1)} %get-tuple-element.27), channel_id=1, source_target_pairs={{0,508},{4,0},{8,4},{12,8},{16,12},{20,16},{24,20},{28,24},{32,28}... | collective-permute-start | bytes 196616 | tf_op jit(solution)/shard_map/ppermute | solution.py:21

commit v4 on v3

--- a/solution.py
+++ b/solution.py
@@ -138,8 +138,11 @@
     rows = feat_count // (nz * ny * nc)
     blocks = whole.reshape(tok_count, nz, ny, nc, rows)
     grads = jnp.einsum("pzyck,ph->cyzkh", blocks, combined, preferred_element_type=jnp.float32)
-    for axis in ("c", "y", "z"):
-        grads = jnp.sum(lax.all_to_all(grads, axis, 0, 0, tiled=True), axis=0)
+    grads = jnp.sum(lax.all_to_all(grads, "c", 0, 0, tiled=True), axis=0)
+    grads = jnp.sum(
+        lax.all_to_all(grads.astype(jnp.bfloat16), "y", 0, 0, tiled=True).astype(jnp.float32), axis=0
+    )
+    grads = jnp.sum(lax.all_to_all(grads, "z", 0, 0, tiled=True), axis=0)
     grads = grads.reshape(rows, 2 * head_width)
     return (grads[:, :head_width], grads[:, head_width:])
 

time: 180 us -> 158 us (0.88)
  blocking collectives: 97.8 us -> 75.3 us
    all_to_all x3, blocking collectives: 77.1 us -> 54.6 us  [the longest x1 31.7 us: per_device(): lax.all_to_all(grads.astype(jnp.bfloat16), 'y', 0, 0, tiled=True)]
where the time goes in v4:
time: 158 us; the launch traced here: 156 us
  blocking collectives  75.3 us (48%)
  starting transfers between devices  30.7 us (19%)
  waiting for transfers between devices  27.9 us (18%)
  local copies, waits for them, and re-layouts  7.64 us (5%)
  other arithmetic  7.54 us (5%)
  matrix products  5.97 us (4%)
    all_to_all x1, blocking collectives, per_device(): lax.all_to_all(grads.astype(jnp.bfloat16), 'y', 0, 0, tiled=True)  31.7 us
    all_to_all x1, blocking collectives, per_device(): lax.all_to_all(return_rows, SEQ, split_axis=0, concat_axis=0, tiled=True)  20.7 us
    all_to_all x1, starting transfers between devices, per_device(): lax.all_to_all(send_rows, SEQ, split_axis=0, concat_axis=0, tiled=True)  17.5 us
    all_to_all x1, waiting for transfers between devices, per_device(): lax.all_to_all(send_rows, SEQ, split_axis=0, concat_axis=0, tiled=True)  14.7 us
    all_to_all x1, blocking collectives, per_device(): grads = jnp.sum(lax.all_to_all(grads, 'z', 0, 0, tiled=True), axis=0)  14.7 us
    all_to_all x1, starting transfers between devices, per_device(): gathered = lax.all_to_all(spread, 'head', 0, 0, tiled=True)  9.31 us
    ppermute x2, waiting for transfers between devices, shifted(): return lax.ppermute(value, axis, pairs)  8.86 us
    all_to_all x1, blocking collectives, per_device(): grads = jnp.sum(lax.all_to_all(grads, 'c', 0, 0, tiled=True), axis=0)  8.17 us
  transfers between devices with their start and end apart: 4, of which 4 were waited for; matrix products, arithmetic and copies ran while one was open for 3% of the time, Pallas kernels for 0%

profile of v4, /device:TPU:6, one launch (start us, length us, event | category | flops | bytes accessed | tf_op | source)
XLA Modules:
  0.0 156.0 jit_solution(4906719321701343881)
XLA Ops:
  0.7 1.3 copy.28
  1.9 1.1 broadcast_in_dim.20
  3.1 9.3 %all-to-all-start = ((bf16[4,128,1024]{1,2,0:T(8,128)(2,1)}), bf16[4,128,1024]{1,2,0:T(8,128)(2,1)S(1)}, u32[]{:S(2)}, u32[]{:S(2)}) async-start(bf16[4,128,1024]{1,2,0:T(8,128)(2,1)} %broadcast_in_dim.20), calls=%async_computation | async-start | bytes 2097152 | tf_op jit(solution)/shard_map/all_to_all | solution.py:34
  12.4 0.7 and_select_fusion.2
  13.2 0.9 copy.29
  14.1 0.7 compare_reduce_fusion
  14.7 0.7 fusion.52
  15.5 1.3 broadcast_select_fusion
  16.9 4.3 %all-to-all-done = bf16[4,128,1024]{1,2,0:T(8,128)(2,1)S(1)} async-done(((bf16[4,128,1024]{1,2,0:T(8,128)(2,1)}), bf16[4,128,1024]{1,2,0:T(8,128)(2,1)S(1)}, u32[]{:S(2)}, u32[]{:S(2)}) %all-to-all-start) | async-done | bytes 1048608 | tf_op jit(solution)/shard_map/all_to_all | solution.py:34
  22.6 0.8 all_to_all.29
  23.4 17.5 %all-to-all-start.1 = ((bf16[128,2,512]{2,1,0:T(2,128)(2,1)}), bf16[128,2,512]{2,1,0:T(2,128)(2,1)S(1)}, u32[]{:S(2)}, u32[]{:S(2)}) async-start(bf16[128,2,512]{2,1,0:T(2,128)(2,1)} %all_to_all.29), calls=%async_computation.1 | async-start | bytes 524288 | tf_op jit(solution)/shard_map/all_to_all | solution.py:73
  40.9 14.7 %all-to-all-done.1 = bf16[128,2,512]{2,1,0:T(2,128)(2,1)S(1)} async-done(((bf16[128,2,512]{2,1,0:T(2,128)(2,1)}), bf16[128,2,512]{2,1,0:T(2,128)(2,1)S(1)}, u32[]{:S(2)}, u32[]{:S(2)}) %all-to-all-start.1) | async-done | bytes 262176 | tf_op jit(solution)/shard_map/all_to_all | solution.py:73
  56.3 2.0 %collective-permute-start = (bf16[64,256]{1,0:T(8,128)(2,1)S(1)}, bf16[64,256]{1,0:T(8,128)(2,1)S(1)}, u32[]{:S(2)}, u32[]{:S(2)}) collective-permute-start(bf16[64,256]{1,0:T(8,128)(2,1)S(1)} %slice.117), channel_id=1, source_target_pairs={{0,4},{4,8},{8,12},{12,16},{16,20},{20,24},{24,28},{28,32},{32,36}... | collective-permute-start | bytes 98312 | tf_op jit(solution)/shard_map/ppermute | solution.py:21
  58.3 6.5 %collective-permute-done = bf16[64,256]{1,0:T(8,128)(2,1)S(1)} collective-permute-done((bf16[64,256]{1,0:T(8,128)(2,1)S(1)}, bf16[64,256]{1,0:T(8,128)(2,1)S(1)}, u32[]{:S(2)}, u32[]{:S(2)}) %collective-permute-start) | collective-permute-done | bytes 32800 | tf_op jit(solution)/shard_map/ppermute | solution.py:21
  66.5 1.9 %collective-permute-start.1 = (f32[64,256]{0,1:T(8,128)S(1)}, f32[64,256]{0,1:T(8,128)S(1)}, u32[]{:S(2)}, u32[]{:S(2)}) collective-permute-start(f32[64,256]{0,1:T(8,128)S(1)} %get-tuple-element.27), channel_id=1, source_target_pairs={{0,508},{4,0},{8,4},{12,8},{16,12},{20,16},{24,20},{28,24},{32,28}... | collective-permute-start | bytes 196616 | tf_op jit(solution)/shard_map/ppermute | solution.py:21
  68.6 2.4 %collective-permute-done.1 = f32[64,256]{0,1:T(8,128)S(1)} collective-permute-done((f32[64,256]{0,1:T(8,128)S(1)}, f32[64,256]{0,1:T(8,128)S(1)}, u32[]{:S(2)}, u32[]{:S(2)}) %collective-permute-start.1) | collective-permute-done | bytes 65568 | tf_op jit(solution)/shard_map/ppermute | solution.py:21
  71.6 20.7 %all_to_all.44 = bf16[128,2,256]{2,1,0:T(2,128)(2,1)S(1)} all-to-all(bf16[128,2,256]{2,1,0:T(2,128)(2,1)S(1)} %all_to_all.32), channel_id=1, replica_groups=mesh['z'=8,'y'=8,'c'=2,'head'=4] {'z','y','c'}, dimensions={0} | all-to-all | bytes 262144 | tf_op jit(solution)/shard_map/all_to_all | solution.py:133
  92.4 2.8 %fusion.2 = f32[256,4096]{0,1} fusion(bf16[128,4096]{0,1:T(8,128)(2,1)S(1)} %bitcast.75, bf16[256,256]{1,0:T(8,128)(2,1)S(1)} %all_to_all.34, s32[128]{0:T(128)S(1)} %fusion.52), kind=kOutput, calls=%fused_computation.8 | convolution fusion | flops 285278208 | bytes 5374464
  95.2 2.5 %copy.31 = f32[2,8,8,32,256]{4,3,1,2,0:T(8,128)S(1)} copy(f32[2,8,8,32,256]{4,3,0,1,2:T(8,128)} %bitcast.72) | data formatting | bytes 8388608 | tf_op jit(solution)/shard_map/pzyck,ph->cyzkh/transpose | solution.py:140
  97.8 8.2 %all_to_all.45 = f32[2,8,8,32,256]{4,3,1,2,0:T(8,128)} all-to-all(f32[2,8,8,32,256]{4,3,1,2,0:T(8,128)S(1)} %copy.31), channel_id=1, replica_groups=mesh['z'=8,'y'=8,'c'=2,'head'=4] {'c'}, dimensions={0} | all-to-all | bytes 8388608 | tf_op jit(solution)/shard_map/all_to_all | solution.py:141
  105.9 2.8 %reduce_sum.101 = bf16[8,8,32,256]{3,2,0,1:T(8,128)(2,1)S(1)} reduce(f32[2,8,8,32,256]{4,3,1,2,0:T(8,128)} %all_to_all.45, f32[]{:T(128)} %constant.84.clone.1), dimensions={0}, to_apply=%region_9.10 | reduce | flops 524288 | bytes 5242884 | tf_op jit(solution)/shard_map/reduce_sum | solution.py:141
  108.8 31.7 %all_to_all.46 = bf16[8,8,32,256]{3,2,1,0:T(8,128)(2,1)S(1)} all-to-all(bf16[8,8,32,256]{3,2,1,0:T(8,128)(2,1)S(1)} %copy.33), channel_id=1, replica_groups=mesh['z'=8,'y'=8,'c'=2,'head'=4] {'y'}, dimensions={0} | all-to-all | bytes 2097152 | tf_op jit(solution)/shard_map/all_to_all | solution.py:143
  140.7 14.7 %all_to_all.47 = f32[8,32,256]{2,1,0:T(8,128)S(1)} all-to-all(f32[8,32,256]{2,1,0:T(8,128)S(1)} %convert_reduce_fusion), channel_id=1, replica_groups=mesh['z'=8,'y'=8,'c'=2,'head'=4] {'z'}, dimensions={0} | all-to-all | bytes 524288 | tf_op jit(solution)/shard_map/all_to_all | solution.py:145
  155.4 0.6 fusion.66
  (46 shorter events, 5.1 us)
Async XLA Ops:
  0.6 20.6 %copy-start = (bf16[4096,128]{1,0:T(8,128)(2,1)S(1)}, bf16[4096,128]{1,0:T(8,128)(2,1)}, u32[]{:S(2)}) copy-start(bf16[4096,128]{1,0:T(8,128)(2,1)} %param.11) | copy-start | bytes 3145732
  0.6 21.0 %copy-start.1 = (bf16[4096,128]{1,0:T(8,128)(2,1)S(1)}, bf16[4096,128]{1,0:T(8,128)(2,1)}, u32[]{:S(2)}) copy-start(bf16[4096,128]{1,0:T(8,128)(2,1)} %param.10) | copy-start | bytes 3145732
  3.1 18.1 %all-to-all-start = ((bf16[4,128,1024]{1,2,0:T(8,128)(2,1)}), bf16[4,128,1024]{1,2,0:T(8,128)(2,1)S(1)}, u32[]{:S(2)}, u32[]{:S(2)}) async-start(bf16[4,128,1024]{1,2,0:T(8,128)(2,1)} %broadcast_in_dim.20), calls=%async_computation | async-start | bytes 2097152 | tf_op jit(solution)/shard_map/all_to_all | solution.py:34
  23.4 32.2 %all-to-all-start.1 = ((bf16[128,2,512]{2,1,0:T(2,128)(2,1)}), bf16[128,2,512]{2,1,0:T(2,128)(2,1)S(1)}, u32[]{:S(2)}, u32[]{:S(2)}) async-start(bf16[128,2,512]{2,1,0:T(2,128)(2,1)} %all_to_all.29), calls=%async_computation.1 | async-start | bytes 524288 | tf_op jit(solution)/shard_map/all_to_all | solution.py:73
  56.3 8.6 %collective-permute-start = (bf16[64,256]{1,0:T(8,128)(2,1)S(1)}, bf16[64,256]{1,0:T(8,128)(2,1)S(1)}, u32[]{:S(2)}, u32[]{:S(2)}) collective-permute-start(bf16[64,256]{1,0:T(8,128)(2,1)S(1)} %slice.117), channel_id=1, source_target_pairs={{0,4},{4,8},{8,12},{12,16},{16,20},{20,24},{24,28},{28,32},{32,36}... | collective-permute-start | bytes 98312 | tf_op jit(solution)/shard_map/ppermute | solution.py:21
  66.5 4.4 %collective-permute-start.1 = (f32[64,256]{0,1:T(8,128)S(1)}, f32[64,256]{0,1:T(8,128)S(1)}, u32[]{:S(2)}, u32[]{:S(2)}) collective-permute-start(f32[64,256]{0,1:T(8,128)S(1)} %get-tuple-element.27), channel_id=1, source_target_pairs={{0,508},{4,0},{8,4},{12,8},{16,12},{20,16},{24,20},{28,24},{32,28}... | collective-permute-start | bytes 196616 | tf_op jit(solution)/shard_map/ppermute | solution.py:21

commit v5 on v4

--- a/solution.py
+++ b/solution.py
@@ -130,15 +130,40 @@
     return_rows = lax.dot_general(
         to_sorted, sorted_grads, (((0,), (0,)), ((), ())), preferred_element_type=jnp.float32
     ).astype(jnp.bfloat16)
-    back_rows = lax.all_to_all(return_rows, SEQ, split_axis=0, concat_axis=0, tiled=True)
-    combined = lax.dot_general(
-        to_buffer, back_rows, (((0,), (0,)), ((), ())), preferred_element_type=jnp.float32
-    ).astype(jnp.bfloat16)
     nz, ny, nc = (lax.axis_size(a) for a in SEQ)
+    my_core = lax.axis_index("c")
+    by_peer = return_rows.reshape(peer_count, capacity, 2 * head_width)
+    peer_core = jnp.arange(peer_count) % nc
+    peer_chip = jnp.arange(peer_count) - peer_core
+    shifted_peers = [peer_chip + (peer_core + j) % nc for j in range(nc)]
+    to_chip = jnp.stack([by_peer[p] for p in shifted_peers], axis=1)
+    back_rows = lax.all_to_all(to_chip, SEQ, split_axis=0, concat_axis=0, tiled=True)
     rows = feat_count // (nz * ny * nc)
-    blocks = whole.reshape(tok_count, nz, ny, nc, rows)
-    grads = jnp.einsum("pzyck,ph->cyzkh", blocks, combined, preferred_element_type=jnp.float32)
-    grads = jnp.sum(lax.all_to_all(grads, "c", 0, 0, tiled=True), axis=0)
+    blocks = whole.reshape(tok_count, nz, ny, nc, rows).transpose(3, 0, 2, 1, 4)
+    shares = blocks.reshape(nc, tok_count, ny * nz * rows)
+    index_block = jnp.zeros((tok_count, head_width), jnp.bfloat16).at[:, 0].set(
+        buffer_index.astype(jnp.bfloat16)
+    )
+    outgoing_shares = jnp.concatenate(
+        [shares, jnp.broadcast_to(index_block[None], (nc, tok_count, head_width))], axis=2
+    )
+    chip_shares = lax.all_to_all(outgoing_shares, "c", 0, 0, tiled=True)
+    grads = jnp.zeros((ny * nz * rows, 2 * head_width), jnp.float32)
+    for source in range(nc):
+        offset = (source - my_core) % nc
+        rows_in = jnp.take(back_rows, offset, axis=1).reshape(peer_count * capacity, 2 * head_width)
+        source_index = chip_shares[source, :, ny * nz * rows].astype(jnp.int32)
+        source_buffer = (buffer_ids[:, None] == source_index[None, :]).astype(jnp.bfloat16)
+        source_grads = lax.dot_general(
+            source_buffer, rows_in, (((0,), (0,)), ((), ())), preferred_element_type=jnp.float32
+        ).astype(jnp.bfloat16)
+        grads = grads + lax.dot_general(
+            chip_shares[source, :, : ny * nz * rows],
+            source_grads,
+            (((0,), (0,)), ((), ())),
+            preferred_element_type=jnp.float32,
+        )
+    grads = grads.reshape(ny, nz, rows, 2 * head_width)
     grads = jnp.sum(
         lax.all_to_all(grads.astype(jnp.bfloat16), "y", 0, 0, tiled=True).astype(jnp.float32), axis=0
     )

time: 158 us -> 156 us (0.987)
  blocking collectives: 75.3 us -> 47.5 us
  waiting for transfers between devices: 27.9 us -> 43 us
  starting transfers between devices: 30.7 us -> 43.5 us
  other arithmetic: 7.54 us -> 5.84 us
    all_to_all x2 -> x0, blocking collectives: 28.9 us -> none  [the longest x1 20.7 us: per_device(): lax.all_to_all(return_rows, SEQ, split_axis=0, concat_axis=0, tiled=True)]
    all_to_all x0 -> x2, waiting for transfers between devices: none -> 14.7 us  [the longest x1 14.7 us: per_device(): lax.all_to_all(to_chip, SEQ, split_axis=0, concat_axis=0, tiled=True)]
    all_to_all x0 -> x2, starting transfers between devices: none -> 12.3 us  [the longest x1 8.7 us: per_device(): lax.all_to_all(to_chip, SEQ, split_axis=0, concat_axis=0, tiled=True)]
    dot_general x0 -> x2, matrix products: none -> 4.4 us  [per_device(): lax.dot_general(chip_shares[source, :, :ny * nz * rows], source_grads, ((...]
    unnamed x1 -> x0, matrix products: 2.84 us -> none
    reduce_sum x1 -> x0, other arithmetic: 2.75 us -> none  [per_device(): grads = jnp.sum(lax.all_to_all(grads, 'c', 0, 0, tiled=True), axis=0)]
    transpose x1, local copies, waits for them, and re-layouts: 2.5 us -> 0.09 us  [per_device(): blocks = whole.reshape(tok_count, nz, ny, nc, rows).transpose(3, 0, 2, 1, 4)]
    all_to_all x1, waiting for transfers between devices: 4.33 us -> 6.33 us  [per_device(): gathered = lax.all_to_all(spread, 'head', 0, 0, tiled=True)]
  transfers between devices with their start and end apart: 4 -> 6, of which waited for: 4 -> 5; matrix products, arithmetic and copies ran while one was open for 3% -> 6% of each run, Pallas kernels for 0% -> 0%
where the time goes in v5:
time: 156 us; the launch traced here: 155 us
  blocking collectives  47.5 us (30%)
  starting transfers between devices  43.5 us (28%)
  waiting for transfers between devices  43 us (28%)
  matrix products  7.52 us (5%)
  local copies, waits for them, and re-layouts  6.17 us (4%)
  other arithmetic  5.84 us (4%)
    all_to_all x1, blocking collectives, per_device(): lax.all_to_all(grads.astype(jnp.bfloat16), 'y', 0, 0, tiled=True)  32.7 us
    all_to_all x1, starting transfers between devices, per_device(): lax.all_to_all(send_rows, SEQ, split_axis=0, concat_axis=0, tiled=True)  17.5 us
    all_to_all x1, blocking collectives, per_device(): grads = jnp.sum(lax.all_to_all(grads, 'z', 0, 0, tiled=True), axis=0)  14.7 us
    all_to_all x1, waiting for transfers between devices, per_device(): lax.all_to_all(to_chip, SEQ, split_axis=0, concat_axis=0, tiled=True)  14.7 us
    all_to_all x1, waiting for transfers between devices, per_device(): lax.all_to_all(send_rows, SEQ, split_axis=0, concat_axis=0, tiled=True)  13.5 us
    all_to_all x1, starting transfers between devices, per_device(): gathered = lax.all_to_all(spread, 'head', 0, 0, tiled=True)  9.44 us
    all_to_all x1, starting transfers between devices, per_device(): lax.all_to_all(to_chip, SEQ, split_axis=0, concat_axis=0, tiled=True)  8.7 us
    ppermute x2, waiting for transfers between devices, shifted(): return lax.ppermute(value, axis, pairs)  8.5 us
  transfers between devices with their start and end apart: 6, of which 5 were waited for; matrix products, arithmetic and copies ran while one was open for 6% of the time, Pallas kernels for 0%

profile of v5, /device:TPU:6, one launch (start us, length us, event | category | flops | bytes accessed | tf_op | source)
XLA Modules:
  0.0 154.6 jit_solution(5253804251405767774)
XLA Ops:
  0.6 1.2 copy.21
  1.9 1.1 broadcast_in_dim.34
  3.0 9.4 %all-to-all-start = ((bf16[4,128,1024]{1,2,0:T(8,128)(2,1)}), bf16[4,128,1024]{1,2,0:T(8,128)(2,1)S(1)}, u32[]{:S(2)}, u32[]{:S(2)}) async-start(bf16[4,128,1024]{1,2,0:T(8,128)(2,1)} %broadcast_in_dim.34), calls=%async_computation | async-start | bytes 2097152 | tf_op jit(solution)/shard_map/all_to_all | solution.py:34
  13.6 0.7 broadcast_select_fusion.3
  14.2 0.7 broadcast_select_fusion.2
  14.9 6.3 %all-to-all-done = bf16[4,128,1024]{1,2,0:T(8,128)(2,1)S(1)} async-done(((bf16[4,128,1024]{1,2,0:T(8,128)(2,1)}), bf16[4,128,1024]{1,2,0:T(8,128)(2,1)S(1)}, u32[]{:S(2)}, u32[]{:S(2)}) %all-to-all-start) | async-done | bytes 1048608 | tf_op jit(solution)/shard_map/all_to_all | solution.py:34
  22.6 0.8 all_to_all.25
  23.4 17.5 %all-to-all-start.2 = ((bf16[128,2,512]{2,1,0:T(2,128)(2,1)}), bf16[128,2,512]{2,1,0:T(2,128)(2,1)S(1)}, u32[]{:S(2)}, u32[]{:S(2)}) async-start(bf16[128,2,512]{2,1,0:T(2,128)(2,1)} %all_to_all.25), calls=%async_computation.2 | async-start | bytes 524288 | tf_op jit(solution)/shard_map/all_to_all | solution.py:73
  41.1 1.1 pad_maximum_fusion
  42.2 13.5 %all-to-all-done.2 = bf16[128,2,512]{2,1,0:T(2,128)(2,1)S(1)} async-done(((bf16[128,2,512]{2,1,0:T(2,128)(2,1)}), bf16[128,2,512]{2,1,0:T(2,128)(2,1)S(1)}, u32[]{:S(2)}, u32[]{:S(2)}) %all-to-all-start.2) | async-done | bytes 262176 | tf_op jit(solution)/shard_map/all_to_all | solution.py:73
  55.6 3.6 %all-to-all-start.1 = ((bf16[2,128,2176]{1,2,0:T(8,128)(2,1)}), bf16[2,128,2176]{1,2,0:T(8,128)(2,1)S(1)}, u32[]{:S(2)}, u32[]{:S(2)}) async-start(bf16[2,128,2176]{1,2,0:T(8,128)(2,1)} %pad_maximum_fusion), calls=%async_computation.1 | async-start | bytes 2228224 | tf_op jit(solution)/shard_map/all_to_all | solution.py:150
  59.9 2.4 %collective-permute-start = (bf16[64,256]{1,0:T(8,128)(2,1)S(1)}, bf16[64,256]{1,0:T(8,128)(2,1)S(1)}, u32[]{:S(2)}, u32[]{:S(2)}) collective-permute-start(bf16[64,256]{1,0:T(8,128)(2,1)S(1)} %slice.164), channel_id=1, source_target_pairs={{0,4},{4,8},{8,12},{12,16},{16,20},{20,24},{24,28},{28,32},{32,36}... | collective-permute-start | bytes 98312 | tf_op jit(solution)/shard_map/ppermute | solution.py:21
  62.3 6.1 %collective-permute-done = bf16[64,256]{1,0:T(8,128)(2,1)S(1)} collective-permute-done((bf16[64,256]{1,0:T(8,128)(2,1)S(1)}, bf16[64,256]{1,0:T(8,128)(2,1)S(1)}, u32[]{:S(2)}, u32[]{:S(2)}) %collective-permute-start) | collective-permute-done | bytes 32800 | tf_op jit(solution)/shard_map/ppermute | solution.py:21
  70.2 1.9 %collective-permute-start.1 = (f32[64,256]{0,1:T(8,128)S(1)}, f32[64,256]{0,1:T(8,128)S(1)}, u32[]{:S(2)}, u32[]{:S(2)}) collective-permute-start(f32[64,256]{0,1:T(8,128)S(1)} %get-tuple-element.57), channel_id=1, source_target_pairs={{0,508},{4,0},{8,4},{12,8},{16,12},{20,16},{24,20},{28,24},{32,28}... | collective-permute-start | bytes 196616 | tf_op jit(solution)/shard_map/ppermute | solution.py:21
  72.2 2.4 %collective-permute-done.1 = f32[64,256]{0,1:T(8,128)S(1)} collective-permute-done((f32[64,256]{0,1:T(8,128)S(1)}, f32[64,256]{0,1:T(8,128)S(1)}, u32[]{:S(2)}, u32[]{:S(2)}) %collective-permute-start.1) | collective-permute-done | bytes 65568 | tf_op jit(solution)/shard_map/ppermute | solution.py:21
  75.3 0.9 gather_fusion.1
  76.2 0.9 gather_fusion
  77.1 1.0 pad_maximum_fusion.1
  78.1 8.7 %all-to-all-start.3 = ((bf16[128,2,2,256]{3,2,1,0:T(2,128)(2,1)}), bf16[128,2,2,256]{3,2,1,0:T(2,128)(2,1)S(1)}, u32[]{:S(2)}, u32[]{:S(2)}) async-start(bf16[128,2,2,256]{3,2,1,0:T(2,128)(2,1)} %pad_maximum_fusion.1), calls=%async_computation.3 | async-start | bytes 524288 | tf_op jit(solution)/shard_map/all_to_all | solution.py:140
  86.9 14.7 %all-to-all-done.3 = bf16[128,2,2,256]{3,2,1,0:T(2,128)(2,1)S(1)} async-done(((bf16[128,2,2,256]{3,2,1,0:T(2,128)(2,1)}), bf16[128,2,2,256]{3,2,1,0:T(2,128)(2,1)S(1)}, u32[]{:S(2)}, u32[]{:S(2)}) %all-to-all-start.3) | async-done | bytes 262176 | tf_op jit(solution)/shard_map/all_to_all | solution.py:140
  101.9 1.7 %fusion.5 = f32[2048,256]{1,0:T(8,128)S(1)} fusion(bf16[256,256]{1,0:T(8,128)(2,1)S(1)} %reshape.438, bf16[2,128,2176]{1,2,0:T(8,128)(2,1)} %copy-done.1, s32[128]{0:T(128)S(1)} %get-tuple-element.53), kind=kOutput, calls=%fused_computation.18 | convolution fusion | flops 151060480 | bytes 2753024 | tf_op jit(solution)/shard_map/dot_general | solution.py:160
  103.6 2.7 %fusion.1 = bf16[2048,256]{1,0:T(8,128)(2,1)} fusion(f32[2048,256]{1,0:T(8,128)S(1)} %fusion.5, bf16[256,256]{1,0:T(8,128)(2,1)S(1)} %reshape.439, bf16[2,128,2176]{1,2,0:T(8,128)(2,1)} %copy-done.1, s32[128]{0:T(128)S(1)} %get-tuple-element.52), kind=kOutput, calls=%fused_computation.4 | convolution fusion | flops 152109056 | bytes 3801600 | tf_op jit(solution)/shard_map/dot_general | solution.py:160
  106.3 32.7 %all_to_all.37 = bf16[8,8,32,256]{3,2,1,0:T(8,128)(2,1)S(1)} all-to-all(bf16[8,8,32,256]{3,2,1,0:T(8,128)(2,1)} %bitcast.106), channel_id=1, replica_groups=mesh['z'=8,'y'=8,'c'=2,'head'=4] {'y'}, dimensions={0} | all-to-all | bytes 2097152 | tf_op jit(solution)/shard_map/all_to_all | solution.py:168
  139.2 14.7 %all_to_all.38 = f32[8,32,256]{2,1,0:T(8,128)S(1)} all-to-all(f32[8,32,256]{2,1,0:T(8,128)S(1)} %convert_reduce_fusion), channel_id=1, replica_groups=mesh['z'=8,'y'=8,'c'=2,'head'=4] {'z'}, dimensions={0} | all-to-all | bytes 524288 | tf_op jit(solution)/shard_map/all_to_all | solution.py:170
  (66 shorter events, 6.8 us)
Async XLA Ops:
  0.6 20.6 %copy-start = (bf16[4096,128]{1,0:T(8,128)(2,1)S(1)}, bf16[4096,128]{1,0:T(8,128)(2,1)}, u32[]{:S(2)}) copy-start(bf16[4096,128]{1,0:T(8,128)(2,1)} %param.15) | copy-start | bytes 3145732
  3.0 9.5 %copy-start.4 = (s32[1,128]{1,0:T(1,128)S(1)}, s32[1,128]{1,0:T(1,128)}, u32[]{:S(2)}) copy-start(s32[1,128]{1,0:T(1,128)} %param.17) | copy-start | bytes 1540
  3.0 9.7 %copy-start.3 = (bf16[128,128]{1,0:T(8,128)(2,1)S(1)}, bf16[128,128]{1,0:T(8,128)(2,1)}, u32[]{:S(2)}) copy-start(bf16[128,128]{1,0:T(8,128)(2,1)} %param.16) | copy-start | bytes 98308
  3.0 18.3 %all-to-all-start = ((bf16[4,128,1024]{1,2,0:T(8,128)(2,1)}), bf16[4,128,1024]{1,2,0:T(8,128)(2,1)S(1)}, u32[]{:S(2)}, u32[]{:S(2)}) async-start(bf16[4,128,1024]{1,2,0:T(8,128)(2,1)} %broadcast_in_dim.34), calls=%async_computation | async-start | bytes 2097152 | tf_op jit(solution)/shard_map/all_to_all | solution.py:34
  12.6 9.1 %copy-start.2 = (bf16[4096,128]{1,0:T(8,128)(2,1)S(1)}, bf16[4096,128]{1,0:T(8,128)(2,1)}, u32[]{:S(2)}) copy-start(bf16[4096,128]{1,0:T(8,128)(2,1)} %param.14) | copy-start | bytes 3145732
  23.4 32.2 %all-to-all-start.2 = ((bf16[128,2,512]{2,1,0:T(2,128)(2,1)}), bf16[128,2,512]{2,1,0:T(2,128)(2,1)S(1)}, u32[]{:S(2)}, u32[]{:S(2)}) async-start(bf16[128,2,512]{2,1,0:T(2,128)(2,1)} %all_to_all.25), calls=%async_computation.2 | async-start | bytes 524288 | tf_op jit(solution)/shard_map/all_to_all | solution.py:73
  55.6 22.5 %all-to-all-start.1 = ((bf16[2,128,2176]{1,2,0:T(8,128)(2,1)}), bf16[2,128,2176]{1,2,0:T(8,128)(2,1)S(1)}, u32[]{:S(2)}, u32[]{:S(2)}) async-start(bf16[2,128,2176]{1,2,0:T(8,128)(2,1)} %pad_maximum_fusion), calls=%async_computation.1 | async-start | bytes 2228224 | tf_op jit(solution)/shard_map/all_to_all | solution.py:150
  59.9 8.6 %collective-permute-start = (bf16[64,256]{1,0:T(8,128)(2,1)S(1)}, bf16[64,256]{1,0:T(8,128)(2,1)S(1)}, u32[]{:S(2)}, u32[]{:S(2)}) collective-permute-start(bf16[64,256]{1,0:T(8,128)(2,1)S(1)} %slice.164), channel_id=1, source_target_pairs={{0,4},{4,8},{8,12},{12,16},{16,20},{20,24},{24,28},{28,32},{32,36}... | collective-permute-start | bytes 98312 | tf_op jit(solution)/shard_map/ppermute | solution.py:21
  70.2 4.4 %collective-permute-start.1 = (f32[64,256]{0,1:T(8,128)S(1)}, f32[64,256]{0,1:T(8,128)S(1)}, u32[]{:S(2)}, u32[]{:S(2)}) collective-permute-start(f32[64,256]{0,1:T(8,128)S(1)} %get-tuple-element.57), channel_id=1, source_target_pairs={{0,508},{4,0},{8,4},{12,8},{16,12},{20,16},{24,20},{28,24},{32,28}... | collective-permute-start | bytes 196616 | tf_op jit(solution)/shard_map/ppermute | solution.py:21
  78.1 23.8 %copy-start.1 = (bf16[2,128,2176]{1,2,0:T(8,128)(2,1)}, bf16[2,128,2176]{1,2,0:T(8,128)(2,1)S(1)}, u32[]{:S(2)}) copy-start(bf16[2,128,2176]{1,2,0:T(8,128)(2,1)S(1)} %all-to-all-done.1) | copy-start | bytes 3342340
  78.1 23.4 %all-to-all-start.3 = ((bf16[128,2,2,256]{3,2,1,0:T(2,128)(2,1)}), bf16[128,2,2,256]{3,2,1,0:T(2,128)(2,1)S(1)}, u32[]{:S(2)}, u32[]{:S(2)}) async-start(bf16[128,2,2,256]{3,2,1,0:T(2,128)(2,1)} %pad_maximum_fusion.1), calls=%async_computation.3 | async-start | bytes 524288 | tf_op jit(solution)/shard_map/all_to_all | solution.py:140

commit v6 on v5

--- a/solution.py
+++ b/solution.py
@@ -139,7 +139,7 @@
     to_chip = jnp.stack([by_peer[p] for p in shifted_peers], axis=1)
     back_rows = lax.all_to_all(to_chip, SEQ, split_axis=0, concat_axis=0, tiled=True)
     rows = feat_count // (nz * ny * nc)
-    blocks = whole.reshape(tok_count, nz, ny, nc, rows).transpose(3, 0, 2, 1, 4)
+    blocks = whole.reshape(tok_count, nz, ny, nc, rows).transpose(3, 0, 1, 2, 4)
     shares = blocks.reshape(nc, tok_count, ny * nz * rows)
     index_block = jnp.zeros((tok_count, head_width), jnp.bfloat16).at[:, 0].set(
         buffer_index.astype(jnp.bfloat16)
@@ -163,11 +163,11 @@
             (((0,), (0,)), ((), ())),
             preferred_element_type=jnp.float32,
         )
-    grads = grads.reshape(ny, nz, rows, 2 * head_width)
+    grads = grads.reshape(nz * ny, rows, 2 * head_width)
     grads = jnp.sum(
-        lax.all_to_all(grads.astype(jnp.bfloat16), "y", 0, 0, tiled=True).astype(jnp.float32), axis=0
-    )
-    grads = jnp.sum(lax.all_to_all(grads, "z", 0, 0, tiled=True), axis=0)
+        lax.all_to_all(grads.astype(jnp.bfloat16), ("z", "y"), 0, 0, tiled=True).astype(jnp.float32),
+        axis=0,
+    )
     grads = grads.reshape(rows, 2 * head_width)
     return (grads[:, :head_width], grads[:, head_width:])
 

time: 156 us -> 144 us (0.923)
  blocking collectives: 47.5 us -> 34.9 us
    all_to_all x2 -> x1, blocking collectives: 47.5 us -> 34.9 us  [per_device(): lax.all_to_all(grads.astype(jnp.bfloat16), ('z', 'y'), 0, 0, tiled=True)]
  transfers between devices with their start and end apart: 6 -> 6, of which waited for: 5 -> 5; matrix products, arithmetic and copies ran while one was open for 6% -> 7% of each run, Pallas kernels for 0% -> 0%
where the time goes in v6:
time: 144 us; the launch traced here: 142 us
  starting transfers between devices  43.5 us (30%)
  waiting for transfers between devices  43 us (30%)
  blocking collectives  34.9 us (24%)
  matrix products  7.52 us (5%)
  local copies, waits for them, and re-layouts  6.17 us (4%)
  other arithmetic  5.82 us (4%)
    all_to_all x1, blocking collectives, per_device(): lax.all_to_all(grads.astype(jnp.bfloat16), ('z', 'y'), 0, 0, tiled=True)  34.9 us
    all_to_all x1, starting transfers between devices, per_device(): lax.all_to_all(send_rows, SEQ, split_axis=0, concat_axis=0, tiled=True)  17.5 us
    all_to_all x1, waiting for transfers between devices, per_device(): lax.all_to_all(to_chip, SEQ, split_axis=0, concat_axis=0, tiled=True)  14.7 us
    all_to_all x1, waiting for transfers between devices, per_device(): lax.all_to_all(send_rows, SEQ, split_axis=0, concat_axis=0, tiled=True)  13.5 us
    all_to_all x1, starting transfers between devices, per_device(): gathered = lax.all_to_all(spread, 'head', 0, 0, tiled=True)  9.44 us
    all_to_all x1, starting transfers between devices, per_device(): lax.all_to_all(to_chip, SEQ, split_axis=0, concat_axis=0, tiled=True)  8.7 us
    ppermute x2, waiting for transfers between devices, shifted(): return lax.ppermute(value, axis, pairs)  8.5 us
    all_to_all x1, waiting for transfers between devices, per_device(): gathered = lax.all_to_all(spread, 'head', 0, 0, tiled=True)  6.33 us
  transfers between devices with their start and end apart: 6, of which 5 were waited for; matrix products, arithmetic and copies ran while one was open for 7% of the time, Pallas kernels for 0%

profile of v6, /device:TPU:6, one launch (start us, length us, event | category | flops | bytes accessed | tf_op | source)
XLA Modules:
  0.0 142.0 jit_solution(13085121990436158965)
XLA Ops:
  0.6 1.2 copy.21
  1.9 1.1 broadcast_in_dim.34
  3.0 9.4 %all-to-all-start = ((bf16[4,128,1024]{1,2,0:T(8,128)(2,1)}), bf16[4,128,1024]{1,2,0:T(8,128)(2,1)S(1)}, u32[]{:S(2)}, u32[]{:S(2)}) async-start(bf16[4,128,1024]{1,2,0:T(8,128)(2,1)} %broadcast_in_dim.34), calls=%async_computation | async-start | bytes 2097152 | tf_op jit(solution)/shard_map/all_to_all | solution.py:34
  12.8 0.7 compare_reduce_fusion
  13.6 0.7 broadcast_select_fusion.3
  14.2 0.7 broadcast_select_fusion.2
  14.9 6.3 %all-to-all-done = bf16[4,128,1024]{1,2,0:T(8,128)(2,1)S(1)} async-done(((bf16[4,128,1024]{1,2,0:T(8,128)(2,1)}), bf16[4,128,1024]{1,2,0:T(8,128)(2,1)S(1)}, u32[]{:S(2)}, u32[]{:S(2)}) %all-to-all-start) | async-done | bytes 1048608 | tf_op jit(solution)/shard_map/all_to_all | solution.py:34
  22.6 0.8 all_to_all.22
  23.4 17.5 %all-to-all-start.2 = ((bf16[128,2,512]{2,1,0:T(2,128)(2,1)}), bf16[128,2,512]{2,1,0:T(2,128)(2,1)S(1)}, u32[]{:S(2)}, u32[]{:S(2)}) async-start(bf16[128,2,512]{2,1,0:T(2,128)(2,1)} %all_to_all.22), calls=%async_computation.2 | async-start | bytes 524288 | tf_op jit(solution)/shard_map/all_to_all | solution.py:73
  41.1 1.1 pad_maximum_fusion
  42.2 13.5 %all-to-all-done.2 = bf16[128,2,512]{2,1,0:T(2,128)(2,1)S(1)} async-done(((bf16[128,2,512]{2,1,0:T(2,128)(2,1)}), bf16[128,2,512]{2,1,0:T(2,128)(2,1)S(1)}, u32[]{:S(2)}, u32[]{:S(2)}) %all-to-all-start.2) | async-done | bytes 262176 | tf_op jit(solution)/shard_map/all_to_all | solution.py:73
  55.6 3.6 %all-to-all-start.1 = ((bf16[2,128,2176]{1,2,0:T(8,128)(2,1)}), bf16[2,128,2176]{1,2,0:T(8,128)(2,1)S(1)}, u32[]{:S(2)}, u32[]{:S(2)}) async-start(bf16[2,128,2176]{1,2,0:T(8,128)(2,1)} %pad_maximum_fusion), calls=%async_computation.1 | async-start | bytes 2228224 | tf_op jit(solution)/shard_map/all_to_all | solution.py:150
  59.9 2.4 %collective-permute-start = (bf16[64,256]{1,0:T(8,128)(2,1)S(1)}, bf16[64,256]{1,0:T(8,128)(2,1)S(1)}, u32[]{:S(2)}, u32[]{:S(2)}) collective-permute-start(bf16[64,256]{1,0:T(8,128)(2,1)S(1)} %slice.164), channel_id=1, source_target_pairs={{0,4},{4,8},{8,12},{12,16},{16,20},{20,24},{24,28},{28,32},{32,36}... | collective-permute-start | bytes 98312 | tf_op jit(solution)/shard_map/ppermute | solution.py:21
  62.3 6.1 %collective-permute-done = bf16[64,256]{1,0:T(8,128)(2,1)S(1)} collective-permute-done((bf16[64,256]{1,0:T(8,128)(2,1)S(1)}, bf16[64,256]{1,0:T(8,128)(2,1)S(1)}, u32[]{:S(2)}, u32[]{:S(2)}) %collective-permute-start) | collective-permute-done | bytes 32800 | tf_op jit(solution)/shard_map/ppermute | solution.py:21
  70.2 1.9 %collective-permute-start.1 = (f32[64,256]{0,1:T(8,128)S(1)}, f32[64,256]{0,1:T(8,128)S(1)}, u32[]{:S(2)}, u32[]{:S(2)}) collective-permute-start(f32[64,256]{0,1:T(8,128)S(1)} %get-tuple-element.57), channel_id=1, source_target_pairs={{0,508},{4,0},{8,4},{12,8},{16,12},{20,16},{24,20},{28,24},{32,28}... | collective-permute-start | bytes 196616 | tf_op jit(solution)/shard_map/ppermute | solution.py:21
  72.2 2.4 %collective-permute-done.1 = f32[64,256]{0,1:T(8,128)S(1)} collective-permute-done((f32[64,256]{0,1:T(8,128)S(1)}, f32[64,256]{0,1:T(8,128)S(1)}, u32[]{:S(2)}, u32[]{:S(2)}) %collective-permute-start.1) | collective-permute-done | bytes 65568 | tf_op jit(solution)/shard_map/ppermute | solution.py:21
  75.3 0.9 gather_fusion.1
  76.2 0.9 gather_fusion
  77.1 1.0 pad_maximum_fusion.1
  78.1 8.7 %all-to-all-start.3 = ((bf16[128,2,2,256]{3,2,1,0:T(2,128)(2,1)}), bf16[128,2,2,256]{3,2,1,0:T(2,128)(2,1)S(1)}, u32[]{:S(2)}, u32[]{:S(2)}) async-start(bf16[128,2,2,256]{3,2,1,0:T(2,128)(2,1)} %pad_maximum_fusion.1), calls=%async_computation.3 | async-start | bytes 524288 | tf_op jit(solution)/shard_map/all_to_all | solution.py:140
  86.9 14.7 %all-to-all-done.3 = bf16[128,2,2,256]{3,2,1,0:T(2,128)(2,1)S(1)} async-done(((bf16[128,2,2,256]{3,2,1,0:T(2,128)(2,1)}), bf16[128,2,2,256]{3,2,1,0:T(2,128)(2,1)S(1)}, u32[]{:S(2)}, u32[]{:S(2)}) %all-to-all-start.3) | async-done | bytes 262176 | tf_op jit(solution)/shard_map/all_to_all | solution.py:140
  101.9 1.7 %fusion.5 = f32[2048,256]{1,0:T(8,128)S(1)} fusion(bf16[256,256]{1,0:T(8,128)(2,1)S(1)} %reshape.438, bf16[2,128,2176]{1,2,0:T(8,128)(2,1)} %copy-done.1, s32[128]{0:T(128)S(1)} %get-tuple-element.53), kind=kOutput, calls=%fused_computation.18 | convolution fusion | flops 151060480 | bytes 2753024 | tf_op jit(solution)/shard_map/dot_general | solution.py:160
  103.6 2.7 %fusion.1 = bf16[2048,256]{1,0:T(8,128)(2,1)} fusion(f32[2048,256]{1,0:T(8,128)S(1)} %fusion.5, bf16[256,256]{1,0:T(8,128)(2,1)S(1)} %reshape.439, bf16[2,128,2176]{1,2,0:T(8,128)(2,1)} %copy-done.1, s32[128]{0:T(128)S(1)} %get-tuple-element.52), kind=kOutput, calls=%fused_computation.4 | convolution fusion | flops 152109056 | bytes 3801600 | tf_op jit(solution)/shard_map/dot_general | solution.py:160
  106.3 34.9 %all_to_all.32 = bf16[64,32,256]{2,1,0:T(8,128)(2,1)S(1)} all-to-all(bf16[64,32,256]{2,1,0:T(8,128)(2,1)} %bitcast.106), channel_id=1, replica_groups=mesh['z'=8,'y'=8,'c'=2,'head'=4] {'z','y'}, dimensions={0} | all-to-all | bytes 2097152 | tf_op jit(solution)/shard_map/all_to_all | solution.py:168
  (64 shorter events, 6.2 us)
Async XLA Ops:
  0.6 20.6 %copy-start = (bf16[4096,128]{1,0:T(8,128)(2,1)S(1)}, bf16[4096,128]{1,0:T(8,128)(2,1)}, u32[]{:S(2)}) copy-start(bf16[4096,128]{1,0:T(8,128)(2,1)} %param.15) | copy-start | bytes 3145732
  3.0 9.5 %copy-start.4 = (s32[1,128]{1,0:T(1,128)S(1)}, s32[1,128]{1,0:T(1,128)}, u32[]{:S(2)}) copy-start(s32[1,128]{1,0:T(1,128)} %param.17) | copy-start | bytes 1540
  3.0 9.7 %copy-start.3 = (bf16[128,128]{1,0:T(8,128)(2,1)S(1)}, bf16[128,128]{1,0:T(8,128)(2,1)}, u32[]{:S(2)}) copy-start(bf16[128,128]{1,0:T(8,128)(2,1)} %param.16) | copy-start | bytes 98308
  3.0 18.3 %all-to-all-start = ((bf16[4,128,1024]{1,2,0:T(8,128)(2,1)}), bf16[4,128,1024]{1,2,0:T(8,128)(2,1)S(1)}, u32[]{:S(2)}, u32[]{:S(2)}) async-start(bf16[4,128,1024]{1,2,0:T(8,128)(2,1)} %broadcast_in_dim.34), calls=%async_computation | async-start | bytes 2097152 | tf_op jit(solution)/shard_map/all_to_all | solution.py:34
  12.6 9.1 %copy-start.2 = (bf16[4096,128]{1,0:T(8,128)(2,1)S(1)}, bf16[4096,128]{1,0:T(8,128)(2,1)}, u32[]{:S(2)}) copy-start(bf16[4096,128]{1,0:T(8,128)(2,1)} %param.14) | copy-start | bytes 3145732
  23.4 32.2 %all-to-all-start.2 = ((bf16[128,2,512]{2,1,0:T(2,128)(2,1)}), bf16[128,2,512]{2,1,0:T(2,128)(2,1)S(1)}, u32[]{:S(2)}, u32[]{:S(2)}) async-start(bf16[128,2,512]{2,1,0:T(2,128)(2,1)} %all_to_all.22), calls=%async_computation.2 | async-start | bytes 524288 | tf_op jit(solution)/shard_map/all_to_all | solution.py:73
  55.6 22.5 %all-to-all-start.1 = ((bf16[2,128,2176]{1,2,0:T(8,128)(2,1)}), bf16[2,128,2176]{1,2,0:T(8,128)(2,1)S(1)}, u32[]{:S(2)}, u32[]{:S(2)}) async-start(bf16[2,128,2176]{1,2,0:T(8,128)(2,1)} %pad_maximum_fusion), calls=%async_computation.1 | async-start | bytes 2228224 | tf_op jit(solution)/shard_map/all_to_all | solution.py:150
  59.9 8.6 %collective-permute-start = (bf16[64,256]{1,0:T(8,128)(2,1)S(1)}, bf16[64,256]{1,0:T(8,128)(2,1)S(1)}, u32[]{:S(2)}, u32[]{:S(2)}) collective-permute-start(bf16[64,256]{1,0:T(8,128)(2,1)S(1)} %slice.164), channel_id=1, source_target_pairs={{0,4},{4,8},{8,12},{12,16},{16,20},{20,24},{24,28},{28,32},{32,36}... | collective-permute-start | bytes 98312 | tf_op jit(solution)/shard_map/ppermute | solution.py:21
  70.2 4.4 %collective-permute-start.1 = (f32[64,256]{0,1:T(8,128)S(1)}, f32[64,256]{0,1:T(8,128)S(1)}, u32[]{:S(2)}, u32[]{:S(2)}) collective-permute-start(f32[64,256]{0,1:T(8,128)S(1)} %get-tuple-element.57), channel_id=1, source_target_pairs={{0,508},{4,0},{8,4},{12,8},{16,12},{20,16},{24,20},{28,24},{32,28}... | collective-permute-start | bytes 196616 | tf_op jit(solution)/shard_map/ppermute | solution.py:21
  78.1 23.8 %copy-start.1 = (bf16[2,128,2176]{1,2,0:T(8,128)(2,1)}, bf16[2,128,2176]{1,2,0:T(8,128)(2,1)S(1)}, u32[]{:S(2)}) copy-start(bf16[2,128,2176]{1,2,0:T(8,128)(2,1)S(1)} %all-to-all-done.1) | copy-start | bytes 3342340
  78.1 23.4 %all-to-all-start.3 = ((bf16[128,2,2,256]{3,2,1,0:T(2,128)(2,1)}), bf16[128,2,2,256]{3,2,1,0:T(2,128)(2,1)S(1)}, u32[]{:S(2)}, u32[]{:S(2)}) async-start(bf16[128,2,2,256]{3,2,1,0:T(2,128)(2,1)} %pad_maximum_fusion.1), calls=%async_computation.3 | async-start | bytes 524288 | tf_op jit(solution)/shard_map/all_to_all | solution.py:140

commit v7 on v6

--- a/solution.py
+++ b/solution.py
@@ -133,10 +133,10 @@
     nz, ny, nc = (lax.axis_size(a) for a in SEQ)
     my_core = lax.axis_index("c")
     by_peer = return_rows.reshape(peer_count, capacity, 2 * head_width)
-    peer_core = jnp.arange(peer_count) % nc
-    peer_chip = jnp.arange(peer_count) - peer_core
-    shifted_peers = [peer_chip + (peer_core + j) % nc for j in range(nc)]
-    to_chip = jnp.stack([by_peer[p] for p in shifted_peers], axis=1)
+    by_chip = by_peer.reshape(peer_count // nc, nc, capacity, 2 * head_width)
+    to_chip = jnp.stack([jnp.roll(by_chip, -j, axis=1) for j in range(nc)], axis=2).reshape(
+        peer_count, nc, capacity, 2 * head_width
+    )
     back_rows = lax.all_to_all(to_chip, SEQ, split_axis=0, concat_axis=0, tiled=True)
     rows = feat_count // (nz * ny * nc)
     blocks = whole.reshape(tok_count, nz, ny, nc, rows).transpose(3, 0, 1, 2, 4)

time: 144 us -> 143 us (level)
  local copies, waits for them, and re-layouts: 6.17 us -> 4.58 us
    gather x2 -> x0, local copies, waits for them, and re-layouts: 1.74 us -> none  [per_device(): to_chip = jnp.stack([by_peer[p] for p in shifted_peers], axis=1)]
  transfers between devices with their start and end apart: 6 -> 6, of which waited for: 5 -> 5; matrix products, arithmetic and copies ran while one was open for 7% -> 6% of each run, Pallas kernels for 0% -> 0%
where the time goes in v7:
time: 143 us; the launch traced here: 141 us
  starting transfers between devices  43.5 us (30%)
  waiting for transfers between devices  43 us (30%)
  blocking collectives  34.9 us (24%)
  matrix products  7.52 us (5%)
  other arithmetic  5.98 us (4%)
  local copies, waits for them, and re-layouts  4.58 us (3%)
    all_to_all x1, blocking collectives, per_device(): lax.all_to_all(grads.astype(jnp.bfloat16), ('z', 'y'), 0, 0, tiled=True)  34.9 us
    all_to_all x1, starting transfers between devices, per_device(): lax.all_to_all(send_rows, SEQ, split_axis=0, concat_axis=0, tiled=True)  17.5 us
    all_to_all x1, waiting for transfers between devices, per_device(): lax.all_to_all(to_chip, SEQ, split_axis=0, concat_axis=0, tiled=True)  14.7 us
    all_to_all x1, waiting for transfers between devices, per_device(): lax.all_to_all(send_rows, SEQ, split_axis=0, concat_axis=0, tiled=True)  13.5 us
    all_to_all x1, starting transfers between devices, per_device(): gathered = lax.all_to_all(spread, 'head', 0, 0, tiled=True)  9.44 us
    all_to_all x1, starting transfers between devices, per_device(): lax.all_to_all(to_chip, SEQ, split_axis=0, concat_axis=0, tiled=True)  8.7 us
    ppermute x2, waiting for transfers between devices, shifted(): return lax.ppermute(value, axis, pairs)  8.5 us
    all_to_all x1, waiting for transfers between devices, per_device(): gathered = lax.all_to_all(spread, 'head', 0, 0, tiled=True)  6.36 us
  transfers between devices with their start and end apart: 6, of which 5 were waited for; matrix products, arithmetic and copies ran while one was open for 6% of the time, Pallas kernels for 0%

profile of v7, /device:TPU:6, one launch (start us, length us, event | category | flops | bytes accessed | tf_op | source)
XLA Modules:
  0.0 140.6 jit_solution(15317553930438270197)
XLA Ops:
  0.6 1.2 copy.22
  1.9 1.1 broadcast_in_dim.34
  3.0 9.4 %all-to-all-start = ((bf16[4,128,1024]{1,2,0:T(8,128)(2,1)}), bf16[4,128,1024]{1,2,0:T(8,128)(2,1)S(1)}, u32[]{:S(2)}, u32[]{:S(2)}) async-start(bf16[4,128,1024]{1,2,0:T(8,128)(2,1)} %broadcast_in_dim.34), calls=%async_computation | async-start | bytes 2097152 | tf_op jit(solution)/shard_map/all_to_all | solution.py:34
  12.8 0.7 compare_reduce_fusion
  13.6 0.7 broadcast_select_fusion.3
  14.2 0.7 broadcast_select_fusion.2
  14.9 6.4 %all-to-all-done = bf16[4,128,1024]{1,2,0:T(8,128)(2,1)S(1)} async-done(((bf16[4,128,1024]{1,2,0:T(8,128)(2,1)}), bf16[4,128,1024]{1,2,0:T(8,128)(2,1)S(1)}, u32[]{:S(2)}, u32[]{:S(2)}) %all-to-all-start) | async-done | bytes 1048608 | tf_op jit(solution)/shard_map/all_to_all | solution.py:34
  21.3 0.5 convolution_convert_fusion.5
  22.6 0.8 all_to_all.22
  23.4 17.5 %all-to-all-start.2 = ((bf16[128,2,512]{2,1,0:T(2,128)(2,1)}), bf16[128,2,512]{2,1,0:T(2,128)(2,1)S(1)}, u32[]{:S(2)}, u32[]{:S(2)}) async-start(bf16[128,2,512]{2,1,0:T(2,128)(2,1)} %all_to_all.22), calls=%async_computation.2 | async-start | bytes 524288 | tf_op jit(solution)/shard_map/all_to_all | solution.py:73
  41.1 1.1 pad_maximum_fusion
  42.1 13.5 %all-to-all-done.2 = bf16[128,2,512]{2,1,0:T(2,128)(2,1)S(1)} async-done(((bf16[128,2,512]{2,1,0:T(2,128)(2,1)}), bf16[128,2,512]{2,1,0:T(2,128)(2,1)S(1)}, u32[]{:S(2)}, u32[]{:S(2)}) %all-to-all-start.2) | async-done | bytes 262176 | tf_op jit(solution)/shard_map/all_to_all | solution.py:73
  55.6 3.6 %all-to-all-start.1 = ((bf16[2,128,2176]{1,2,0:T(8,128)(2,1)}), bf16[2,128,2176]{1,2,0:T(8,128)(2,1)S(1)}, u32[]{:S(2)}, u32[]{:S(2)}) async-start(bf16[2,128,2176]{1,2,0:T(8,128)(2,1)} %pad_maximum_fusion), calls=%async_computation.1 | async-start | bytes 2228224 | tf_op jit(solution)/shard_map/all_to_all | solution.py:150
  59.9 2.4 %collective-permute-start = (bf16[64,256]{1,0:T(8,128)(2,1)S(1)}, bf16[64,256]{1,0:T(8,128)(2,1)S(1)}, u32[]{:S(2)}, u32[]{:S(2)}) collective-permute-start(bf16[64,256]{1,0:T(8,128)(2,1)S(1)} %slice.170), channel_id=1, source_target_pairs={{0,4},{4,8},{8,12},{12,16},{16,20},{20,24},{24,28},{28,32},{32,36}... | collective-permute-start | bytes 98312 | tf_op jit(solution)/shard_map/ppermute | solution.py:21
  62.3 6.1 %collective-permute-done = bf16[64,256]{1,0:T(8,128)(2,1)S(1)} collective-permute-done((bf16[64,256]{1,0:T(8,128)(2,1)S(1)}, bf16[64,256]{1,0:T(8,128)(2,1)S(1)}, u32[]{:S(2)}, u32[]{:S(2)}) %collective-permute-start) | collective-permute-done | bytes 32800 | tf_op jit(solution)/shard_map/ppermute | solution.py:21
  70.2 1.9 %collective-permute-start.1 = (f32[64,256]{0,1:T(8,128)S(1)}, f32[64,256]{0,1:T(8,128)S(1)}, u32[]{:S(2)}, u32[]{:S(2)}) collective-permute-start(f32[64,256]{0,1:T(8,128)S(1)} %get-tuple-element.57), channel_id=1, source_target_pairs={{0,508},{4,0},{8,4},{12,8},{16,12},{20,16},{24,20},{28,24},{32,28}... | collective-permute-start | bytes 196616 | tf_op jit(solution)/shard_map/ppermute | solution.py:21
  72.2 2.4 %collective-permute-done.1 = f32[64,256]{0,1:T(8,128)S(1)} collective-permute-done((f32[64,256]{0,1:T(8,128)S(1)}, f32[64,256]{0,1:T(8,128)S(1)}, u32[]{:S(2)}, u32[]{:S(2)}) %collective-permute-start.1) | collective-permute-done | bytes 65568 | tf_op jit(solution)/shard_map/ppermute | solution.py:21
  75.7 1.0 pad_maximum_fusion.1
  76.7 8.7 %all-to-all-start.3 = ((bf16[128,2,2,256]{3,2,1,0:T(2,128)(2,1)}), bf16[128,2,2,256]{3,2,1,0:T(2,128)(2,1)S(1)}, u32[]{:S(2)}, u32[]{:S(2)}) async-start(bf16[128,2,2,256]{3,2,1,0:T(2,128)(2,1)} %pad_maximum_fusion.1), calls=%async_computation.3 | async-start | bytes 524288 | tf_op jit(solution)/shard_map/all_to_all | solution.py:140
  85.5 14.7 %all-to-all-done.3 = bf16[128,2,2,256]{3,2,1,0:T(2,128)(2,1)S(1)} async-done(((bf16[128,2,2,256]{3,2,1,0:T(2,128)(2,1)}), bf16[128,2,2,256]{3,2,1,0:T(2,128)(2,1)S(1)}, u32[]{:S(2)}, u32[]{:S(2)}) %all-to-all-start.3) | async-done | bytes 262176 | tf_op jit(solution)/shard_map/all_to_all | solution.py:140
  100.5 1.7 %fusion.5 = f32[2048,256]{1,0:T(8,128)S(1)} fusion(bf16[256,256]{1,0:T(8,128)(2,1)S(1)} %reshape.316, bf16[2,128,2176]{1,2,0:T(8,128)(2,1)} %copy-done.1, s32[128]{0:T(128)S(1)} %get-tuple-element.53), kind=kOutput, calls=%fused_computation.16 | convolution fusion | flops 151060480 | bytes 2753024 | tf_op jit(solution)/shard_map/dot_general | solution.py:160
  102.2 2.7 %fusion.1 = bf16[2048,256]{1,0:T(8,128)(2,1)} fusion(f32[2048,256]{1,0:T(8,128)S(1)} %fusion.5, bf16[256,256]{1,0:T(8,128)(2,1)S(1)} %reshape.317, bf16[2,128,2176]{1,2,0:T(8,128)(2,1)} %copy-done.1, s32[128]{0:T(128)S(1)} %get-tuple-element.52), kind=kOutput, calls=%fused_computation.2 | convolution fusion | flops 152109056 | bytes 3801600 | tf_op jit(solution)/shard_map/dot_general | solution.py:160
  104.9 34.9 %all_to_all.32 = bf16[64,32,256]{2,1,0:T(8,128)(2,1)S(1)} all-to-all(bf16[64,32,256]{2,1,0:T(8,128)(2,1)} %bitcast.102), channel_id=1, replica_groups=mesh['z'=8,'y'=8,'c'=2,'head'=4] {'z','y'}, dimensions={0} | all-to-all | bytes 2097152 | tf_op jit(solution)/shard_map/all_to_all | solution.py:168
  140.0 0.6 fusion.75
  (62 shorter events, 5.4 us)
Async XLA Ops:
  0.6 20.6 %copy-start = (bf16[4096,128]{1,0:T(8,128)(2,1)S(1)}, bf16[4096,128]{1,0:T(8,128)(2,1)}, u32[]{:S(2)}) copy-start(bf16[4096,128]{1,0:T(8,128)(2,1)} %param.15) | copy-start | bytes 3145732
  3.0 9.4 %copy-start.4 = (s32[1,128]{1,0:T(1,128)S(1)}, s32[1,128]{1,0:T(1,128)}, u32[]{:S(2)}) copy-start(s32[1,128]{1,0:T(1,128)} %param.17) | copy-start | bytes 1540
  3.0 9.7 %copy-start.3 = (bf16[128,128]{1,0:T(8,128)(2,1)S(1)}, bf16[128,128]{1,0:T(8,128)(2,1)}, u32[]{:S(2)}) copy-start(bf16[128,128]{1,0:T(8,128)(2,1)} %param.16) | copy-start | bytes 98308
  3.0 18.3 %all-to-all-start = ((bf16[4,128,1024]{1,2,0:T(8,128)(2,1)}), bf16[4,128,1024]{1,2,0:T(8,128)(2,1)S(1)}, u32[]{:S(2)}, u32[]{:S(2)}) async-start(bf16[4,128,1024]{1,2,0:T(8,128)(2,1)} %broadcast_in_dim.34), calls=%async_computation | async-start | bytes 2097152 | tf_op jit(solution)/shard_map/all_to_all | solution.py:34
  12.6 9.1 %copy-start.2 = (bf16[4096,128]{1,0:T(8,128)(2,1)S(1)}, bf16[4096,128]{1,0:T(8,128)(2,1)}, u32[]{:S(2)}) copy-start(bf16[4096,128]{1,0:T(8,128)(2,1)} %param.14) | copy-start | bytes 3145732
  23.4 32.2 %all-to-all-start.2 = ((bf16[128,2,512]{2,1,0:T(2,128)(2,1)}), bf16[128,2,512]{2,1,0:T(2,128)(2,1)S(1)}, u32[]{:S(2)}, u32[]{:S(2)}) async-start(bf16[128,2,512]{2,1,0:T(2,128)(2,1)} %all_to_all.22), calls=%async_computation.2 | async-start | bytes 524288 | tf_op jit(solution)/shard_map/all_to_all | solution.py:73
  55.6 21.1 %all-to-all-start.1 = ((bf16[2,128,2176]{1,2,0:T(8,128)(2,1)}), bf16[2,128,2176]{1,2,0:T(8,128)(2,1)S(1)}, u32[]{:S(2)}, u32[]{:S(2)}) async-start(bf16[2,128,2176]{1,2,0:T(8,128)(2,1)} %pad_maximum_fusion), calls=%async_computation.1 | async-start | bytes 2228224 | tf_op jit(solution)/shard_map/all_to_all | solution.py:150
  59.9 8.6 %collective-permute-start = (bf16[64,256]{1,0:T(8,128)(2,1)S(1)}, bf16[64,256]{1,0:T(8,128)(2,1)S(1)}, u32[]{:S(2)}, u32[]{:S(2)}) collective-permute-start(bf16[64,256]{1,0:T(8,128)(2,1)S(1)} %slice.170), channel_id=1, source_target_pairs={{0,4},{4,8},{8,12},{12,16},{16,20},{20,24},{24,28},{28,32},{32,36}... | collective-permute-start | bytes 98312 | tf_op jit(solution)/shard_map/ppermute | solution.py:21
  70.2 4.4 %collective-permute-start.1 = (f32[64,256]{0,1:T(8,128)S(1)}, f32[64,256]{0,1:T(8,128)S(1)}, u32[]{:S(2)}, u32[]{:S(2)}) collective-permute-start(f32[64,256]{0,1:T(8,128)S(1)} %get-tuple-element.57), channel_id=1, source_target_pairs={{0,508},{4,0},{8,4},{12,8},{16,12},{20,16},{24,20},{28,24},{32,28}... | collective-permute-start | bytes 196616 | tf_op jit(solution)/shard_map/ppermute | solution.py:21
  76.7 23.8 %copy-start.1 = (bf16[2,128,2176]{1,2,0:T(8,128)(2,1)}, bf16[2,128,2176]{1,2,0:T(8,128)(2,1)S(1)}, u32[]{:S(2)}) copy-start(bf16[2,128,2176]{1,2,0:T(8,128)(2,1)S(1)} %all-to-all-done.1) | copy-start | bytes 3342340
  76.7 23.4 %all-to-all-start.3 = ((bf16[128,2,2,256]{3,2,1,0:T(2,128)(2,1)}), bf16[128,2,2,256]{3,2,1,0:T(2,128)(2,1)S(1)}, u32[]{:S(2)}, u32[]{:S(2)}) async-start(bf16[128,2,2,256]{3,2,1,0:T(2,128)(2,1)} %pad_maximum_fusion.1), calls=%async_computation.3 | async-start | bytes 524288 | tf_op jit(solution)/shard_map/all_to_all | solution.py:140

commit v8 on v7

--- a/solution.py
+++ b/solution.py
@@ -54,29 +54,51 @@
     buffer_index = target * capacity + jnp.sum(before * one_hot.astype(jnp.float32), axis=1).astype(
         jnp.int32
     )
-    slot_block = jnp.zeros((tok_count, head_width), jnp.bfloat16).at[:, 0].set(
-        local_slot.astype(jnp.bfloat16)
-    )
-    payload = jnp.concatenate([query, values, head_grad, slot_block], axis=1)
+    is_tail = local_slot >= tail_start
+    tail_hot = one_hot * is_tail[:, None].astype(jnp.bfloat16)
+    before_tail = jnp.dot(earlier_rows, tail_hot, preferred_element_type=jnp.float32)
+    tail_rank = jnp.sum(before_tail * one_hot.astype(jnp.float32), axis=1).astype(jnp.int32)
+    lanes = 2 * capacity
+    main_slot = target * lanes + buffer_index % capacity
+    next_slot = ((target + 1) % peer_count) * lanes + capacity + tail_rank
+    window = GROUP + tok_count
+    main_index = jnp.zeros((tok_count, head_width), jnp.bfloat16).at[:, 0].set(
+        (local_slot + GROUP).astype(jnp.bfloat16)
+    )
+    next_index = jnp.zeros((tok_count, head_width), jnp.bfloat16).at[:, 0].set(
+        (local_slot - tail_start).astype(jnp.bfloat16)
+    )
+    rows_main = jnp.concatenate([query, values, head_grad, main_index], axis=1)
+    rows_next = jnp.concatenate([query, values, head_grad, next_index], axis=1)
     buffer_ids = jnp.arange(peer_count * capacity, dtype=jnp.int32)
+    send_ids = jnp.arange(peer_count * lanes, dtype=jnp.int32)
     to_buffer = (buffer_ids[:, None] == buffer_index[None, :]).astype(jnp.bfloat16)
-    send_rows = jnp.dot(to_buffer, payload, preferred_element_type=jnp.float32).astype(jnp.bfloat16)
-    empty = (buffer_ids[:, None] * 0 + jnp.arange(head_width)[None, :]) == 0
-    used = jnp.sum(to_buffer.astype(jnp.float32), axis=1) > 0
+    to_main = (send_ids[:, None] == main_slot[None, :]).astype(jnp.bfloat16)
+    to_next = ((send_ids[:, None] == next_slot[None, :]) & is_tail[None, :]).astype(jnp.bfloat16)
+    send_rows = (
+        jnp.dot(to_main, rows_main, preferred_element_type=jnp.float32)
+        + jnp.dot(to_next, rows_next, preferred_element_type=jnp.float32)
+    ).astype(jnp.bfloat16)
+    empty = (send_ids[:, None] * 0 + jnp.arange(head_width)[None, :]) == 0
+    used = jnp.sum(to_main.astype(jnp.float32) + to_next.astype(jnp.float32), axis=1) > 0
     send_rows = send_rows.at[:, 3 * head_width :].set(
         jnp.where(
             empty & ~used[:, None],
-            jnp.bfloat16(tok_count),
+            jnp.bfloat16(window),
             send_rows[:, 3 * head_width :],
         )
     )
     recv_rows = lax.all_to_all(send_rows, SEQ, split_axis=0, concat_axis=0, tiled=True)
-    recv_slots = recv_rows[:, 3 * head_width].astype(jnp.int32)
-    to_sorted = (row_ids[:, None] == recv_slots[None, :]).astype(jnp.bfloat16)
-    sorted_rows = jnp.dot(
-        to_sorted, recv_rows[:, : 3 * head_width], preferred_element_type=jnp.float32
+    recv_index = recv_rows[:, 3 * head_width].astype(jnp.int32)
+    window_ids = jnp.arange(window, dtype=jnp.int32)
+    to_window = (window_ids[:, None] == recv_index[None, :]).astype(jnp.bfloat16)
+    window_rows = jnp.dot(
+        to_window, recv_rows[:, : 3 * head_width], preferred_element_type=jnp.float32
     ).astype(jnp.bfloat16)
-    halo_rows = shifted(sorted_rows[tail_start:, : 2 * head_width], SEQ, 1)
+    halo_rows = window_rows[:GROUP, : 2 * head_width]
+    sorted_rows = window_rows[GROUP:]
+    recv_main = recv_index.reshape(peer_count, lanes)[:, :capacity].reshape(-1) - GROUP
+    to_sorted = (row_ids[:, None] == recv_main[None, :]).astype(jnp.bfloat16)
     sorted_query = sorted_rows[:, :head_width]
     own_keys = unit_keys(sorted_query).reshape(group_count, GROUP, head_width)
     halo_keys = unit_keys(halo_rows[:, :head_width])

time: 143 us -> 143 us (level)
  waiting for transfers between devices: 43 us -> 41.3 us
    ppermute x2 -> x1, waiting for transfers between devices: 8.5 us -> 2.34 us  [shifted(): return lax.ppermute(value, axis, pairs)]
    all_to_all x1, waiting for transfers between devices: 13.5 us -> 18.2 us  [per_device(): lax.all_to_all(send_rows, SEQ, split_axis=0, concat_axis=0, tiled=True)]
    ppermute x2 -> x1, starting transfers between devices: 4.32 us -> 4.42 us  [shifted(): return lax.ppermute(value, axis, pairs)]
  transfers between devices with their start and end apart: 6 -> 5, of which waited for: 5 -> 4; matrix products, arithmetic and copies ran while one was open for 6% -> 6% of each run, Pallas kernels for 0% -> 0%
where the time goes in v8:
time: 143 us; the launch traced here: 141 us
  starting transfers between devices  44.1 us (31%)
  waiting for transfers between devices  41.3 us (29%)
  blocking collectives  34.9 us (24%)
  matrix products  8.16 us (6%)
  other arithmetic  6.18 us (4%)
  local copies, waits for them, and re-layouts  5.11 us (4%)
    all_to_all x1, blocking collectives, per_device(): lax.all_to_all(grads.astype(jnp.bfloat16), ('z', 'y'), 0, 0, tiled=True)  34.9 us
    all_to_all x1, waiting for transfers between devices, per_device(): lax.all_to_all(send_rows, SEQ, split_axis=0, concat_axis=0, tiled=True)  18.2 us
    all_to_all x1, starting transfers between devices, per_device(): lax.all_to_all(send_rows, SEQ, split_axis=0, concat_axis=0, tiled=True)  17.5 us
    all_to_all x1, waiting for transfers between devices, per_device(): lax.all_to_all(to_chip, SEQ, split_axis=0, concat_axis=0, tiled=True)  14.7 us
    all_to_all x1, starting transfers between devices, per_device(): gathered = lax.all_to_all(spread, 'head', 0, 0, tiled=True)  9.44 us
    all_to_all x1, starting transfers between devices, per_device(): lax.all_to_all(to_chip, SEQ, split_axis=0, concat_axis=0, tiled=True)  9.14 us
    all_to_all x1, waiting for transfers between devices, per_device(): gathered = lax.all_to_all(spread, 'head', 0, 0, tiled=True)  6.1 us
    ppermute x1, starting transfers between devices, shifted(): return lax.ppermute(value, axis, pairs)  4.42 us
  transfers between devices with their start and end apart: 5, of which 4 were waited for; matrix products, arithmetic and copies ran while one was open for 6% of the time, Pallas kernels for 0%

profile of v8, /device:TPU:6, one launch (start us, length us, event | category | flops | bytes accessed | tf_op | source)
XLA Modules:
  0.0 140.8 jit_solution(15737627798198232276)
XLA Ops:
  0.6 1.2 copy.26
  1.9 1.1 broadcast_in_dim.32
  3.0 9.4 %all-to-all-start = ((bf16[4,128,1024]{1,2,0:T(8,128)(2,1)}), bf16[4,128,1024]{1,2,0:T(8,128)(2,1)S(1)}, u32[]{:S(2)}, u32[]{:S(2)}) async-start(bf16[4,128,1024]{1,2,0:T(8,128)(2,1)} %broadcast_in_dim.32), calls=%async_computation | async-start | bytes 2097152 | tf_op jit(solution)/shard_map/all_to_all | solution.py:34
  12.4 0.6 compare_reduce_fusion
  13.8 0.7 broadcast_select_fusion.4
  14.5 0.7 broadcast_select_fusion.2
  15.2 6.1 %all-to-all-done = bf16[4,128,1024]{1,2,0:T(8,128)(2,1)S(1)} async-done(((bf16[4,128,1024]{1,2,0:T(8,128)(2,1)}), bf16[4,128,1024]{1,2,0:T(8,128)(2,1)S(1)}, u32[]{:S(2)}, u32[]{:S(2)}) %all-to-all-start) | async-done | bytes 1048608 | tf_op jit(solution)/shard_map/all_to_all | solution.py:34
  21.3 0.5 convolution_convert_fusion.4
  21.8 0.5 convolution_convert_fusion.5
  23.1 0.9 all_to_all.22
  24.1 17.5 %all-to-all-start.2 = ((bf16[128,4,512]{2,1,0:T(4,128)(2,1)}), bf16[128,4,512]{2,1,0:T(4,128)(2,1)S(1)}, u32[]{:S(2)}, u32[]{:S(2)}) async-start(bf16[128,4,512]{2,1,0:T(4,128)(2,1)} %all_to_all.22), calls=%async_computation.2 | async-start | bytes 1048576 | tf_op jit(solution)/shard_map/all_to_all | solution.py:91
  41.7 1.1 pad_maximum_fusion
  42.7 18.2 %all-to-all-done.2 = bf16[128,4,512]{2,1,0:T(4,128)(2,1)S(1)} async-done(((bf16[128,4,512]{2,1,0:T(4,128)(2,1)}), bf16[128,4,512]{2,1,0:T(4,128)(2,1)S(1)}, u32[]{:S(2)}, u32[]{:S(2)}) %all-to-all-start.2) | async-done | bytes 524320 | tf_op jit(solution)/shard_map/all_to_all | solution.py:91
  61.0 3.6 %all-to-all-start.1 = ((bf16[2,128,2176]{1,2,0:T(8,128)(2,1)}), bf16[2,128,2176]{1,2,0:T(8,128)(2,1)S(1)}, u32[]{:S(2)}, u32[]{:S(2)}) async-start(bf16[2,128,2176]{1,2,0:T(8,128)(2,1)} %pad_maximum_fusion), calls=%async_computation.1 | async-start | bytes 2228224 | tf_op jit(solution)/shard_map/all_to_all | solution.py:172
  66.1 0.4 fusion.62
  67.4 4.4 %collective-permute-start = (f32[64,256]{0,1:T(8,128)S(1)}, f32[64,256]{0,1:T(8,128)S(1)}, u32[]{:S(2)}, u32[]{:S(2)}) collective-permute-start(f32[64,256]{0,1:T(8,128)S(1)} %get-tuple-element.73), channel_id=1, source_target_pairs={{0,508},{4,0},{8,4},{12,8},{16,12},{20,16},{24,20},{28,24},{32,28}... | collective-permute-start | bytes 196616 | tf_op jit(solution)/shard_map/ppermute | solution.py:21
  72.0 2.3 %collective-permute-done = f32[64,256]{0,1:T(8,128)S(1)} collective-permute-done((f32[64,256]{0,1:T(8,128)S(1)}, f32[64,256]{0,1:T(8,128)S(1)}, u32[]{:S(2)}, u32[]{:S(2)}) %collective-permute-start) | collective-permute-done | bytes 65568 | tf_op jit(solution)/shard_map/ppermute | solution.py:21
  75.4 1.0 pad_maximum_fusion.1
  76.5 9.1 %all-to-all-start.3 = ((bf16[128,2,2,256]{3,2,1,0:T(2,128)(2,1)}), bf16[128,2,2,256]{3,2,1,0:T(2,128)(2,1)S(1)}, u32[]{:S(2)}, u32[]{:S(2)}) async-start(bf16[128,2,2,256]{3,2,1,0:T(2,128)(2,1)} %pad_maximum_fusion.1), calls=%async_computation.3 | async-start | bytes 524288 | tf_op jit(solution)/shard_map/all_to_all | solution.py:162
  85.7 14.7 %all-to-all-done.3 = bf16[128,2,2,256]{3,2,1,0:T(2,128)(2,1)S(1)} async-done(((bf16[128,2,2,256]{3,2,1,0:T(2,128)(2,1)}), bf16[128,2,2,256]{3,2,1,0:T(2,128)(2,1)S(1)}, u32[]{:S(2)}, u32[]{:S(2)}) %all-to-all-start.3) | async-done | bytes 262176 | tf_op jit(solution)/shard_map/all_to_all | solution.py:162
  100.7 1.7 %fusion.6 = f32[2048,256]{1,0:T(8,128)S(1)} fusion(bf16[256,256]{1,0:T(8,128)(2,1)S(1)} %reshape.395, bf16[2,128,2176]{1,2,0:T(8,128)(2,1)} %copy-done.1, s32[128]{0:T(128)S(1)} %get-tuple-element.69), kind=kOutput, calls=%fused_computation.18 | convolution fusion | flops 151060480 | bytes 2753024 | tf_op jit(solution)/shard_map/dot_general | solution.py:182
  102.4 2.7 %fusion.1 = bf16[2048,256]{1,0:T(8,128)(2,1)} fusion(f32[2048,256]{1,0:T(8,128)S(1)} %fusion.6, bf16[256,256]{1,0:T(8,128)(2,1)S(1)} %reshape.396, bf16[2,128,2176]{1,2,0:T(8,128)(2,1)} %copy-done.1, s32[128]{0:T(128)S(1)} %get-tuple-element.68), kind=kOutput, calls=%fused_computation.2 | convolution fusion | flops 152109056 | bytes 3801600 | tf_op jit(solution)/shard_map/dot_general | solution.py:182
  105.1 34.9 %all_to_all.32 = bf16[64,32,256]{2,1,0:T(8,128)(2,1)S(1)} all-to-all(bf16[64,32,256]{2,1,0:T(8,128)(2,1)} %bitcast.116), channel_id=1, replica_groups=mesh['z'=8,'y'=8,'c'=2,'head'=4] {'z','y'}, dimensions={0} | all-to-all | bytes 2097152 | tf_op jit(solution)/shard_map/all_to_all | solution.py:190
  140.2 0.6 fusion.99
  (64 shorter events, 5.7 us)
Async XLA Ops:
  0.6 20.6 %copy-start = (bf16[4096,128]{1,0:T(8,128)(2,1)S(1)}, bf16[4096,128]{1,0:T(8,128)(2,1)}, u32[]{:S(2)}) copy-start(bf16[4096,128]{1,0:T(8,128)(2,1)} %param.17) | copy-start | bytes 3145732
  3.0 10.1 %copy-start.4 = (s32[1,128]{1,0:T(1,128)S(1)}, s32[1,128]{1,0:T(1,128)}, u32[]{:S(2)}) copy-start(s32[1,128]{1,0:T(1,128)} %param.19) | copy-start | bytes 1540
  3.0 10.5 %copy-start.3 = (bf16[128,128]{1,0:T(8,128)(2,1)S(1)}, bf16[128,128]{1,0:T(8,128)(2,1)}, u32[]{:S(2)}) copy-start(bf16[128,128]{1,0:T(8,128)(2,1)} %param.18) | copy-start | bytes 98308
  3.0 18.3 %all-to-all-start = ((bf16[4,128,1024]{1,2,0:T(8,128)(2,1)}), bf16[4,128,1024]{1,2,0:T(8,128)(2,1)S(1)}, u32[]{:S(2)}, u32[]{:S(2)}) async-start(bf16[4,128,1024]{1,2,0:T(8,128)(2,1)} %broadcast_in_dim.32), calls=%async_computation | async-start | bytes 2097152 | tf_op jit(solution)/shard_map/all_to_all | solution.py:34
  13.5 8.3 %copy-start.2 = (bf16[4096,128]{1,0:T(8,128)(2,1)S(1)}, bf16[4096,128]{1,0:T(8,128)(2,1)}, u32[]{:S(2)}) copy-start(bf16[4096,128]{1,0:T(8,128)(2,1)} %param.16) | copy-start | bytes 3145732
  24.1 36.9 %all-to-all-start.2 = ((bf16[128,4,512]{2,1,0:T(4,128)(2,1)}), bf16[128,4,512]{2,1,0:T(4,128)(2,1)S(1)}, u32[]{:S(2)}, u32[]{:S(2)}) async-start(bf16[128,4,512]{2,1,0:T(4,128)(2,1)} %all_to_all.22), calls=%async_computation.2 | async-start | bytes 1048576 | tf_op jit(solution)/shard_map/all_to_all | solution.py:91
  61.0 15.5 %all-to-all-start.1 = ((bf16[2,128,2176]{1,2,0:T(8,128)(2,1)}), bf16[2,128,2176]{1,2,0:T(8,128)(2,1)S(1)}, u32[]{:S(2)}, u32[]{:S(2)}) async-start(bf16[2,128,2176]{1,2,0:T(8,128)(2,1)} %pad_maximum_fusion), calls=%async_computation.1 | async-start | bytes 2228224 | tf_op jit(solution)/shard_map/all_to_all | solution.py:172
  67.4 6.9 %collective-permute-start = (f32[64,256]{0,1:T(8,128)S(1)}, f32[64,256]{0,1:T(8,128)S(1)}, u32[]{:S(2)}, u32[]{:S(2)}) collective-permute-start(f32[64,256]{0,1:T(8,128)S(1)} %get-tuple-element.73), channel_id=1, source_target_pairs={{0,508},{4,0},{8,4},{12,8},{16,12},{20,16},{24,20},{28,24},{32,28}... | collective-permute-start | bytes 196616 | tf_op jit(solution)/shard_map/ppermute | solution.py:21
  76.5 24.2 %copy-start.1 = (bf16[2,128,2176]{1,2,0:T(8,128)(2,1)}, bf16[2,128,2176]{1,2,0:T(8,128)(2,1)S(1)}, u32[]{:S(2)}) copy-start(bf16[2,128,2176]{1,2,0:T(8,128)(2,1)S(1)} %all-to-all-done.1) | copy-start | bytes 3342340
  76.5 23.9 %all-to-all-start.3 = ((bf16[128,2,2,256]{3,2,1,0:T(2,128)(2,1)}), bf16[128,2,2,256]{3,2,1,0:T(2,128)(2,1)S(1)}, u32[]{:S(2)}, u32[]{:S(2)}) async-start(bf16[128,2,2,256]{3,2,1,0:T(2,128)(2,1)} %pad_maximum_fusion.1), calls=%async_computation.3 | async-start | bytes 524288 | tf_op jit(solution)/shard_map/all_to_all | solution.py:162

commit v9 on v7

--- a/solution.py
+++ b/solution.py
@@ -127,15 +127,17 @@
     sorted_grads = jnp.concatenate(
         [dshared_s.astype(jnp.bfloat16), dvalue_s.astype(jnp.bfloat16)], axis=1
     )
-    return_rows = lax.dot_general(
-        to_sorted, sorted_grads, (((0,), (0,)), ((), ())), preferred_element_type=jnp.float32
-    ).astype(jnp.bfloat16)
     nz, ny, nc = (lax.axis_size(a) for a in SEQ)
     my_core = lax.axis_index("c")
-    by_peer = return_rows.reshape(peer_count, capacity, 2 * head_width)
-    by_chip = by_peer.reshape(peer_count // nc, nc, capacity, 2 * head_width)
-    to_chip = jnp.stack([jnp.roll(by_chip, -j, axis=1) for j in range(nc)], axis=2).reshape(
-        peer_count, nc, capacity, 2 * head_width
+    slot_chip = recv_slots.reshape(peer_count // nc, nc, capacity)
+    fanned = jnp.stack([jnp.roll(slot_chip, -j, axis=1) for j in range(nc)], axis=2).reshape(-1)
+    to_fanned = (row_ids[:, None] == fanned[None, :]).astype(jnp.bfloat16)
+    to_chip = (
+        lax.dot_general(
+            to_fanned, sorted_grads, (((0,), (0,)), ((), ())), preferred_element_type=jnp.float32
+        )
+        .astype(jnp.bfloat16)
+        .reshape(peer_count, nc, capacity, 2 * head_width)
     )
     back_rows = lax.all_to_all(to_chip, SEQ, split_axis=0, concat_axis=0, tiled=True)
     rows = feat_count // (nz * ny * nc)
@@ -148,21 +150,23 @@
         [shares, jnp.broadcast_to(index_block[None], (nc, tok_count, head_width))], axis=2
     )
     chip_shares = lax.all_to_all(outgoing_shares, "c", 0, 0, tiled=True)
-    grads = jnp.zeros((ny * nz * rows, 2 * head_width), jnp.float32)
+    source_grads = []
     for source in range(nc):
         offset = (source - my_core) % nc
         rows_in = jnp.take(back_rows, offset, axis=1).reshape(peer_count * capacity, 2 * head_width)
         source_index = chip_shares[source, :, ny * nz * rows].astype(jnp.int32)
         source_buffer = (buffer_ids[:, None] == source_index[None, :]).astype(jnp.bfloat16)
-        source_grads = lax.dot_general(
-            source_buffer, rows_in, (((0,), (0,)), ((), ())), preferred_element_type=jnp.float32
-        ).astype(jnp.bfloat16)
-        grads = grads + lax.dot_general(
-            chip_shares[source, :, : ny * nz * rows],
-            source_grads,
-            (((0,), (0,)), ((), ())),
-            preferred_element_type=jnp.float32,
+        source_grads.append(
+            lax.dot_general(
+                source_buffer, rows_in, (((0,), (0,)), ((), ())), preferred_element_type=jnp.float32
+            ).astype(jnp.bfloat16)
         )
+    grads = lax.dot_general(
+        chip_shares[:, :, : ny * nz * rows].reshape(nc * tok_count, ny * nz * rows),
+        jnp.concatenate(source_grads, axis=0),
+        (((0,), (0,)), ((), ())),
+        preferred_element_type=jnp.float32,
+    )
     grads = grads.reshape(nz * ny, rows, 2 * head_width)
     grads = jnp.sum(
         lax.all_to_all(grads.astype(jnp.bfloat16), ("z", "y"), 0, 0, tiled=True).astype(jnp.float32),

time: 143 us -> 138 us (0.965)
  local copies, waits for them, and re-layouts: 4.58 us -> 8.73 us
  matrix products: 7.52 us -> 4.05 us
  waiting for transfers between devices: 43 us -> 39.6 us
    dot_general x3 -> x4, matrix products: 4.62 us -> 1.15 us  [the longest x1 0.44 us: per_device(): lax.dot_general(chip_shares[:, :, :ny * nz * rows].reshape(nc * tok_count...]
    all_to_all x1, waiting for transfers between devices: 14.7 us -> 11.8 us  [per_device(): lax.all_to_all(to_chip, SEQ, split_axis=0, concat_axis=0, tiled=True)]
    dot_general x0 -> x1, local copies, waits for them, and re-layouts: none -> 1.47 us  [per_device(): lax.dot_general(chip_shares[:, :, :ny * nz * rows].reshape(nc * tok_count...]
  transfers between devices with their start and end apart: 6 -> 6, of which waited for: 5 -> 5; matrix products, arithmetic and copies ran while one was open for 6% -> 8% of each run, Pallas kernels for 0% -> 0%
where the time goes in v9:
time: 138 us; the launch traced here: 136 us
  starting transfers between devices  43.5 us (32%)
  waiting for transfers between devices  39.6 us (29%)
  blocking collectives  34.1 us (25%)
  local copies, waits for them, and re-layouts  8.73 us (6%)
  other arithmetic  4.89 us (4%)
  matrix products  4.05 us (3%)
    all_to_all x1, blocking collectives, per_device(): lax.all_to_all(grads.astype(jnp.bfloat16), ('z', 'y'), 0, 0, tiled=True)  34.1 us
    all_to_all x1, starting transfers between devices, per_device(): lax.all_to_all(send_rows, SEQ, split_axis=0, concat_axis=0, tiled=True)  17.5 us
    all_to_all x1, waiting for transfers between devices, per_device(): lax.all_to_all(send_rows, SEQ, split_axis=0, concat_axis=0, tiled=True)  12.8 us
    all_to_all x1, waiting for transfers between devices, per_device(): lax.all_to_all(to_chip, SEQ, split_axis=0, concat_axis=0, tiled=True)  11.8 us
    all_to_all x1, starting transfers between devices, per_device(): gathered = lax.all_to_all(spread, 'head', 0, 0, tiled=True)  9.44 us
    all_to_all x1, starting transfers between devices, per_device(): lax.all_to_all(to_chip, SEQ, split_axis=0, concat_axis=0, tiled=True)  8.7 us
    ppermute x2, waiting for transfers between devices, shifted(): return lax.ppermute(value, axis, pairs)  8.01 us
    all_to_all x1, waiting for transfers between devices, per_device(): gathered = lax.all_to_all(spread, 'head', 0, 0, tiled=True)  7.02 us
  transfers between devices with their start and end apart: 6, of which 5 were waited for; matrix products, arithmetic and copies ran while one was open for 8% of the time, Pallas kernels for 0%

profile of v9, /device:TPU:6, one launch (start us, length us, event | category | flops | bytes accessed | tf_op | source)
XLA Modules:
  0.0 136.0 jit_solution(2462614351419412609)
XLA Ops:
  0.6 1.2 copy.44
  1.9 1.1 broadcast_in_dim.34
  3.0 9.4 %all-to-all-start = ((bf16[4,128,1024]{1,2,0:T(8,128)(2,1)}), bf16[4,128,1024]{1,2,0:T(8,128)(2,1)S(1)}, u32[]{:S(2)}, u32[]{:S(2)}) async-start(bf16[4,128,1024]{1,2,0:T(8,128)(2,1)} %broadcast_in_dim.34), calls=%async_computation | async-start | bytes 2097152 | tf_op jit(solution)/shard_map/all_to_all | solution.py:34
  12.8 0.7 compare_reduce_fusion
  13.6 0.7 broadcast_select_fusion.2
  14.2 7.0 %all-to-all-done = bf16[4,128,1024]{1,2,0:T(8,128)(2,1)S(1)} async-done(((bf16[4,128,1024]{1,2,0:T(8,128)(2,1)}), bf16[4,128,1024]{1,2,0:T(8,128)(2,1)S(1)}, u32[]{:S(2)}, u32[]{:S(2)}) %all-to-all-start) | async-done | bytes 1048608 | tf_op jit(solution)/shard_map/all_to_all | solution.py:34
  21.3 0.5 convolution_convert_fusion.6
  22.6 0.8 all_to_all.22
  23.4 17.5 %all-to-all-start.2 = ((bf16[128,2,512]{2,1,0:T(2,128)(2,1)}), bf16[128,2,512]{2,1,0:T(2,128)(2,1)S(1)}, u32[]{:S(2)}, u32[]{:S(2)}) async-start(bf16[128,2,512]{2,1,0:T(2,128)(2,1)} %all_to_all.22), calls=%async_computation.2 | async-start | bytes 524288 | tf_op jit(solution)/shard_map/all_to_all | solution.py:73
  40.9 0.7 broadcast_select_fusion.3
  41.7 1.1 pad_maximum_fusion
  42.8 12.8 %all-to-all-done.2 = bf16[128,2,512]{2,1,0:T(2,128)(2,1)S(1)} async-done(((bf16[128,2,512]{2,1,0:T(2,128)(2,1)}), bf16[128,2,512]{2,1,0:T(2,128)(2,1)S(1)}, u32[]{:S(2)}, u32[]{:S(2)}) %all-to-all-start.2) | async-done | bytes 262176 | tf_op jit(solution)/shard_map/all_to_all | solution.py:73
  55.6 3.6 %all-to-all-start.1 = ((bf16[2,128,2176]{1,2,0:T(8,128)(2,1)}), bf16[2,128,2176]{1,2,0:T(8,128)(2,1)S(1)}, u32[]{:S(2)}, u32[]{:S(2)}) async-start(bf16[2,128,2176]{1,2,0:T(8,128)(2,1)} %pad_maximum_fusion), calls=%async_computation.1 | async-start | bytes 2228224 | tf_op jit(solution)/shard_map/all_to_all | solution.py:152
  60.3 2.4 %collective-permute-start = (bf16[64,256]{1,0:T(8,128)(2,1)S(1)}, bf16[64,256]{1,0:T(8,128)(2,1)S(1)}, u32[]{:S(2)}, u32[]{:S(2)}) collective-permute-start(bf16[64,256]{1,0:T(8,128)(2,1)S(1)} %slice.168), channel_id=1, source_target_pairs={{0,4},{4,8},{8,12},{12,16},{16,20},{20,24},{24,28},{28,32},{32,36}... | collective-permute-start | bytes 98312 | tf_op jit(solution)/shard_map/ppermute | solution.py:21
  63.2 5.6 %collective-permute-done = bf16[64,256]{1,0:T(8,128)(2,1)S(1)} collective-permute-done((bf16[64,256]{1,0:T(8,128)(2,1)S(1)}, bf16[64,256]{1,0:T(8,128)(2,1)S(1)}, u32[]{:S(2)}, u32[]{:S(2)}) %collective-permute-start) | collective-permute-done | bytes 32800 | tf_op jit(solution)/shard_map/ppermute | solution.py:21
  70.5 1.9 %collective-permute-start.1 = (f32[64,256]{0,1:T(8,128)S(1)}, f32[64,256]{0,1:T(8,128)S(1)}, u32[]{:S(2)}, u32[]{:S(2)}) collective-permute-start(f32[64,256]{0,1:T(8,128)S(1)} %get-tuple-element.57), channel_id=1, source_target_pairs={{0,508},{4,0},{8,4},{12,8},{16,12},{20,16},{24,20},{28,24},{32,28}... | collective-permute-start | bytes 196616 | tf_op jit(solution)/shard_map/ppermute | solution.py:21
  72.6 2.4 %collective-permute-done.1 = f32[64,256]{0,1:T(8,128)S(1)} collective-permute-done((f32[64,256]{0,1:T(8,128)S(1)}, f32[64,256]{0,1:T(8,128)S(1)}, u32[]{:S(2)}, u32[]{:S(2)}) %collective-permute-start.1) | collective-permute-done | bytes 65568 | tf_op jit(solution)/shard_map/ppermute | solution.py:21
  75.6 0.8 reshape.335
  76.5 8.7 %all-to-all-start.3 = ((bf16[128,2,2,256]{3,2,1,0:T(2,128)(2,1)}), bf16[128,2,2,256]{3,2,1,0:T(2,128)(2,1)S(1)}, u32[]{:S(2)}, u32[]{:S(2)}) async-start(bf16[128,2,2,256]{3,2,1,0:T(2,128)(2,1)} %reshape.335), calls=%async_computation.3 | async-start | bytes 524288 | tf_op jit(solution)/shard_map/all_to_all | solution.py:142
  85.3 1.3 copy.46
  86.6 1.5 %copy.47 = bf16[2048,256]{1,0:T(8,128)(2,1)S(1)} copy(bf16[2048,256]{0,1:T(8,128)(2,1)} %bitcast.104) | data formatting | bytes 2097152 | tf_op jit(solution)/shard_map/dot_general | solution.py:164
  88.1 11.8 %all-to-all-done.3 = bf16[128,2,2,256]{3,2,1,0:T(2,128)(2,1)S(1)} async-done(((bf16[128,2,2,256]{3,2,1,0:T(2,128)(2,1)}), bf16[128,2,2,256]{3,2,1,0:T(2,128)(2,1)S(1)}, u32[]{:S(2)}, u32[]{:S(2)}) %all-to-all-start.3) | async-done | bytes 262176 | tf_op jit(solution)/shard_map/all_to_all | solution.py:142
  101.1 34.1 %all_to_all.32 = bf16[64,32,256]{2,1,0:T(8,128)(2,1)S(1)} all-to-all(bf16[64,32,256]{2,1,0:T(8,128)(2,1)S(1)} %convolution_convert_fusion), channel_id=1, replica_groups=mesh['z'=8,'y'=8,'c'=2,'head'=4] {'z','y'}, dimensions={0} | all-to-all | bytes 2097152 | tf_op jit(solution)/shard_map/all_to_all | solution.py:172
  135.4 0.6 fusion.74
  (67 shorter events, 6.8 us)
Async XLA Ops:
  0.6 20.6 %copy-start = (bf16[4096,128]{1,0:T(8,128)(2,1)S(1)}, bf16[4096,128]{1,0:T(8,128)(2,1)}, u32[]{:S(2)}) copy-start(bf16[4096,128]{1,0:T(8,128)(2,1)} %param.15) | copy-start | bytes 3145732
  3.0 9.4 %copy-start.3 = (s32[1,128]{1,0:T(1,128)S(1)}, s32[1,128]{1,0:T(1,128)}, u32[]{:S(2)}) copy-start(s32[1,128]{1,0:T(1,128)} %param.17) | copy-start | bytes 1540
  3.0 9.7 %copy-start.2 = (bf16[128,128]{1,0:T(8,128)(2,1)S(1)}, bf16[128,128]{1,0:T(8,128)(2,1)}, u32[]{:S(2)}) copy-start(bf16[128,128]{1,0:T(8,128)(2,1)} %param.16) | copy-start | bytes 98308
  3.0 18.3 %all-to-all-start = ((bf16[4,128,1024]{1,2,0:T(8,128)(2,1)}), bf16[4,128,1024]{1,2,0:T(8,128)(2,1)S(1)}, u32[]{:S(2)}, u32[]{:S(2)}) async-start(bf16[4,128,1024]{1,2,0:T(8,128)(2,1)} %broadcast_in_dim.34), calls=%async_computation | async-start | bytes 2097152 | tf_op jit(solution)/shard_map/all_to_all | solution.py:34
  12.6 9.1 %copy-start.1 = (bf16[4096,128]{1,0:T(8,128)(2,1)S(1)}, bf16[4096,128]{1,0:T(8,128)(2,1)}, u32[]{:S(2)}) copy-start(bf16[4096,128]{1,0:T(8,128)(2,1)} %param.14) | copy-start | bytes 3145732
  23.4 32.2 %all-to-all-start.2 = ((bf16[128,2,512]{2,1,0:T(2,128)(2,1)}), bf16[128,2,512]{2,1,0:T(2,128)(2,1)S(1)}, u32[]{:S(2)}, u32[]{:S(2)}) async-start(bf16[128,2,512]{2,1,0:T(2,128)(2,1)} %all_to_all.22), calls=%async_computation.2 | async-start | bytes 524288 | tf_op jit(solution)/shard_map/all_to_all | solution.py:73
  55.6 20.8 %all-to-all-start.1 = ((bf16[2,128,2176]{1,2,0:T(8,128)(2,1)}), bf16[2,128,2176]{1,2,0:T(8,128)(2,1)S(1)}, u32[]{:S(2)}, u32[]{:S(2)}) async-start(bf16[2,128,2176]{1,2,0:T(8,128)(2,1)} %pad_maximum_fusion), calls=%async_computation.1 | async-start | bytes 2228224 | tf_op jit(solution)/shard_map/all_to_all | solution.py:152
  60.3 8.6 %collective-permute-start = (bf16[64,256]{1,0:T(8,128)(2,1)S(1)}, bf16[64,256]{1,0:T(8,128)(2,1)S(1)}, u32[]{:S(2)}, u32[]{:S(2)}) collective-permute-start(bf16[64,256]{1,0:T(8,128)(2,1)S(1)} %slice.168), channel_id=1, source_target_pairs={{0,4},{4,8},{8,12},{12,16},{16,20},{20,24},{24,28},{28,32},{32,36}... | collective-permute-start | bytes 98312 | tf_op jit(solution)/shard_map/ppermute | solution.py:21
  70.5 4.4 %collective-permute-start.1 = (f32[64,256]{0,1:T(8,128)S(1)}, f32[64,256]{0,1:T(8,128)S(1)}, u32[]{:S(2)}, u32[]{:S(2)}) collective-permute-start(f32[64,256]{0,1:T(8,128)S(1)} %get-tuple-element.57), channel_id=1, source_target_pairs={{0,508},{4,0},{8,4},{12,8},{16,12},{20,16},{24,20},{28,24},{32,28}... | collective-permute-start | bytes 196616 | tf_op jit(solution)/shard_map/ppermute | solution.py:21
  76.5 23.4 %all-to-all-start.3 = ((bf16[128,2,2,256]{3,2,1,0:T(2,128)(2,1)}), bf16[128,2,2,256]{3,2,1,0:T(2,128)(2,1)S(1)}, u32[]{:S(2)}, u32[]{:S(2)}) async-start(bf16[128,2,2,256]{3,2,1,0:T(2,128)(2,1)} %reshape.335), calls=%async_computation.3 | async-start | bytes 524288 | tf_op jit(solution)/shard_map/all_to_all | solution.py:142

commit v10 on v9

--- a/solution.py
+++ b/solution.py
@@ -149,12 +149,14 @@
     outgoing_shares = jnp.concatenate(
         [shares, jnp.broadcast_to(index_block[None], (nc, tok_count, head_width))], axis=2
     )
-    chip_shares = lax.all_to_all(outgoing_shares, "c", 0, 0, tiled=True)
+    got_shares = []
     source_grads = []
-    for source in range(nc):
-        offset = (source - my_core) % nc
-        rows_in = jnp.take(back_rows, offset, axis=1).reshape(peer_count * capacity, 2 * head_width)
-        source_index = chip_shares[source, :, ny * nz * rows].astype(jnp.int32)
+    for j in range(nc):
+        mine = jnp.take(outgoing_shares, (my_core + j) % nc, axis=0)
+        got = mine if j == 0 else shifted(mine, "c", j)
+        got_shares.append(got[:, : ny * nz * rows])
+        rows_in = back_rows[:, (-j) % nc].reshape(peer_count * capacity, 2 * head_width)
+        source_index = got[:, ny * nz * rows].astype(jnp.int32)
         source_buffer = (buffer_ids[:, None] == source_index[None, :]).astype(jnp.bfloat16)
         source_grads.append(
             lax.dot_general(
@@ -162,7 +164,7 @@
             ).astype(jnp.bfloat16)
         )
     grads = lax.dot_general(
-        chip_shares[:, :, : ny * nz * rows].reshape(nc * tok_count, ny * nz * rows),
+        jnp.concatenate(got_shares, axis=0),
         jnp.concatenate(source_grads, axis=0),
         (((0,), (0,)), ((), ())),
         preferred_element_type=jnp.float32,

time: 138 us -> 135 us (0.978)
  starting transfers between devices: 43.5 us -> 41.5 us
    all_to_all x1 -> x0, starting transfers between devices: 3.59 us -> none  [per_device(): chip_shares = lax.all_to_all(outgoing_shares, 'c', 0, 0, tiled=True)]
    ppermute x2 -> x3, starting transfers between devices: 4.32 us -> 5.88 us  [shifted(): return lax.ppermute(value, axis, pairs)]
    dot_general x1 -> x0, local copies, waits for them, and re-layouts: 1.47 us -> none  [per_device(): lax.dot_general(chip_shares[:, :, :ny * nz * rows].reshape(nc * tok_count...]
    ppermute x2 -> x3, waiting for transfers between devices: 8.01 us -> 8.37 us  [shifted(): return lax.ppermute(value, axis, pairs)]
  transfers between devices with their start and end apart: 6 -> 6, of which waited for: 5 -> 5; matrix products, arithmetic and copies ran while one was open for 8% -> 7% of each run, Pallas kernels for 0% -> 0%
where the time goes in v10:
time: 135 us; the launch traced here: 133 us
  starting transfers between devices  41.5 us (31%)
  waiting for transfers between devices  40 us (30%)
  blocking collectives  34.1 us (25%)
  local copies, waits for them, and re-layouts  7.86 us (6%)
  other arithmetic  4.52 us (3%)
  matrix products  4.03 us (3%)
    all_to_all x1, blocking collectives, per_device(): lax.all_to_all(grads.astype(jnp.bfloat16), ('z', 'y'), 0, 0, tiled=True)  34.1 us
    all_to_all x1, starting transfers between devices, per_device(): lax.all_to_all(send_rows, SEQ, split_axis=0, concat_axis=0, tiled=True)  17.5 us
    all_to_all x1, waiting for transfers between devices, per_device(): lax.all_to_all(to_chip, SEQ, split_axis=0, concat_axis=0, tiled=True)  12.9 us
    all_to_all x1, waiting for transfers between devices, per_device(): lax.all_to_all(send_rows, SEQ, split_axis=0, concat_axis=0, tiled=True)  11.7 us
    all_to_all x1, starting transfers between devices, per_device(): gathered = lax.all_to_all(spread, 'head', 0, 0, tiled=True)  9.44 us
    all_to_all x1, starting transfers between devices, per_device(): lax.all_to_all(to_chip, SEQ, split_axis=0, concat_axis=0, tiled=True)  8.7 us
    ppermute x3, waiting for transfers between devices, shifted(): return lax.ppermute(value, axis, pairs)  8.37 us
    all_to_all x1, waiting for transfers between devices, per_device(): gathered = lax.all_to_all(spread, 'head', 0, 0, tiled=True)  7.04 us
  transfers between devices with their start and end apart: 6, of which 5 were waited for; matrix products, arithmetic and copies ran while one was open for 7% of the time, Pallas kernels for 0%

profile of v10, /device:TPU:6, one launch (start us, length us, event | category | flops | bytes accessed | tf_op | source)
XLA Modules:
  0.0 133.0 jit_solution(12022992524738438477)
XLA Ops:
  0.6 1.2 copy.36
  1.9 1.1 broadcast_in_dim.34
  3.0 9.4 %all-to-all-start = ((bf16[4,128,1024]{1,2,0:T(8,128)(2,1)}), bf16[4,128,1024]{1,2,0:T(8,128)(2,1)S(1)}, u32[]{:S(2)}, u32[]{:S(2)}) async-start(bf16[4,128,1024]{1,2,0:T(8,128)(2,1)} %broadcast_in_dim.34), calls=%async_computation | async-start | bytes 2097152 | tf_op jit(solution)/shard_map/all_to_all | solution.py:34
  12.8 0.7 compare_reduce_fusion
  13.6 0.7 broadcast_select_fusion
  14.2 7.0 %all-to-all-done = bf16[4,128,1024]{1,2,0:T(8,128)(2,1)S(1)} async-done(((bf16[4,128,1024]{1,2,0:T(8,128)(2,1)}), bf16[4,128,1024]{1,2,0:T(8,128)(2,1)S(1)}, u32[]{:S(2)}, u32[]{:S(2)}) %all-to-all-start) | async-done | bytes 1048608 | tf_op jit(solution)/shard_map/all_to_all | solution.py:34
  21.3 0.5 convolution_convert_fusion.6
  21.7 0.7 copy-done.1
  23.4 0.8 all_to_all.18
  24.2 17.5 %all-to-all-start.1 = ((bf16[128,2,512]{2,1,0:T(2,128)(2,1)}), bf16[128,2,512]{2,1,0:T(2,128)(2,1)S(1)}, u32[]{:S(2)}, u32[]{:S(2)}) async-start(bf16[128,2,512]{2,1,0:T(2,128)(2,1)} %all_to_all.18), calls=%async_computation.1 | async-start | bytes 524288 | tf_op jit(solution)/shard_map/all_to_all | solution.py:73
  41.6 0.7 broadcast_select_fusion.1
  42.7 1.9 %collective-permute-start = (bf16[128,2176]{0,1:T(8,128)(2,1)S(1)}, bf16[128,2176]{0,1:T(8,128)(2,1)}, u32[]{:S(2)}, u32[]{:S(2)}) collective-permute-start(bf16[128,2176]{0,1:T(8,128)(2,1)S(1)} %get-tuple-element.53), channel_id=1, source_target_pairs={{0,4},{4,0},{1,5},{5,1},{2,6},{6,2},{3,7},{7,3},{8,12},{12,8},{9,1... | collective-permute-start | bytes 1671176 | tf_op jit(solution)/shard_map/ppermute | solution.py:21
  44.7 11.7 %all-to-all-done.1 = bf16[128,2,512]{2,1,0:T(2,128)(2,1)S(1)} async-done(((bf16[128,2,512]{2,1,0:T(2,128)(2,1)}), bf16[128,2,512]{2,1,0:T(2,128)(2,1)S(1)}, u32[]{:S(2)}, u32[]{:S(2)}) %all-to-all-start.1) | async-done | bytes 262176 | tf_op jit(solution)/shard_map/all_to_all | solution.py:73
  57.4 2.0 %collective-permute-start.1 = (bf16[64,256]{1,0:T(8,128)(2,1)S(1)}, bf16[64,256]{1,0:T(8,128)(2,1)S(1)}, u32[]{:S(2)}, u32[]{:S(2)}) collective-permute-start(bf16[64,256]{1,0:T(8,128)(2,1)S(1)} %slice.179), channel_id=1, source_target_pairs={{0,4},{4,8},{8,12},{12,16},{16,20},{20,24},{24,28},{28,32},{32,36}... | collective-permute-start | bytes 98312 | tf_op jit(solution)/shard_map/ppermute | solution.py:21
  59.9 6.0 %collective-permute-done.1 = bf16[64,256]{1,0:T(8,128)(2,1)S(1)} collective-permute-done((bf16[64,256]{1,0:T(8,128)(2,1)S(1)}, bf16[64,256]{1,0:T(8,128)(2,1)S(1)}, u32[]{:S(2)}, u32[]{:S(2)}) %collective-permute-start.1) | collective-permute-done | bytes 32800 | tf_op jit(solution)/shard_map/ppermute | solution.py:21
  67.6 1.9 %collective-permute-start.2 = (f32[64,256]{0,1:T(8,128)S(1)}, f32[64,256]{0,1:T(8,128)S(1)}, u32[]{:S(2)}, u32[]{:S(2)}) collective-permute-start(f32[64,256]{0,1:T(8,128)S(1)} %get-tuple-element.57), channel_id=1, source_target_pairs={{0,508},{4,0},{8,4},{12,8},{16,12},{20,16},{24,20},{28,24},{32,28}... | collective-permute-start | bytes 196616 | tf_op jit(solution)/shard_map/ppermute | solution.py:21
  69.7 2.4 %collective-permute-done.2 = f32[64,256]{0,1:T(8,128)S(1)} collective-permute-done((f32[64,256]{0,1:T(8,128)S(1)}, f32[64,256]{0,1:T(8,128)S(1)}, u32[]{:S(2)}, u32[]{:S(2)}) %collective-permute-start.2) | collective-permute-done | bytes 65568 | tf_op jit(solution)/shard_map/ppermute | solution.py:21
  72.8 0.8 reshape.325
  73.6 8.7 %all-to-all-start.2 = ((bf16[128,2,2,256]{3,2,1,0:T(2,128)(2,1)}), bf16[128,2,2,256]{3,2,1,0:T(2,128)(2,1)S(1)}, u32[]{:S(2)}, u32[]{:S(2)}) async-start(bf16[128,2,2,256]{3,2,1,0:T(2,128)(2,1)} %reshape.325), calls=%async_computation.2 | async-start | bytes 524288 | tf_op jit(solution)/shard_map/all_to_all | solution.py:142
  82.3 1.1 slice.171
  83.4 0.7 fusion.62
  84.1 12.9 %all-to-all-done.2 = bf16[128,2,2,256]{3,2,1,0:T(2,128)(2,1)S(1)} async-done(((bf16[128,2,2,256]{3,2,1,0:T(2,128)(2,1)}), bf16[128,2,2,256]{3,2,1,0:T(2,128)(2,1)S(1)}, u32[]{:S(2)}, u32[]{:S(2)}) %all-to-all-start.2) | async-done | bytes 262176 | tf_op jit(solution)/shard_map/all_to_all | solution.py:142
  98.2 34.1 %all_to_all.27 = bf16[64,32,256]{2,1,0:T(8,128)(2,1)S(1)} all-to-all(bf16[64,32,256]{2,1,0:T(8,128)(2,1)S(1)} %bitcast.96), channel_id=1, replica_groups=mesh['z'=8,'y'=8,'c'=2,'head'=4] {'z','y'}, dimensions={0} | all-to-all | bytes 2097152 | tf_op jit(solution)/shard_map/all_to_all | solution.py:174
  132.4 0.6 fusion.83
  (67 shorter events, 6.9 us)
Async XLA Ops:
  0.6 20.6 %copy-start = (bf16[4096,128]{1,0:T(8,128)(2,1)S(1)}, bf16[4096,128]{1,0:T(8,128)(2,1)}, u32[]{:S(2)}) copy-start(bf16[4096,128]{1,0:T(8,128)(2,1)} %param.15) | copy-start | bytes 3145732
  3.0 9.4 %copy-start.3 = (s32[1,128]{1,0:T(1,128)S(1)}, s32[1,128]{1,0:T(1,128)}, u32[]{:S(2)}) copy-start(s32[1,128]{1,0:T(1,128)} %param.17) | copy-start | bytes 1540
  3.0 9.7 %copy-start.2 = (bf16[128,128]{1,0:T(8,128)(2,1)S(1)}, bf16[128,128]{1,0:T(8,128)(2,1)}, u32[]{:S(2)}) copy-start(bf16[128,128]{1,0:T(8,128)(2,1)} %param.16) | copy-start | bytes 98308
  3.0 18.3 %all-to-all-start = ((bf16[4,128,1024]{1,2,0:T(8,128)(2,1)}), bf16[4,128,1024]{1,2,0:T(8,128)(2,1)S(1)}, u32[]{:S(2)}, u32[]{:S(2)}) async-start(bf16[4,128,1024]{1,2,0:T(8,128)(2,1)} %broadcast_in_dim.34), calls=%async_computation | async-start | bytes 2097152 | tf_op jit(solution)/shard_map/all_to_all | solution.py:34
  21.3 1.2 copy-start.1
  24.2 32.2 %all-to-all-start.1 = ((bf16[128,2,512]{2,1,0:T(2,128)(2,1)}), bf16[128,2,512]{2,1,0:T(2,128)(2,1)S(1)}, u32[]{:S(2)}, u32[]{:S(2)}) async-start(bf16[128,2,512]{2,1,0:T(2,128)(2,1)} %all_to_all.18), calls=%async_computation.1 | async-start | bytes 524288 | tf_op jit(solution)/shard_map/all_to_all | solution.py:73
  42.7 39.6 %collective-permute-start = (bf16[128,2176]{0,1:T(8,128)(2,1)S(1)}, bf16[128,2176]{0,1:T(8,128)(2,1)}, u32[]{:S(2)}, u32[]{:S(2)}) collective-permute-start(bf16[128,2176]{0,1:T(8,128)(2,1)S(1)} %get-tuple-element.53), channel_id=1, source_target_pairs={{0,4},{4,0},{1,5},{5,1},{2,6},{6,2},{3,7},{7,3},{8,12},{12,8},{9,1... | collective-permute-start | bytes 1671176 | tf_op jit(solution)/shard_map/ppermute | solution.py:21
  57.4 8.6 %collective-permute-start.1 = (bf16[64,256]{1,0:T(8,128)(2,1)S(1)}, bf16[64,256]{1,0:T(8,128)(2,1)S(1)}, u32[]{:S(2)}, u32[]{:S(2)}) collective-permute-start(bf16[64,256]{1,0:T(8,128)(2,1)S(1)} %slice.179), channel_id=1, source_target_pairs={{0,4},{4,8},{8,12},{12,16},{16,20},{20,24},{24,28},{28,32},{32,36}... | collective-permute-start | bytes 98312 | tf_op jit(solution)/shard_map/ppermute | solution.py:21
  67.6 4.4 %collective-permute-start.2 = (f32[64,256]{0,1:T(8,128)S(1)}, f32[64,256]{0,1:T(8,128)S(1)}, u32[]{:S(2)}, u32[]{:S(2)}) collective-permute-start(f32[64,256]{0,1:T(8,128)S(1)} %get-tuple-element.57), channel_id=1, source_target_pairs={{0,508},{4,0},{8,4},{12,8},{16,12},{20,16},{24,20},{28,24},{32,28}... | collective-permute-start | bytes 196616 | tf_op jit(solution)/shard_map/ppermute | solution.py:21
  73.6 23.4 %all-to-all-start.2 = ((bf16[128,2,2,256]{3,2,1,0:T(2,128)(2,1)}), bf16[128,2,2,256]{3,2,1,0:T(2,128)(2,1)S(1)}, u32[]{:S(2)}, u32[]{:S(2)}) async-start(bf16[128,2,2,256]{3,2,1,0:T(2,128)(2,1)} %reshape.325), calls=%async_computation.2 | async-start | bytes 524288 | tf_op jit(solution)/shard_map/all_to_all | solution.py:142

commit v11 on v10

--- a/solution.py
+++ b/solution.py
@@ -30,8 +30,9 @@
 def per_device(tokens, shared_weight, value_weight, head_grad, sorted_slot):
     tok_count = tokens.shape[0]
     head_n = lax.axis_size("head")
-    spread = jnp.broadcast_to(tokens[None], (head_n,) + tokens.shape)
-    gathered = lax.all_to_all(spread, "head", 0, 0, tiled=True)
+    me_head = lax.axis_index("head")
+    parts = jnp.stack([tokens] + [shifted(tokens, "head", j) for j in range(1, head_n)])
+    gathered = jnp.take(parts, (me_head - jnp.arange(head_n)) % head_n, axis=0)
     whole = gathered.transpose(1, 0, 2).reshape(tok_count, head_n * tokens.shape[1])
     feat_count = whole.shape[1]
     head_width = shared_weight.shape[1]

time: 135 us -> 136 us (level)
  waiting for transfers between devices: 40 us -> 36 us
  other arithmetic: 4.52 us -> 7.77 us
  starting transfers between devices: 41.5 us -> 44 us
    ppermute x3 -> x6, starting transfers between devices: 5.88 us -> 19 us  [shifted(): return lax.ppermute(value, axis, pairs)]
    all_to_all x1 -> x0, starting transfers between devices: 9.44 us -> none  [per_device(): gathered = lax.all_to_all(spread, 'head', 0, 0, tiled=True)]
    all_to_all x1 -> x0, waiting for transfers between devices: 7.04 us -> none  [per_device(): gathered = lax.all_to_all(spread, 'head', 0, 0, tiled=True)]
    ppermute x3 -> x6, waiting for transfers between devices: 8.37 us -> 11.4 us  [shifted(): return lax.ppermute(value, axis, pairs)]
    another operation x2 -> x3, other arithmetic: 1.31 us -> 3.05 us
  transfers between devices with their start and end apart: 6 -> 8, of which waited for: 5 -> 5; matrix products, arithmetic and copies ran while one was open for 7% -> 9% of each run, Pallas kernels for 0% -> 0%
where the time goes in v11:
time: 136 us; the launch traced here: 135 us
  starting transfers between devices  44 us (32%)
  waiting for transfers between devices  36 us (26%)
  blocking collectives  34.1 us (25%)
  other arithmetic  7.77 us (6%)
  local copies, waits for them, and re-layouts  7.54 us (6%)
  matrix products  4.04 us (3%)
    all_to_all x1, blocking collectives, per_device(): lax.all_to_all(grads.astype(jnp.bfloat16), ('z', 'y'), 0, 0, tiled=True)  34.1 us
    ppermute x6, starting transfers between devices, shifted(): return lax.ppermute(value, axis, pairs)  19 us
    all_to_all x1, starting transfers between devices, per_device(): lax.all_to_all(send_rows, SEQ, split_axis=0, concat_axis=0, tiled=True)  16.3 us
    all_to_all x1, waiting for transfers between devices, per_device(): lax.all_to_all(to_chip, SEQ, split_axis=0, concat_axis=0, tiled=True)  12.9 us
    all_to_all x1, waiting for transfers between devices, per_device(): lax.all_to_all(send_rows, SEQ, split_axis=0, concat_axis=0, tiled=True)  11.7 us
    ppermute x6, waiting for transfers between devices, shifted(): return lax.ppermute(value, axis, pairs)  11.4 us
    all_to_all x1, starting transfers between devices, per_device(): lax.all_to_all(to_chip, SEQ, split_axis=0, concat_axis=0, tiled=True)  8.7 us
  transfers between devices with their start and end apart: 8, of which 5 were waited for; matrix products, arithmetic and copies ran while one was open for 9% of the time, Pallas kernels for 0%

profile of v11, /device:TPU:6, one launch (start us, length us, event | category | flops | bytes accessed | tf_op | source)
XLA Modules:
  0.0 134.5 jit_solution(13103562213609032149)
XLA Ops:
  0.6 7.9 %collective-permute-start = (bf16[128,1024]{1,0:T(8,128)(2,1)}, bf16[128,1024]{1,0:T(8,128)(2,1)S(1)}, u32[]{:S(2)}, u32[]{:S(2)}) collective-permute-start(bf16[128,1024]{1,0:T(8,128)(2,1)} %param.13), channel_id=1, source_target_pairs={{0,1},{1,2},{2,3},{3,0},{4,5},{5,6},{6,7},{7,4},{8,9},{9,10},{10,1... | collective-permute-start | bytes 786440 | tf_op jit(solution)/shard_map/ppermute | solution.py:21
  8.5 1.9 %collective-permute-start.2 = (bf16[128,1024]{1,0:T(8,128)(2,1)}, bf16[128,1024]{1,0:T(8,128)(2,1)S(1)}, u32[]{:S(2)}, u32[]{:S(2)}) collective-permute-start(bf16[128,1024]{1,0:T(8,128)(2,1)} %param.13), channel_id=1, source_target_pairs={{0,3},{1,0},{2,1},{3,2},{4,7},{5,4},{6,5},{7,6},{8,11},{9,8},{10,9... | collective-permute-start | bytes 786440 | tf_op jit(solution)/shard_map/ppermute | solution.py:21
  10.4 3.4 %collective-permute-start.1 = (bf16[128,1024]{1,0:T(8,128)(2,1)}, bf16[128,1024]{1,0:T(8,128)(2,1)S(1)}, u32[]{:S(2)}, u32[]{:S(2)}) collective-permute-start(bf16[128,1024]{1,0:T(8,128)(2,1)} %param.13), channel_id=1, source_target_pairs={{0,2},{1,3},{2,0},{3,1},{4,6},{5,7},{6,4},{7,5},{8,10},{9,11},{10,... | collective-permute-start | bytes 786440 | tf_op jit(solution)/shard_map/ppermute | solution.py:21
  13.9 0.7 and_select_fusion.2
  14.7 0.7 fusion.67
  15.5 0.9 copy.41
  17.1 1.3 broadcast_select_fusion
  18.4 3.0 %collective-permute-done.2 = bf16[128,1024]{1,0:T(8,128)(2,1)S(1)} collective-permute-done((bf16[128,1024]{1,0:T(8,128)(2,1)}, bf16[128,1024]{1,0:T(8,128)(2,1)S(1)}, u32[]{:S(2)}, u32[]{:S(2)}) %collective-permute-start.2) | collective-permute-done | bytes 262176 | tf_op jit(solution)/shard_map/ppermute | solution.py:21
  21.4 1.1 pad_maximum_fusion
  24.5 0.7 copy-done.1
  26.1 0.8 all_to_all.14
  26.9 16.3 %all-to-all-start = ((bf16[128,2,512]{2,1,0:T(2,128)(2,1)}), bf16[128,2,512]{2,1,0:T(2,128)(2,1)S(1)}, u32[]{:S(2)}, u32[]{:S(2)}) async-start(bf16[128,2,512]{2,1,0:T(2,128)(2,1)} %all_to_all.14), calls=%async_computation | async-start | bytes 524288 | tf_op jit(solution)/shard_map/all_to_all | solution.py:74
  44.2 1.9 %collective-permute-start.3 = (bf16[128,2176]{0,1:T(8,128)(2,1)S(1)}, bf16[128,2176]{0,1:T(8,128)(2,1)}, u32[]{:S(2)}, u32[]{:S(2)}) collective-permute-start(bf16[128,2176]{0,1:T(8,128)(2,1)S(1)} %get-tuple-element.53), channel_id=1, source_target_pairs={{0,4},{4,0},{1,5},{5,1},{2,6},{6,2},{3,7},{7,3},{8,12},{12,8},{9,1... | collective-permute-start | bytes 1671176 | tf_op jit(solution)/shard_map/ppermute | solution.py:21
  46.2 11.7 %all-to-all-done = bf16[128,2,512]{2,1,0:T(2,128)(2,1)S(1)} async-done(((bf16[128,2,512]{2,1,0:T(2,128)(2,1)}), bf16[128,2,512]{2,1,0:T(2,128)(2,1)S(1)}, u32[]{:S(2)}, u32[]{:S(2)}) %all-to-all-start) | async-done | bytes 262176 | tf_op jit(solution)/shard_map/all_to_all | solution.py:74
  58.9 2.0 %collective-permute-start.4 = (bf16[64,256]{1,0:T(8,128)(2,1)S(1)}, bf16[64,256]{1,0:T(8,128)(2,1)S(1)}, u32[]{:S(2)}, u32[]{:S(2)}) collective-permute-start(bf16[64,256]{1,0:T(8,128)(2,1)S(1)} %slice.181), channel_id=1, source_target_pairs={{0,4},{4,8},{8,12},{12,16},{16,20},{20,24},{24,28},{28,32},{32,36}... | collective-permute-start | bytes 98312 | tf_op jit(solution)/shard_map/ppermute | solution.py:21
  61.5 6.0 %collective-permute-done.4 = bf16[64,256]{1,0:T(8,128)(2,1)S(1)} collective-permute-done((bf16[64,256]{1,0:T(8,128)(2,1)S(1)}, bf16[64,256]{1,0:T(8,128)(2,1)S(1)}, u32[]{:S(2)}, u32[]{:S(2)}) %collective-permute-start.4) | collective-permute-done | bytes 32800 | tf_op jit(solution)/shard_map/ppermute | solution.py:21
  69.1 1.9 %collective-permute-start.5 = (f32[64,256]{0,1:T(8,128)S(1)}, f32[64,256]{0,1:T(8,128)S(1)}, u32[]{:S(2)}, u32[]{:S(2)}) collective-permute-start(f32[64,256]{0,1:T(8,128)S(1)} %get-tuple-element.57), channel_id=1, source_target_pairs={{0,508},{4,0},{8,4},{12,8},{16,12},{20,16},{24,20},{28,24},{32,28}... | collective-permute-start | bytes 196616 | tf_op jit(solution)/shard_map/ppermute | solution.py:21
  71.2 2.4 %collective-permute-done.5 = f32[64,256]{0,1:T(8,128)S(1)} collective-permute-done((f32[64,256]{0,1:T(8,128)S(1)}, f32[64,256]{0,1:T(8,128)S(1)}, u32[]{:S(2)}, u32[]{:S(2)}) %collective-permute-start.5) | collective-permute-done | bytes 65568 | tf_op jit(solution)/shard_map/ppermute | solution.py:21
  74.3 0.8 reshape.378
  75.1 8.7 %all-to-all-start.1 = ((bf16[128,2,2,256]{3,2,1,0:T(2,128)(2,1)}), bf16[128,2,2,256]{3,2,1,0:T(2,128)(2,1)S(1)}, u32[]{:S(2)}, u32[]{:S(2)}) async-start(bf16[128,2,2,256]{3,2,1,0:T(2,128)(2,1)} %reshape.378), calls=%async_computation.1 | async-start | bytes 524288 | tf_op jit(solution)/shard_map/all_to_all | solution.py:143
  83.8 1.1 slice.173
  84.9 0.7 fusion.65
  85.6 12.9 %all-to-all-done.1 = bf16[128,2,2,256]{3,2,1,0:T(2,128)(2,1)S(1)} async-done(((bf16[128,2,2,256]{3,2,1,0:T(2,128)(2,1)}), bf16[128,2,2,256]{3,2,1,0:T(2,128)(2,1)S(1)}, u32[]{:S(2)}, u32[]{:S(2)}) %all-to-all-start.1) | async-done | bytes 262176 | tf_op jit(solution)/shard_map/all_to_all | solution.py:143
  99.7 34.1 %all_to_all.22 = bf16[64,32,256]{2,1,0:T(8,128)(2,1)S(1)} all-to-all(bf16[64,32,256]{2,1,0:T(8,128)(2,1)S(1)} %bitcast.101), channel_id=1, replica_groups=mesh['z'=8,'y'=8,'c'=2,'head'=4] {'z','y'}, dimensions={0} | all-to-all | bytes 2097152 | tf_op jit(solution)/shard_map/all_to_all | solution.py:175
  (72 shorter events, 10.7 us)
Async XLA Ops:
  0.6 23.3 %copy-start = (bf16[4096,128]{1,0:T(8,128)(2,1)S(1)}, bf16[4096,128]{1,0:T(8,128)(2,1)}, u32[]{:S(2)}) copy-start(bf16[4096,128]{1,0:T(8,128)(2,1)} %param.15) | copy-start | bytes 3145732
  0.6 17.7 %collective-permute-start = (bf16[128,1024]{1,0:T(8,128)(2,1)}, bf16[128,1024]{1,0:T(8,128)(2,1)S(1)}, u32[]{:S(2)}, u32[]{:S(2)}) collective-permute-start(bf16[128,1024]{1,0:T(8,128)(2,1)} %param.13), channel_id=1, source_target_pairs={{0,1},{1,2},{2,3},{3,0},{4,5},{5,6},{6,7},{7,4},{8,9},{9,10},{10,1... | collective-permute-start | bytes 786440 | tf_op jit(solution)/shard_map/ppermute | solution.py:21
  8.5 12.9 %collective-permute-start.2 = (bf16[128,1024]{1,0:T(8,128)(2,1)}, bf16[128,1024]{1,0:T(8,128)(2,1)S(1)}, u32[]{:S(2)}, u32[]{:S(2)}) collective-permute-start(bf16[128,1024]{1,0:T(8,128)(2,1)} %param.13), channel_id=1, source_target_pairs={{0,3},{1,0},{2,1},{3,2},{4,7},{5,4},{6,5},{7,6},{8,11},{9,8},{10,9... | collective-permute-start | bytes 786440 | tf_op jit(solution)/shard_map/ppermute | solution.py:21
  10.4 11.0 %collective-permute-start.1 = (bf16[128,1024]{1,0:T(8,128)(2,1)}, bf16[128,1024]{1,0:T(8,128)(2,1)S(1)}, u32[]{:S(2)}, u32[]{:S(2)}) collective-permute-start(bf16[128,1024]{1,0:T(8,128)(2,1)} %param.13), channel_id=1, source_target_pairs={{0,2},{1,3},{2,0},{3,1},{4,6},{5,7},{6,4},{7,5},{8,10},{9,11},{10,... | collective-permute-start | bytes 786440 | tf_op jit(solution)/shard_map/ppermute | solution.py:21
  24.0 1.2 copy-start.1
  26.9 31.0 %all-to-all-start = ((bf16[128,2,512]{2,1,0:T(2,128)(2,1)}), bf16[128,2,512]{2,1,0:T(2,128)(2,1)S(1)}, u32[]{:S(2)}, u32[]{:S(2)}) async-start(bf16[128,2,512]{2,1,0:T(2,128)(2,1)} %all_to_all.14), calls=%async_computation | async-start | bytes 524288 | tf_op jit(solution)/shard_map/all_to_all | solution.py:74
  44.2 39.6 %collective-permute-start.3 = (bf16[128,2176]{0,1:T(8,128)(2,1)S(1)}, bf16[128,2176]{0,1:T(8,128)(2,1)}, u32[]{:S(2)}, u32[]{:S(2)}) collective-permute-start(bf16[128,2176]{0,1:T(8,128)(2,1)S(1)} %get-tuple-element.53), channel_id=1, source_target_pairs={{0,4},{4,0},{1,5},{5,1},{2,6},{6,2},{3,7},{7,3},{8,12},{12,8},{9,1... | collective-permute-start | bytes 1671176 | tf_op jit(solution)/shard_map/ppermute | solution.py:21
  58.9 8.6 %collective-permute-start.4 = (bf16[64,256]{1,0:T(8,128)(2,1)S(1)}, bf16[64,256]{1,0:T(8,128)(2,1)S(1)}, u32[]{:S(2)}, u32[]{:S(2)}) collective-permute-start(bf16[64,256]{1,0:T(8,128)(2,1)S(1)} %slice.181), channel_id=1, source_target_pairs={{0,4},{4,8},{8,12},{12,16},{16,20},{20,24},{24,28},{28,32},{32,36}... | collective-permute-start | bytes 98312 | tf_op jit(solution)/shard_map/ppermute | solution.py:21
  69.1 4.4 %collective-permute-start.5 = (f32[64,256]{0,1:T(8,128)S(1)}, f32[64,256]{0,1:T(8,128)S(1)}, u32[]{:S(2)}, u32[]{:S(2)}) collective-permute-start(f32[64,256]{0,1:T(8,128)S(1)} %get-tuple-element.57), channel_id=1, source_target_pairs={{0,508},{4,0},{8,4},{12,8},{16,12},{20,16},{24,20},{28,24},{32,28}... | collective-permute-start | bytes 196616 | tf_op jit(solution)/shard_map/ppermute | solution.py:21
  75.1 23.4 %all-to-all-start.1 = ((bf16[128,2,2,256]{3,2,1,0:T(2,128)(2,1)}), bf16[128,2,2,256]{3,2,1,0:T(2,128)(2,1)S(1)}, u32[]{:S(2)}, u32[]{:S(2)}) async-start(bf16[128,2,2,256]{3,2,1,0:T(2,128)(2,1)} %reshape.378), calls=%async_computation.1 | async-start | bytes 524288 | tf_op jit(solution)/shard_map/all_to_all | solution.py:143

commit v12 on v10

--- a/solution.py
+++ b/solution.py
@@ -54,39 +54,65 @@
     buffer_index = target * capacity + jnp.sum(before * one_hot.astype(jnp.float32), axis=1).astype(
         jnp.int32
     )
-    slot_block = jnp.zeros((tok_count, head_width), jnp.bfloat16).at[:, 0].set(
-        local_slot.astype(jnp.bfloat16)
-    )
-    payload = jnp.concatenate([query, values, head_grad, slot_block], axis=1)
+    is_tail = local_slot >= tail_start
+    is_head = local_slot < GROUP
+
+    def rank_within(mask):
+        hot = one_hot * mask[:, None].astype(jnp.bfloat16)
+        seen = jnp.dot(earlier_rows, hot, preferred_element_type=jnp.float32)
+        return jnp.sum(seen * one_hot.astype(jnp.float32), axis=1).astype(jnp.int32)
+
+    lanes = 3 * capacity
+    slots = [
+        target * lanes + buffer_index % capacity,
+        ((target + 1) % peer_count) * lanes + capacity + rank_within(is_tail),
+        ((target - 1) % peer_count) * lanes + 2 * capacity + rank_within(is_head),
+    ]
+    masks = [every_row, is_tail, is_head]
+    window = 2 * GROUP + tok_count
+    places = [local_slot + GROUP, local_slot - tail_start, local_slot + GROUP + tok_count]
+    send_ids = jnp.arange(peer_count * lanes, dtype=jnp.int32)
+    send_rows = jnp.zeros((peer_count * lanes, 4 * head_width), jnp.float32)
+    used = jnp.zeros((peer_count * lanes,), jnp.float32)
+    for slot, mask, place in zip(slots, masks, places):
+        index_block = jnp.zeros((tok_count, head_width), jnp.bfloat16).at[:, 0].set(
+            place.astype(jnp.bfloat16)
+        )
+        rows = jnp.concatenate([query, values, head_grad, index_block], axis=1)
+        pick = ((send_ids[:, None] == slot[None, :]) & mask[None, :]).astype(jnp.bfloat16)
+        send_rows = send_rows + jnp.dot(pick, rows, preferred_element_type=jnp.float32)
+        used = used + jnp.sum(pick.astype(jnp.float32), axis=1)
+    send_rows = send_rows.astype(jnp.bfloat16)
+    empty = (send_ids[:, None] * 0 + jnp.arange(head_width)[None, :]) == 0
+    send_rows = send_rows.at[:, 3 * head_width :].set(
+        jnp.where(
+            empty & (used[:, None] == 0),
+            jnp.bfloat16(window),
+            send_rows[:, 3 * head_width :],
+        )
+    )
     buffer_ids = jnp.arange(peer_count * capacity, dtype=jnp.int32)
     to_buffer = (buffer_ids[:, None] == buffer_index[None, :]).astype(jnp.bfloat16)
-    send_rows = jnp.dot(to_buffer, payload, preferred_element_type=jnp.float32).astype(jnp.bfloat16)
-    empty = (buffer_ids[:, None] * 0 + jnp.arange(head_width)[None, :]) == 0
-    used = jnp.sum(to_buffer.astype(jnp.float32), axis=1) > 0
-    send_rows = send_rows.at[:, 3 * head_width :].set(
-        jnp.where(
-            empty & ~used[:, None],
-            jnp.bfloat16(tok_count),
-            send_rows[:, 3 * head_width :],
-        )
-    )
     recv_rows = lax.all_to_all(send_rows, SEQ, split_axis=0, concat_axis=0, tiled=True)
-    recv_slots = recv_rows[:, 3 * head_width].astype(jnp.int32)
+    recv_index = recv_rows[:, 3 * head_width].astype(jnp.int32)
+    window_ids = jnp.arange(window, dtype=jnp.int32)
+    to_window = (window_ids[:, None] == recv_index[None, :]).astype(jnp.bfloat16)
+    window_rows = jnp.dot(
+        to_window, recv_rows[:, : 3 * head_width], preferred_element_type=jnp.float32
+    ).astype(jnp.bfloat16)
+    recv_slots = recv_index.reshape(peer_count, lanes)[:, :capacity].reshape(-1) - GROUP
     to_sorted = (row_ids[:, None] == recv_slots[None, :]).astype(jnp.bfloat16)
-    sorted_rows = jnp.dot(
-        to_sorted, recv_rows[:, : 3 * head_width], preferred_element_type=jnp.float32
-    ).astype(jnp.bfloat16)
-    halo_rows = shifted(sorted_rows[tail_start:, : 2 * head_width], SEQ, 1)
+    sorted_rows = window_rows[GROUP : GROUP + tok_count]
     sorted_query = sorted_rows[:, :head_width]
-    own_keys = unit_keys(sorted_query).reshape(group_count, GROUP, head_width)
-    halo_keys = unit_keys(halo_rows[:, :head_width])
-    q_blocks = sorted_query.reshape(group_count, GROUP, head_width)
-    v_blocks = sorted_rows[:, head_width : 2 * head_width].reshape(group_count, GROUP, head_width)
-    g_blocks = sorted_rows[:, 2 * head_width :].reshape(group_count, GROUP, head_width)
-    prev_keys = jnp.concatenate([halo_keys[None], own_keys[:-1]], axis=0)
-    prev_values = jnp.concatenate([halo_rows[None, :, head_width:], v_blocks[:-1]], axis=0)
-    key_window = jnp.concatenate([own_keys, prev_keys], axis=1)
-    value_window = jnp.concatenate([v_blocks, prev_values], axis=1)
+    span = group_count + 2
+    all_q = window_rows[:, :head_width].reshape(span, GROUP, head_width)
+    all_v = window_rows[:, head_width : 2 * head_width].reshape(span, GROUP, head_width)
+    all_g = window_rows[:, 2 * head_width :].reshape(span, GROUP, head_width)
+    all_k = unit_keys(window_rows[:, :head_width]).reshape(span, GROUP, head_width)
+    q_blocks = all_q[1:]
+    g_blocks = all_g[1:]
+    key_window = jnp.concatenate([all_k[1:], all_k[:-1]], axis=1)
+    value_window = jnp.concatenate([all_v[1:], all_v[:-1]], axis=1)
     scores = (
         jnp.einsum("cqd,ckd->cqk", q_blocks, key_window, preferred_element_type=jnp.float32)
         * scale_factor
@@ -99,7 +125,8 @@
     probs_low = probs.astype(jnp.bfloat16)
     dscore_low = dscore.astype(jnp.bfloat16)
     dquery = (
-        jnp.einsum("cqk,ckd->cqd", dscore_low, key_window, preferred_element_type=jnp.float32)
+        jnp.einsum("cqk,ckd->cqd", dscore_low[:group_count], key_window[:group_count],
+                   preferred_element_type=jnp.float32)
         * scale_factor
     )
     dkey_window = (
@@ -110,11 +137,7 @@
         "cqk,cqd->ckd", probs_low, g_blocks, preferred_element_type=jnp.float32
     )
     grad_window = jnp.concatenate([dkey_window, dvalue_window], axis=-1)
-    own_part = grad_window[:, :GROUP]
-    later_part = grad_window[1:, GROUP:]
-    outgoing = grad_window[0, GROUP:]
-    incoming = shifted(outgoing, SEQ, -1)
-    key_value = (own_part + jnp.concatenate([later_part, incoming[None]], axis=0)).reshape(
+    key_value = (grad_window[:group_count, :GROUP] + grad_window[1:, GROUP:]).reshape(
         tok_count, 2 * head_width
     )
     dquery_s = dquery.reshape(tok_count, head_width)

time: 135 us -> 141 us (1.044)
  starting transfers between devices: 41.5 us -> 35.9 us
  waiting for transfers between devices: 40 us -> 45.5 us
  matrix products: 4.03 us -> 6.77 us
  other arithmetic: 4.52 us -> 6.63 us
  local copies, waits for them, and re-layouts: 7.86 us -> 9.82 us
    all_to_all x1, waiting for transfers between devices: 11.7 us -> 27.1 us  [per_device(): lax.all_to_all(send_rows, SEQ, split_axis=0, concat_axis=0, tiled=True)]
    ppermute x3 -> x1, waiting for transfers between devices: 8.37 us -> 0.01 us  [shifted(): return lax.ppermute(value, axis, pairs)]
    ppermute x3 -> x1, starting transfers between devices: 5.88 us -> 1.91 us  [shifted(): return lax.ppermute(value, axis, pairs)]
    dot_general x3 -> x7, matrix products: 0.56 us -> 3.07 us  [the longest x1 1.44 us: per_device(): jnp.dot(to_window, recv_rows[:, :3 * head_width], preferred_element_type=...]
    all_to_all x1, starting transfers between devices: 8.7 us -> 7.16 us  [per_device(): lax.all_to_all(to_chip, SEQ, split_axis=0, concat_axis=0, tiled=True)]
    all_to_all x2, local copies, waits for them, and re-layouts: 0.9 us -> 2.39 us  [per_device(): lax.all_to_all(send_rows, SEQ, split_axis=0, concat_axis=0, tiled=True)]
    all_to_all x1, waiting for transfers between devices: 7.04 us -> 5.56 us  [per_device(): gathered = lax.all_to_all(spread, 'head', 0, 0, tiled=True)]
  transfers between devices with their start and end apart: 6 -> 4, of which waited for: 5 -> 3; matrix products, arithmetic and copies ran while one was open for 7% -> 10% of each run, Pallas kernels for 0% -> 0%
where the time goes in v12:
time: 141 us; the launch traced here: 140 us
  waiting for transfers between devices  45.5 us (32%)
  starting transfers between devices  35.9 us (25%)
  blocking collectives  34.1 us (24%)
  local copies, waits for them, and re-layouts  9.82 us (7%)
  matrix products  6.77 us (5%)
  other arithmetic  6.63 us (5%)
    all_to_all x1, blocking collectives, per_device(): lax.all_to_all(grads.astype(jnp.bfloat16), ('z', 'y'), 0, 0, tiled=True)  34.1 us
    all_to_all x1, waiting for transfers between devices, per_device(): lax.all_to_all(send_rows, SEQ, split_axis=0, concat_axis=0, tiled=True)  27.1 us
    all_to_all x1, starting transfers between devices, per_device(): lax.all_to_all(send_rows, SEQ, split_axis=0, concat_axis=0, tiled=True)  17.5 us
    all_to_all x1, waiting for transfers between devices, per_device(): lax.all_to_all(to_chip, SEQ, split_axis=0, concat_axis=0, tiled=True)  12.9 us
    all_to_all x1, starting transfers between devices, per_device(): gathered = lax.all_to_all(spread, 'head', 0, 0, tiled=True)  9.31 us
    all_to_all x1, starting transfers between devices, per_device(): lax.all_to_all(to_chip, SEQ, split_axis=0, concat_axis=0, tiled=True)  7.16 us
    all_to_all x1, waiting for transfers between devices, per_device(): gathered = lax.all_to_all(spread, 'head', 0, 0, tiled=True)  5.56 us
  transfers between devices with their start and end apart: 4, of which 3 were waited for; matrix products, arithmetic and copies ran while one was open for 10% of the time, Pallas kernels for 0%

profile of v12, /device:TPU:6, one launch (start us, length us, event | category | flops | bytes accessed | tf_op | source)
XLA Modules:
  0.0 139.8 jit_solution(479377037964610293)
XLA Ops:
  0.6 1.2 copy.35
  1.9 1.1 broadcast_in_dim.26
  3.0 9.3 %all-to-all-start = ((bf16[4,128,1024]{1,2,0:T(8,128)(2,1)}), bf16[4,128,1024]{1,2,0:T(8,128)(2,1)S(1)}, u32[]{:S(2)}, u32[]{:S(2)}) async-start(bf16[4,128,1024]{1,2,0:T(8,128)(2,1)} %broadcast_in_dim.26), calls=%async_computation | async-start | bytes 2097152 | tf_op jit(solution)/shard_map/all_to_all | solution.py:34
  12.6 0.6 compare_reduce_fusion
  14.2 0.7 broadcast_select_fusion
  14.9 0.7 broadcast_select_fusion.1
  15.6 5.6 %all-to-all-done = bf16[4,128,1024]{1,2,0:T(8,128)(2,1)S(1)} async-done(((bf16[4,128,1024]{1,2,0:T(8,128)(2,1)}), bf16[4,128,1024]{1,2,0:T(8,128)(2,1)S(1)}, u32[]{:S(2)}, u32[]{:S(2)}) %all-to-all-start) | async-done | bytes 1048608 | tf_op jit(solution)/shard_map/all_to_all | solution.py:34
  23.6 1.3 all_to_all.18
  24.9 17.5 %all-to-all-start.1 = ((bf16[128,6,512]{2,1,0:T(8,128)(2,1)}), bf16[128,6,512]{2,1,0:T(8,128)(2,1)S(1)}, u32[]{:S(2)}, u32[]{:S(2)}) async-start(bf16[128,6,512]{2,1,0:T(8,128)(2,1)} %all_to_all.18), calls=%async_computation.1 | async-start | bytes 2097152 | tf_op jit(solution)/shard_map/all_to_all | solution.py:96
  42.5 1.0 fusion.16
  43.6 1.9 %collective-permute-start = (bf16[128,2176]{0,1:T(8,128)(2,1)}, bf16[128,2176]{0,1:T(8,128)(2,1)}, u32[]{:S(2)}, u32[]{:S(2)}) collective-permute-start(bf16[128,2176]{0,1:T(8,128)(2,1)} %get-tuple-element.83), channel_id=1, source_target_pairs={{0,4},{4,0},{1,5},{5,1},{2,6},{6,2},{3,7},{7,3},{8,12},{12,8},{9,1... | collective-permute-start | bytes 1671176 | tf_op jit(solution)/shard_map/ppermute | solution.py:21
  45.5 27.1 %all-to-all-done.1 = bf16[128,6,512]{2,1,0:T(8,128)(2,1)S(1)} async-done(((bf16[128,6,512]{2,1,0:T(8,128)(2,1)}), bf16[128,6,512]{2,1,0:T(8,128)(2,1)S(1)}, u32[]{:S(2)}, u32[]{:S(2)}) %all-to-all-start.1) | async-done | bytes 786464 | tf_op jit(solution)/shard_map/all_to_all | solution.py:96
  72.6 1.1 all_to_all.20
  73.7 1.1 convert_reduce_fusion.1
  74.8 1.4 %convolution_convert_fusion.2 = bf16[256,384]{1,0:T(8,128)(2,1)S(1)} fusion(bf16[768,512]{1,0:T(8,128)(2,1)} %all_to_all.20, s32[768]{0:T(1024)S(1)} %convert_reduce_fusion.1), kind=kOutput, calls=%fused_computation.7 | convolution fusion | flops 151289856 | bytes 789504 | tf_op jit(solution)/shard_map/dot_general | solution.py:100
  76.9 0.6 fusion.81
  78.3 1.1 slice_reduce_fusion
  81.0 0.8 reshape.456
  81.8 7.2 %all-to-all-start.2 = ((bf16[128,2,2,256]{3,2,1,0:T(2,128)(2,1)}), bf16[128,2,2,256]{3,2,1,0:T(2,128)(2,1)S(1)}, u32[]{:S(2)}, u32[]{:S(2)}) async-start(bf16[128,2,2,256]{3,2,1,0:T(2,128)(2,1)} %reshape.456), calls=%async_computation.2 | async-start | bytes 524288 | tf_op jit(solution)/shard_map/all_to_all | solution.py:165
  89.0 1.1 slice.235
  90.1 0.7 fusion.105
  90.8 12.9 %all-to-all-done.2 = bf16[128,2,2,256]{3,2,1,0:T(2,128)(2,1)S(1)} async-done(((bf16[128,2,2,256]{3,2,1,0:T(2,128)(2,1)}), bf16[128,2,2,256]{3,2,1,0:T(2,128)(2,1)S(1)}, u32[]{:S(2)}, u32[]{:S(2)}) %all-to-all-start.2) | async-done | bytes 262176 | tf_op jit(solution)/shard_map/all_to_all | solution.py:165
  104.9 34.1 %all_to_all.27 = bf16[64,32,256]{2,1,0:T(8,128)(2,1)S(1)} all-to-all(bf16[64,32,256]{2,1,0:T(8,128)(2,1)S(1)} %bitcast.115), channel_id=1, replica_groups=mesh['z'=8,'y'=8,'c'=2,'head'=4] {'z','y'}, dimensions={0} | all-to-all | bytes 2097152 | tf_op jit(solution)/shard_map/all_to_all | solution.py:197
  139.1 0.6 fusion.142
  (68 shorter events, 8.1 us)
Async XLA Ops:
  0.6 20.5 %copy-start = (bf16[4096,128]{1,0:T(8,128)(2,1)S(1)}, bf16[4096,128]{1,0:T(8,128)(2,1)}, u32[]{:S(2)}) copy-start(bf16[4096,128]{1,0:T(8,128)(2,1)} %param.19) | copy-start | bytes 3145732
  1.9 10.5 %copy-start.3 = (s32[1,128]{1,0:T(1,128)S(1)}, s32[1,128]{1,0:T(1,128)}, u32[]{:S(2)}) copy-start(s32[1,128]{1,0:T(1,128)} %param.21) | copy-start | bytes 1540
  1.9 11.7 %copy-start.2 = (bf16[128,128]{1,0:T(8,128)(2,1)S(1)}, bf16[128,128]{1,0:T(8,128)(2,1)}, u32[]{:S(2)}) copy-start(bf16[128,128]{1,0:T(8,128)(2,1)} %param.20) | copy-start | bytes 98308
  3.0 18.1 %all-to-all-start = ((bf16[4,128,1024]{1,2,0:T(8,128)(2,1)}), bf16[4,128,1024]{1,2,0:T(8,128)(2,1)S(1)}, u32[]{:S(2)}, u32[]{:S(2)}) async-start(bf16[4,128,1024]{1,2,0:T(8,128)(2,1)} %broadcast_in_dim.26), calls=%async_computation | async-start | bytes 2097152 | tf_op jit(solution)/shard_map/all_to_all | solution.py:34
  12.3 9.3 %copy-start.1 = (bf16[4096,128]{1,0:T(8,128)(2,1)S(1)}, bf16[4096,128]{1,0:T(8,128)(2,1)}, u32[]{:S(2)}) copy-start(bf16[4096,128]{1,0:T(8,128)(2,1)} %param.18) | copy-start | bytes 3145732
  24.9 47.7 %all-to-all-start.1 = ((bf16[128,6,512]{2,1,0:T(8,128)(2,1)}), bf16[128,6,512]{2,1,0:T(8,128)(2,1)S(1)}, u32[]{:S(2)}, u32[]{:S(2)}) async-start(bf16[128,6,512]{2,1,0:T(8,128)(2,1)} %all_to_all.18), calls=%async_computation.1 | async-start | bytes 2097152 | tf_op jit(solution)/shard_map/all_to_all | solution.py:96
  43.6 45.5 %collective-permute-start = (bf16[128,2176]{0,1:T(8,128)(2,1)}, bf16[128,2176]{0,1:T(8,128)(2,1)}, u32[]{:S(2)}, u32[]{:S(2)}) collective-permute-start(bf16[128,2176]{0,1:T(8,128)(2,1)} %get-tuple-element.83), channel_id=1, source_target_pairs={{0,4},{4,0},{1,5},{5,1},{2,6},{6,2},{3,7},{7,3},{8,12},{12,8},{9,1... | collective-permute-start | bytes 1671176 | tf_op jit(solution)/shard_map/ppermute | solution.py:21
  81.8 21.9 %all-to-all-start.2 = ((bf16[128,2,2,256]{3,2,1,0:T(2,128)(2,1)}), bf16[128,2,2,256]{3,2,1,0:T(2,128)(2,1)S(1)}, u32[]{:S(2)}, u32[]{:S(2)}) async-start(bf16[128,2,2,256]{3,2,1,0:T(2,128)(2,1)} %reshape.456), calls=%async_computation.2 | async-start | bytes 524288 | tf_op jit(solution)/shard_map/all_to_all | solution.py:165

commit v13 on v10

--- a/solution.py
+++ b/solution.py
@@ -141,7 +141,7 @@
     )
     back_rows = lax.all_to_all(to_chip, SEQ, split_axis=0, concat_axis=0, tiled=True)
     rows = feat_count // (nz * ny * nc)
-    blocks = whole.reshape(tok_count, nz, ny, nc, rows).transpose(3, 0, 1, 2, 4)
+    blocks = whole.reshape(tok_count, nz, ny, nc, rows).transpose(3, 0, 2, 1, 4)
     shares = blocks.reshape(nc, tok_count, ny * nz * rows)
     index_block = jnp.zeros((tok_count, head_width), jnp.bfloat16).at[:, 0].set(
         buffer_index.astype(jnp.bfloat16)
@@ -169,9 +169,9 @@
         (((0,), (0,)), ((), ())),
         preferred_element_type=jnp.float32,
     )
-    grads = grads.reshape(nz * ny, rows, 2 * head_width)
+    grads = grads.reshape(ny * nz, rows, 2 * head_width)
     grads = jnp.sum(
-        lax.all_to_all(grads.astype(jnp.bfloat16), ("z", "y"), 0, 0, tiled=True).astype(jnp.float32),
+        lax.all_to_all(grads.astype(jnp.bfloat16), ("y", "z"), 0, 0, tiled=True).astype(jnp.float32),
         axis=0,
     )
     grads = grads.reshape(rows, 2 * head_width)

time: 135 us -> 136 us (level)
  the two profiles are of different devices: /device:TPU:6 before, /device:TPU:16 now
where the time goes in v13:
time: 136 us; the launch traced here: 135 us
  waiting for transfers between devices  41.3 us (30%)
  starting transfers between devices  40.4 us (30%)
  blocking collectives  36 us (26%)
  local copies, waits for them, and re-layouts  7.86 us (6%)
  other arithmetic  4.52 us (3%)
  matrix products  4.04 us (3%)
    all_to_all x1, blocking collectives, per_device(): lax.all_to_all(grads.astype(jnp.bfloat16), ('y', 'z'), 0, 0, tiled=True)  36 us
    all_to_all x1, starting transfers between devices, per_device(): lax.all_to_all(send_rows, SEQ, split_axis=0, concat_axis=0, tiled=True)  17.3 us
    all_to_all x1, waiting for transfers between devices, per_device(): gathered = lax.all_to_all(spread, 'head', 0, 0, tiled=True)  13.3 us
    all_to_all x1, starting transfers between devices, per_device(): lax.all_to_all(to_chip, SEQ, split_axis=0, concat_axis=0, tiled=True)  12.8 us
    all_to_all x1, waiting for transfers between devices, per_device(): lax.all_to_all(to_chip, SEQ, split_axis=0, concat_axis=0, tiled=True)  12.1 us
    all_to_all x1, waiting for transfers between devices, per_device(): lax.all_to_all(send_rows, SEQ, split_axis=0, concat_axis=0, tiled=True)  10.8 us
    ppermute x3, starting transfers between devices, shifted(): return lax.ppermute(value, axis, pairs)  5.87 us
    ppermute x3, waiting for transfers between devices, shifted(): return lax.ppermute(value, axis, pairs)  5.17 us
  transfers between devices with their start and end apart: 6, of which 5 were waited for; matrix products, arithmetic and copies ran while one was open for 7% of the time, Pallas kernels for 0%

profile of v13, /device:TPU:16, one launch (start us, length us, event | category | flops | bytes accessed | tf_op | source)
XLA Modules:
  0.0 135.2 jit_solution(16775655404123433630)
XLA Ops:
  0.6 1.2 copy.36
  1.9 1.1 broadcast_in_dim.34
  3.0 4.4 %all-to-all-start = ((bf16[4,128,1024]{1,2,0:T(8,128)(2,1)}), bf16[4,128,1024]{1,2,0:T(8,128)(2,1)S(1)}, u32[]{:S(2)}, u32[]{:S(2)}) async-start(bf16[4,128,1024]{1,2,0:T(8,128)(2,1)} %broadcast_in_dim.34), calls=%async_computation | async-start | bytes 2097152 | tf_op jit(solution)/shard_map/all_to_all | solution.py:34
  7.7 0.7 compare_reduce_fusion
  8.5 0.7 broadcast_select_fusion
  9.2 13.3 %all-to-all-done = bf16[4,128,1024]{1,2,0:T(8,128)(2,1)S(1)} async-done(((bf16[4,128,1024]{1,2,0:T(8,128)(2,1)}), bf16[4,128,1024]{1,2,0:T(8,128)(2,1)S(1)}, u32[]{:S(2)}, u32[]{:S(2)}) %all-to-all-start) | async-done | bytes 1048608 | tf_op jit(solution)/shard_map/all_to_all | solution.py:34
  22.5 0.5 convolution_convert_fusion.6
  23.0 0.7 copy-done.1
  24.6 0.8 all_to_all.18
  25.4 17.3 %all-to-all-start.1 = ((bf16[128,2,512]{2,1,0:T(2,128)(2,1)}), bf16[128,2,512]{2,1,0:T(2,128)(2,1)S(1)}, u32[]{:S(2)}, u32[]{:S(2)}) async-start(bf16[128,2,512]{2,1,0:T(2,128)(2,1)} %all_to_all.18), calls=%async_computation.1 | async-start | bytes 524288 | tf_op jit(solution)/shard_map/all_to_all | solution.py:73
  42.7 0.7 broadcast_select_fusion.1
  43.8 2.0 %collective-permute-start = (bf16[128,2176]{0,1:T(8,128)(2,1)S(1)}, bf16[128,2176]{0,1:T(8,128)(2,1)}, u32[]{:S(2)}, u32[]{:S(2)}) collective-permute-start(bf16[128,2176]{0,1:T(8,128)(2,1)S(1)} %get-tuple-element.53), channel_id=1, source_target_pairs={{0,4},{4,0},{1,5},{5,1},{2,6},{6,2},{3,7},{7,3},{8,12},{12,8},{9,1... | collective-permute-start | bytes 1671176 | tf_op jit(solution)/shard_map/ppermute | solution.py:21
  45.8 10.8 %all-to-all-done.1 = bf16[128,2,512]{2,1,0:T(2,128)(2,1)S(1)} async-done(((bf16[128,2,512]{2,1,0:T(2,128)(2,1)}), bf16[128,2,512]{2,1,0:T(2,128)(2,1)S(1)}, u32[]{:S(2)}, u32[]{:S(2)}) %all-to-all-start.1) | async-done | bytes 262176 | tf_op jit(solution)/shard_map/all_to_all | solution.py:73
  57.6 1.9 %collective-permute-start.1 = (bf16[64,256]{1,0:T(8,128)(2,1)S(1)}, bf16[64,256]{1,0:T(8,128)(2,1)S(1)}, u32[]{:S(2)}, u32[]{:S(2)}) collective-permute-start(bf16[64,256]{1,0:T(8,128)(2,1)S(1)} %slice.179), channel_id=1, source_target_pairs={{0,4},{4,8},{8,12},{12,16},{16,20},{20,24},{24,28},{28,32},{32,36}... | collective-permute-start | bytes 98312 | tf_op jit(solution)/shard_map/ppermute | solution.py:21
  60.0 2.8 %collective-permute-done.1 = bf16[64,256]{1,0:T(8,128)(2,1)S(1)} collective-permute-done((bf16[64,256]{1,0:T(8,128)(2,1)S(1)}, bf16[64,256]{1,0:T(8,128)(2,1)S(1)}, u32[]{:S(2)}, u32[]{:S(2)}) %collective-permute-start.1) | collective-permute-done | bytes 32800 | tf_op jit(solution)/shard_map/ppermute | solution.py:21
  64.5 1.9 %collective-permute-start.2 = (f32[64,256]{0,1:T(8,128)S(1)}, f32[64,256]{0,1:T(8,128)S(1)}, u32[]{:S(2)}, u32[]{:S(2)}) collective-permute-start(f32[64,256]{0,1:T(8,128)S(1)} %get-tuple-element.57), channel_id=1, source_target_pairs={{0,508},{4,0},{8,4},{12,8},{16,12},{20,16},{24,20},{28,24},{32,28}... | collective-permute-start | bytes 196616 | tf_op jit(solution)/shard_map/ppermute | solution.py:21
  66.6 2.4 %collective-permute-done.2 = f32[64,256]{0,1:T(8,128)S(1)} collective-permute-done((f32[64,256]{0,1:T(8,128)S(1)}, f32[64,256]{0,1:T(8,128)S(1)}, u32[]{:S(2)}, u32[]{:S(2)}) %collective-permute-start.2) | collective-permute-done | bytes 65568 | tf_op jit(solution)/shard_map/ppermute | solution.py:21
  69.7 0.8 reshape.325
  70.5 12.8 %all-to-all-start.2 = ((bf16[128,2,2,256]{3,2,1,0:T(2,128)(2,1)}), bf16[128,2,2,256]{3,2,1,0:T(2,128)(2,1)S(1)}, u32[]{:S(2)}, u32[]{:S(2)}) async-start(bf16[128,2,2,256]{3,2,1,0:T(2,128)(2,1)} %reshape.325), calls=%async_computation.2 | async-start | bytes 524288 | tf_op jit(solution)/shard_map/all_to_all | solution.py:142
  83.4 1.1 slice.171
  84.4 0.7 fusion.62
  85.1 12.1 %all-to-all-done.2 = bf16[128,2,2,256]{3,2,1,0:T(2,128)(2,1)S(1)} async-done(((bf16[128,2,2,256]{3,2,1,0:T(2,128)(2,1)}), bf16[128,2,2,256]{3,2,1,0:T(2,128)(2,1)S(1)}, u32[]{:S(2)}, u32[]{:S(2)}) %all-to-all-start.2) | async-done | bytes 262176 | tf_op jit(solution)/shard_map/all_to_all | solution.py:142
  98.4 36.0 %all_to_all.27 = bf16[64,32,256]{2,1,0:T(8,128)(2,1)S(1)} all-to-all(bf16[64,32,256]{2,1,0:T(8,128)(2,1)S(1)} %bitcast.96), channel_id=1, replica_groups=mesh['z'=8,'y'=8,'c'=2,'head'=4] {'y','z'}, dimensions={0} | all-to-all | bytes 2097152 | tf_op jit(solution)/shard_map/all_to_all | solution.py:174
  134.6 0.6 fusion.83
  (67 shorter events, 6.9 us)
Async XLA Ops:
  0.6 21.9 %copy-start = (bf16[4096,128]{1,0:T(8,128)(2,1)S(1)}, bf16[4096,128]{1,0:T(8,128)(2,1)}, u32[]{:S(2)}) copy-start(bf16[4096,128]{1,0:T(8,128)(2,1)} %param.15) | copy-start | bytes 3145732
  3.0 4.4 %copy-start.3 = (s32[1,128]{1,0:T(1,128)S(1)}, s32[1,128]{1,0:T(1,128)}, u32[]{:S(2)}) copy-start(s32[1,128]{1,0:T(1,128)} %param.17) | copy-start | bytes 1540
  3.0 4.6 %copy-start.2 = (bf16[128,128]{1,0:T(8,128)(2,1)S(1)}, bf16[128,128]{1,0:T(8,128)(2,1)}, u32[]{:S(2)}) copy-start(bf16[128,128]{1,0:T(8,128)(2,1)} %param.16) | copy-start | bytes 98308
  3.0 19.5 %all-to-all-start = ((bf16[4,128,1024]{1,2,0:T(8,128)(2,1)}), bf16[4,128,1024]{1,2,0:T(8,128)(2,1)S(1)}, u32[]{:S(2)}, u32[]{:S(2)}) async-start(bf16[4,128,1024]{1,2,0:T(8,128)(2,1)} %broadcast_in_dim.34), calls=%async_computation | async-start | bytes 2097152 | tf_op jit(solution)/shard_map/all_to_all | solution.py:34
  22.5 1.2 copy-start.1
  25.4 31.2 %all-to-all-start.1 = ((bf16[128,2,512]{2,1,0:T(2,128)(2,1)}), bf16[128,2,512]{2,1,0:T(2,128)(2,1)S(1)}, u32[]{:S(2)}, u32[]{:S(2)}) async-start(bf16[128,2,512]{2,1,0:T(2,128)(2,1)} %all_to_all.18), calls=%async_computation.1 | async-start | bytes 524288 | tf_op jit(solution)/shard_map/all_to_all | solution.py:73
  43.8 39.6 %collective-permute-start = (bf16[128,2176]{0,1:T(8,128)(2,1)S(1)}, bf16[128,2176]{0,1:T(8,128)(2,1)}, u32[]{:S(2)}, u32[]{:S(2)}) collective-permute-start(bf16[128,2176]{0,1:T(8,128)(2,1)S(1)} %get-tuple-element.53), channel_id=1, source_target_pairs={{0,4},{4,0},{1,5},{5,1},{2,6},{6,2},{3,7},{7,3},{8,12},{12,8},{9,1... | collective-permute-start | bytes 1671176 | tf_op jit(solution)/shard_map/ppermute | solution.py:21
  57.6 5.2 %collective-permute-start.1 = (bf16[64,256]{1,0:T(8,128)(2,1)S(1)}, bf16[64,256]{1,0:T(8,128)(2,1)S(1)}, u32[]{:S(2)}, u32[]{:S(2)}) collective-permute-start(bf16[64,256]{1,0:T(8,128)(2,1)S(1)} %slice.179), channel_id=1, source_target_pairs={{0,4},{4,8},{8,12},{12,16},{16,20},{20,24},{24,28},{28,32},{32,36}... | collective-permute-start | bytes 98312 | tf_op jit(solution)/shard_map/ppermute | solution.py:21
  64.5 4.4 %collective-permute-start.2 = (f32[64,256]{0,1:T(8,128)S(1)}, f32[64,256]{0,1:T(8,128)S(1)}, u32[]{:S(2)}, u32[]{:S(2)}) collective-permute-start(f32[64,256]{0,1:T(8,128)S(1)} %get-tuple-element.57), channel_id=1, source_target_pairs={{0,508},{4,0},{8,4},{12,8},{16,12},{20,16},{24,20},{28,24},{32,28}... | collective-permute-start | bytes 196616 | tf_op jit(solution)/shard_map/ppermute | solution.py:21
  70.5 26.7 %all-to-all-start.2 = ((bf16[128,2,2,256]{3,2,1,0:T(2,128)(2,1)}), bf16[128,2,2,256]{3,2,1,0:T(2,128)(2,1)S(1)}, u32[]{:S(2)}, u32[]{:S(2)}) async-start(bf16[128,2,2,256]{3,2,1,0:T(2,128)(2,1)} %reshape.325), calls=%async_computation.2 | async-start | bytes 524288 | tf_op jit(solution)/shard_map/all_to_all | solution.py:142

commit v14 on v10

--- a/solution.py
+++ b/solution.py
@@ -55,23 +55,14 @@
         jnp.int32
     )
     slot_block = jnp.zeros((tok_count, head_width), jnp.bfloat16).at[:, 0].set(
-        local_slot.astype(jnp.bfloat16)
+        (local_slot + 1).astype(jnp.bfloat16)
     )
     payload = jnp.concatenate([query, values, head_grad, slot_block], axis=1)
     buffer_ids = jnp.arange(peer_count * capacity, dtype=jnp.int32)
     to_buffer = (buffer_ids[:, None] == buffer_index[None, :]).astype(jnp.bfloat16)
     send_rows = jnp.dot(to_buffer, payload, preferred_element_type=jnp.float32).astype(jnp.bfloat16)
-    empty = (buffer_ids[:, None] * 0 + jnp.arange(head_width)[None, :]) == 0
-    used = jnp.sum(to_buffer.astype(jnp.float32), axis=1) > 0
-    send_rows = send_rows.at[:, 3 * head_width :].set(
-        jnp.where(
-            empty & ~used[:, None],
-            jnp.bfloat16(tok_count),
-            send_rows[:, 3 * head_width :],
-        )
-    )
     recv_rows = lax.all_to_all(send_rows, SEQ, split_axis=0, concat_axis=0, tiled=True)
-    recv_slots = recv_rows[:, 3 * head_width].astype(jnp.int32)
+    recv_slots = recv_rows[:, 3 * head_width].astype(jnp.int32) - 1
     to_sorted = (row_ids[:, None] == recv_slots[None, :]).astype(jnp.bfloat16)
     sorted_rows = jnp.dot(
         to_sorted, recv_rows[:, : 3 * head_width], preferred_element_type=jnp.float32

time: 135 us -> 135 us (level)
  no operation moved by 1% of the time
where the time goes in v14:
time: 135 us; the launch traced here: 133 us
  starting transfers between devices  41.5 us (31%)
  waiting for transfers between devices  40.1 us (30%)
  blocking collectives  34.1 us (25%)
  local copies, waits for them, and re-layouts  7.86 us (6%)
  other arithmetic  4.25 us (3%)
  matrix products  4.03 us (3%)
    all_to_all x1, blocking collectives, per_device(): lax.all_to_all(grads.astype(jnp.bfloat16), ('z', 'y'), 0, 0, tiled=True)  34.1 us
    all_to_all x1, starting transfers between devices, per_device(): lax.all_to_all(send_rows, SEQ, split_axis=0, concat_axis=0, tiled=True)  17.5 us
    all_to_all x1, waiting for transfers between devices, per_device(): lax.all_to_all(to_chip, SEQ, split_axis=0, concat_axis=0, tiled=True)  12.9 us
    all_to_all x1, waiting for transfers between devices, per_device(): lax.all_to_all(send_rows, SEQ, split_axis=0, concat_axis=0, tiled=True)  11.7 us
    all_to_all x1, starting transfers between devices, per_device(): gathered = lax.all_to_all(spread, 'head', 0, 0, tiled=True)  9.44 us
    all_to_all x1, starting transfers between devices, per_device(): lax.all_to_all(to_chip, SEQ, split_axis=0, concat_axis=0, tiled=True)  8.7 us
    ppermute x3, waiting for transfers between devices, shifted(): return lax.ppermute(value, axis, pairs)  8.37 us
    all_to_all x1, waiting for transfers between devices, per_device(): gathered = lax.all_to_all(spread, 'head', 0, 0, tiled=True)  7.17 us
  transfers between devices with their start and end apart: 6, of which 5 were waited for; matrix products, arithmetic and copies ran while one was open for 7% of the time, Pallas kernels for 0%

profile of v14, /device:TPU:6, one launch (start us, length us, event | category | flops | bytes accessed | tf_op | source)
XLA Modules:
  0.0 132.9 jit_solution(1822930568033678175)
XLA Ops:
  0.6 1.2 copy.36
  1.9 1.1 broadcast_in_dim.30
  3.0 9.4 %all-to-all-start = ((bf16[4,128,1024]{1,2,0:T(8,128)(2,1)}), bf16[4,128,1024]{1,2,0:T(8,128)(2,1)S(1)}, u32[]{:S(2)}, u32[]{:S(2)}) async-start(bf16[4,128,1024]{1,2,0:T(8,128)(2,1)} %broadcast_in_dim.30), calls=%async_computation | async-start | bytes 2097152 | tf_op jit(solution)/shard_map/all_to_all | solution.py:34
  12.6 0.7 compare_reduce_fusion
  13.4 0.7 broadcast_select_fusion
  14.1 7.2 %all-to-all-done = bf16[4,128,1024]{1,2,0:T(8,128)(2,1)S(1)} async-done(((bf16[4,128,1024]{1,2,0:T(8,128)(2,1)}), bf16[4,128,1024]{1,2,0:T(8,128)(2,1)S(1)}, u32[]{:S(2)}, u32[]{:S(2)}) %all-to-all-start) | async-done | bytes 1048608 | tf_op jit(solution)/shard_map/all_to_all | solution.py:34
  21.3 0.5 convolution_convert_fusion.6
  21.7 0.7 copy-done.1
  23.2 0.8 all_to_all.18
  24.0 17.5 %all-to-all-start.1 = ((bf16[128,2,512]{2,1,0:T(2,128)(2,1)}), bf16[128,2,512]{2,1,0:T(2,128)(2,1)S(1)}, u32[]{:S(2)}, u32[]{:S(2)}) async-start(bf16[128,2,512]{2,1,0:T(2,128)(2,1)} %all_to_all.18), calls=%async_computation.1 | async-start | bytes 524288 | tf_op jit(solution)/shard_map/all_to_all | solution.py:64
  41.5 0.7 broadcast_select_fusion.1
  42.6 1.9 %collective-permute-start = (bf16[128,2176]{0,1:T(8,128)(2,1)S(1)}, bf16[128,2176]{0,1:T(8,128)(2,1)}, u32[]{:S(2)}, u32[]{:S(2)}) collective-permute-start(bf16[128,2176]{0,1:T(8,128)(2,1)S(1)} %get-tuple-element.41), channel_id=1, source_target_pairs={{0,4},{4,0},{1,5},{5,1},{2,6},{6,2},{3,7},{7,3},{8,12},{12,8},{9,1... | collective-permute-start | bytes 1671176 | tf_op jit(solution)/shard_map/ppermute | solution.py:21
  44.5 11.7 %all-to-all-done.1 = bf16[128,2,512]{2,1,0:T(2,128)(2,1)S(1)} async-done(((bf16[128,2,512]{2,1,0:T(2,128)(2,1)}), bf16[128,2,512]{2,1,0:T(2,128)(2,1)S(1)}, u32[]{:S(2)}, u32[]{:S(2)}) %all-to-all-start.1) | async-done | bytes 262176 | tf_op jit(solution)/shard_map/all_to_all | solution.py:64
  57.2 2.0 %collective-permute-start.1 = (bf16[64,256]{1,0:T(8,128)(2,1)S(1)}, bf16[64,256]{1,0:T(8,128)(2,1)S(1)}, u32[]{:S(2)}, u32[]{:S(2)}) collective-permute-start(bf16[64,256]{1,0:T(8,128)(2,1)S(1)} %slice.157), channel_id=1, source_target_pairs={{0,4},{4,8},{8,12},{12,16},{16,20},{20,24},{24,28},{28,32},{32,36}... | collective-permute-start | bytes 98312 | tf_op jit(solution)/shard_map/ppermute | solution.py:21
  59.8 6.0 %collective-permute-done.1 = bf16[64,256]{1,0:T(8,128)(2,1)S(1)} collective-permute-done((bf16[64,256]{1,0:T(8,128)(2,1)S(1)}, bf16[64,256]{1,0:T(8,128)(2,1)S(1)}, u32[]{:S(2)}, u32[]{:S(2)}) %collective-permute-start.1) | collective-permute-done | bytes 32800 | tf_op jit(solution)/shard_map/ppermute | solution.py:21
  67.5 1.9 %collective-permute-start.2 = (f32[64,256]{0,1:T(8,128)S(1)}, f32[64,256]{0,1:T(8,128)S(1)}, u32[]{:S(2)}, u32[]{:S(2)}) collective-permute-start(f32[64,256]{0,1:T(8,128)S(1)} %get-tuple-element.45), channel_id=1, source_target_pairs={{0,508},{4,0},{8,4},{12,8},{16,12},{20,16},{24,20},{28,24},{32,28}... | collective-permute-start | bytes 196616 | tf_op jit(solution)/shard_map/ppermute | solution.py:21
  69.6 2.4 %collective-permute-done.2 = f32[64,256]{0,1:T(8,128)S(1)} collective-permute-done((f32[64,256]{0,1:T(8,128)S(1)}, f32[64,256]{0,1:T(8,128)S(1)}, u32[]{:S(2)}, u32[]{:S(2)}) %collective-permute-start.2) | collective-permute-done | bytes 65568 | tf_op jit(solution)/shard_map/ppermute | solution.py:21
  72.6 0.8 reshape.305
  73.4 8.7 %all-to-all-start.2 = ((bf16[128,2,2,256]{3,2,1,0:T(2,128)(2,1)}), bf16[128,2,2,256]{3,2,1,0:T(2,128)(2,1)S(1)}, u32[]{:S(2)}, u32[]{:S(2)}) async-start(bf16[128,2,2,256]{3,2,1,0:T(2,128)(2,1)} %reshape.305), calls=%async_computation.2 | async-start | bytes 524288 | tf_op jit(solution)/shard_map/all_to_all | solution.py:133
  82.2 1.1 slice.150
  83.3 0.7 fusion.60
  84.0 12.9 %all-to-all-done.2 = bf16[128,2,2,256]{3,2,1,0:T(2,128)(2,1)S(1)} async-done(((bf16[128,2,2,256]{3,2,1,0:T(2,128)(2,1)}), bf16[128,2,2,256]{3,2,1,0:T(2,128)(2,1)S(1)}, u32[]{:S(2)}, u32[]{:S(2)}) %all-to-all-start.2) | async-done | bytes 262176 | tf_op jit(solution)/shard_map/all_to_all | solution.py:133
  98.0 34.1 %all_to_all.27 = bf16[64,32,256]{2,1,0:T(8,128)(2,1)S(1)} all-to-all(bf16[64,32,256]{2,1,0:T(8,128)(2,1)S(1)} %bitcast.98), channel_id=1, replica_groups=mesh['z'=8,'y'=8,'c'=2,'head'=4] {'z','y'}, dimensions={0} | all-to-all | bytes 2097152 | tf_op jit(solution)/shard_map/all_to_all | solution.py:165
  132.3 0.6 fusion.82
  (63 shorter events, 6.6 us)
Async XLA Ops:
  0.6 20.6 %copy-start = (bf16[4096,128]{1,0:T(8,128)(2,1)S(1)}, bf16[4096,128]{1,0:T(8,128)(2,1)}, u32[]{:S(2)}) copy-start(bf16[4096,128]{1,0:T(8,128)(2,1)} %param.13) | copy-start | bytes 3145732
  3.0 9.4 %copy-start.2 = (bf16[128,128]{1,0:T(8,128)(2,1)S(1)}, bf16[128,128]{1,0:T(8,128)(2,1)}, u32[]{:S(2)}) copy-start(bf16[128,128]{1,0:T(8,128)(2,1)} %param.14) | copy-start | bytes 98308
  3.0 10.2 %copy-start.3 = (s32[1,128]{1,0:T(1,128)S(1)}, s32[1,128]{1,0:T(1,128)}, u32[]{:S(2)}) copy-start(s32[1,128]{1,0:T(1,128)} %param.15) | copy-start | bytes 1540
  3.0 18.3 %all-to-all-start = ((bf16[4,128,1024]{1,2,0:T(8,128)(2,1)}), bf16[4,128,1024]{1,2,0:T(8,128)(2,1)S(1)}, u32[]{:S(2)}, u32[]{:S(2)}) async-start(bf16[4,128,1024]{1,2,0:T(8,128)(2,1)} %broadcast_in_dim.30), calls=%async_computation | async-start | bytes 2097152 | tf_op jit(solution)/shard_map/all_to_all | solution.py:34
  21.3 1.2 copy-start.1
  24.0 32.2 %all-to-all-start.1 = ((bf16[128,2,512]{2,1,0:T(2,128)(2,1)}), bf16[128,2,512]{2,1,0:T(2,128)(2,1)S(1)}, u32[]{:S(2)}, u32[]{:S(2)}) async-start(bf16[128,2,512]{2,1,0:T(2,128)(2,1)} %all_to_all.18), calls=%async_computation.1 | async-start | bytes 524288 | tf_op jit(solution)/shard_map/all_to_all | solution.py:64
  42.6 39.6 %collective-permute-start = (bf16[128,2176]{0,1:T(8,128)(2,1)S(1)}, bf16[128,2176]{0,1:T(8,128)(2,1)}, u32[]{:S(2)}, u32[]{:S(2)}) collective-permute-start(bf16[128,2176]{0,1:T(8,128)(2,1)S(1)} %get-tuple-element.41), channel_id=1, source_target_pairs={{0,4},{4,0},{1,5},{5,1},{2,6},{6,2},{3,7},{7,3},{8,12},{12,8},{9,1... | collective-permute-start | bytes 1671176 | tf_op jit(solution)/shard_map/ppermute | solution.py:21
  57.2 8.6 %collective-permute-start.1 = (bf16[64,256]{1,0:T(8,128)(2,1)S(1)}, bf16[64,256]{1,0:T(8,128)(2,1)S(1)}, u32[]{:S(2)}, u32[]{:S(2)}) collective-permute-start(bf16[64,256]{1,0:T(8,128)(2,1)S(1)} %slice.157), channel_id=1, source_target_pairs={{0,4},{4,8},{8,12},{12,16},{16,20},{20,24},{24,28},{28,32},{32,36}... | collective-permute-start | bytes 98312 | tf_op jit(solution)/shard_map/ppermute | solution.py:21
  67.5 4.4 %collective-permute-start.2 = (f32[64,256]{0,1:T(8,128)S(1)}, f32[64,256]{0,1:T(8,128)S(1)}, u32[]{:S(2)}, u32[]{:S(2)}) collective-permute-start(f32[64,256]{0,1:T(8,128)S(1)} %get-tuple-element.45), channel_id=1, source_target_pairs={{0,508},{4,0},{8,4},{12,8},{16,12},{20,16},{24,20},{28,24},{32,28}... | collective-permute-start | bytes 196616 | tf_op jit(solution)/shard_map/ppermute | solution.py:21
  73.4 23.4 %all-to-all-start.2 = ((bf16[128,2,2,256]{3,2,1,0:T(2,128)(2,1)}), bf16[128,2,2,256]{3,2,1,0:T(2,128)(2,1)S(1)}, u32[]{:S(2)}, u32[]{:S(2)}) async-start(bf16[128,2,2,256]{3,2,1,0:T(2,128)(2,1)} %reshape.305), calls=%async_computation.2 | async-start | bytes 524288 | tf_op jit(solution)/shard_map/all_to_all | solution.py:133

commit v15 on v14

--- a/solution.py
+++ b/solution.py
@@ -40,8 +40,13 @@
     group_count = tok_count // GROUP
     tail_start = tok_count - GROUP
     scale_factor = 1.0 / math.sqrt(head_width)
-    query = jnp.dot(whole, shared_weight, preferred_element_type=jnp.float32).astype(jnp.bfloat16)
-    values = jnp.dot(whole, value_weight, preferred_element_type=jnp.float32).astype(jnp.bfloat16)
+    both = jnp.dot(
+        whole,
+        jnp.concatenate([shared_weight, value_weight], axis=1),
+        preferred_element_type=jnp.float32,
+    ).astype(jnp.bfloat16)
+    query = both[:, :head_width]
+    values = both[:, head_width:]
     slot_ids = sorted_slot[0]
     target = slot_ids // tok_count
     local_slot = slot_ids - target * tok_count

time: 135 us -> 133 us (0.985)
  local copies, waits for them, and re-layouts: 7.86 us -> 5.99 us
  waiting for transfers between devices: 40.1 us -> 41.8 us
    all_to_all x1, waiting for transfers between devices: 12.9 us -> 14.6 us  [per_device(): lax.all_to_all(to_chip, SEQ, split_axis=0, concat_axis=0, tiled=True)]
  transfers between devices with their start and end apart: 6 -> 6, of which waited for: 5 -> 5; matrix products, arithmetic and copies ran while one was open for 7% -> 6% of each run, Pallas kernels for 0% -> 0%
where the time goes in v15:
time: 133 us; the launch traced here: 132 us
  waiting for transfers between devices  41.8 us (31%)
  starting transfers between devices  41.5 us (31%)
  blocking collectives  34 us (26%)
  local copies, waits for them, and re-layouts  5.99 us (5%)
  matrix products  3.84 us (3%)
  other arithmetic  3.57 us (3%)
    all_to_all x1, blocking collectives, per_device(): lax.all_to_all(grads.astype(jnp.bfloat16), ('z', 'y'), 0, 0, tiled=True)  34 us
    all_to_all x1, starting transfers between devices, per_device(): lax.all_to_all(send_rows, SEQ, split_axis=0, concat_axis=0, tiled=True)  17.5 us
    all_to_all x1, waiting for transfers between devices, per_device(): lax.all_to_all(to_chip, SEQ, split_axis=0, concat_axis=0, tiled=True)  14.6 us
    all_to_all x1, waiting for transfers between devices, per_device(): lax.all_to_all(send_rows, SEQ, split_axis=0, concat_axis=0, tiled=True)  11.7 us
    all_to_all x1, starting transfers between devices, per_device(): gathered = lax.all_to_all(spread, 'head', 0, 0, tiled=True)  9.45 us
    all_to_all x1, starting transfers between devices, per_device(): lax.all_to_all(to_chip, SEQ, split_axis=0, concat_axis=0, tiled=True)  8.7 us
    ppermute x3, waiting for transfers between devices, shifted(): return lax.ppermute(value, axis, pairs)  8.37 us
    all_to_all x1, waiting for transfers between devices, per_device(): gathered = lax.all_to_all(spread, 'head', 0, 0, tiled=True)  7.17 us
  transfers between devices with their start and end apart: 6, of which 5 were waited for; matrix products, arithmetic and copies ran while one was open for 6% of the time, Pallas kernels for 0%

profile of v15, /device:TPU:6, one launch (start us, length us, event | category | flops | bytes accessed | tf_op | source)
XLA Modules:
  0.0 131.8 jit_solution(1165580087287386313)
XLA Ops:
  0.6 1.1 copy.36
  1.8 1.1 broadcast_in_dim.30
  2.9 9.5 %all-to-all-start = ((bf16[4,128,1024]{1,2,0:T(8,128)(2,1)}), bf16[4,128,1024]{1,2,0:T(8,128)(2,1)S(1)}, u32[]{:S(2)}, u32[]{:S(2)}) async-start(bf16[4,128,1024]{1,2,0:T(8,128)(2,1)} %broadcast_in_dim.30), calls=%async_computation | async-start | bytes 2097152 | tf_op jit(solution)/shard_map/all_to_all | solution.py:34
  12.5 0.7 compare_reduce_fusion
  13.3 0.7 broadcast_select_fusion
  14.0 7.2 %all-to-all-done = bf16[4,128,1024]{1,2,0:T(8,128)(2,1)S(1)} async-done(((bf16[4,128,1024]{1,2,0:T(8,128)(2,1)}), bf16[4,128,1024]{1,2,0:T(8,128)(2,1)S(1)}, u32[]{:S(2)}, u32[]{:S(2)}) %all-to-all-start) | async-done | bytes 1048608 | tf_op jit(solution)/shard_map/all_to_all | solution.py:34
  21.2 0.8 fusion.10
  22.2 0.8 all_to_all.18
  23.0 17.5 %all-to-all-start.1 = ((bf16[128,2,512]{2,1,0:T(2,128)(2,1)}), bf16[128,2,512]{2,1,0:T(2,128)(2,1)S(1)}, u32[]{:S(2)}, u32[]{:S(2)}) async-start(bf16[128,2,512]{2,1,0:T(2,128)(2,1)} %all_to_all.18), calls=%async_computation.1 | async-start | bytes 524288 | tf_op jit(solution)/shard_map/all_to_all | solution.py:69
  40.5 0.7 broadcast_select_fusion.1
  41.5 1.9 %collective-permute-start = (bf16[128,2176]{0,1:T(8,128)(2,1)S(1)}, bf16[128,2176]{0,1:T(8,128)(2,1)S(1)}, u32[]{:S(2)}, u32[]{:S(2)}) collective-permute-start(bf16[128,2176]{0,1:T(8,128)(2,1)S(1)} %get-tuple-element.41), channel_id=1, source_target_pairs={{0,4},{4,0},{1,5},{5,1},{2,6},{6,2},{3,7},{7,3},{8,12},{12,8},{9,1... | collective-permute-start | bytes 1671176 | tf_op jit(solution)/shard_map/ppermute | solution.py:21
  43.5 11.7 %all-to-all-done.1 = bf16[128,2,512]{2,1,0:T(2,128)(2,1)S(1)} async-done(((bf16[128,2,512]{2,1,0:T(2,128)(2,1)}), bf16[128,2,512]{2,1,0:T(2,128)(2,1)S(1)}, u32[]{:S(2)}, u32[]{:S(2)}) %all-to-all-start.1) | async-done | bytes 262176 | tf_op jit(solution)/shard_map/all_to_all | solution.py:69
  56.2 2.0 %collective-permute-start.1 = (bf16[64,256]{1,0:T(8,128)(2,1)S(1)}, bf16[64,256]{1,0:T(8,128)(2,1)S(1)}, u32[]{:S(2)}, u32[]{:S(2)}) collective-permute-start(bf16[64,256]{1,0:T(8,128)(2,1)S(1)} %slice.160), channel_id=1, source_target_pairs={{0,4},{4,8},{8,12},{12,16},{16,20},{20,24},{24,28},{28,32},{32,36}... | collective-permute-start | bytes 98312 | tf_op jit(solution)/shard_map/ppermute | solution.py:21
  58.8 6.0 %collective-permute-done.1 = bf16[64,256]{1,0:T(8,128)(2,1)S(1)} collective-permute-done((bf16[64,256]{1,0:T(8,128)(2,1)S(1)}, bf16[64,256]{1,0:T(8,128)(2,1)S(1)}, u32[]{:S(2)}, u32[]{:S(2)}) %collective-permute-start.1) | collective-permute-done | bytes 32800 | tf_op jit(solution)/shard_map/ppermute | solution.py:21
  65.0 0.3 fusion.92
  65.3 0.4 fusion.63
  66.5 1.9 %collective-permute-start.2 = (f32[64,256]{0,1:T(8,128)S(1)}, f32[64,256]{0,1:T(8,128)S(1)}, u32[]{:S(2)}, u32[]{:S(2)}) collective-permute-start(f32[64,256]{0,1:T(8,128)S(1)} %get-tuple-element.45), channel_id=1, source_target_pairs={{0,508},{4,0},{8,4},{12,8},{16,12},{20,16},{24,20},{28,24},{32,28}... | collective-permute-start | bytes 196616 | tf_op jit(solution)/shard_map/ppermute | solution.py:21
  68.5 2.4 %collective-permute-done.2 = f32[64,256]{0,1:T(8,128)S(1)} collective-permute-done((f32[64,256]{0,1:T(8,128)S(1)}, f32[64,256]{0,1:T(8,128)S(1)}, u32[]{:S(2)}, u32[]{:S(2)}) %collective-permute-start.2) | collective-permute-done | bytes 65568 | tf_op jit(solution)/shard_map/ppermute | solution.py:21
  71.6 0.8 reshape.305
  72.4 8.7 %all-to-all-start.2 = ((bf16[128,2,2,256]{3,2,1,0:T(2,128)(2,1)}), bf16[128,2,2,256]{3,2,1,0:T(2,128)(2,1)S(1)}, u32[]{:S(2)}, u32[]{:S(2)}) async-start(bf16[128,2,2,256]{3,2,1,0:T(2,128)(2,1)} %reshape.305), calls=%async_computation.2 | async-start | bytes 524288 | tf_op jit(solution)/shard_map/all_to_all | solution.py:138
  81.2 14.6 %all-to-all-done.2 = bf16[128,2,2,256]{3,2,1,0:T(2,128)(2,1)S(1)} async-done(((bf16[128,2,2,256]{3,2,1,0:T(2,128)(2,1)}), bf16[128,2,2,256]{3,2,1,0:T(2,128)(2,1)S(1)}, u32[]{:S(2)}, u32[]{:S(2)}) %all-to-all-start.2) | async-done | bytes 262176 | tf_op jit(solution)/shard_map/all_to_all | solution.py:138
  96.6 0.4 convolution_convert_fusion
  97.0 34.0 %all_to_all.27 = bf16[64,32,256]{2,1,0:T(8,128)(2,1)S(1)} all-to-all(bf16[64,32,256]{2,1,0:T(8,128)(2,1)S(1)} %bitcast.96), channel_id=1, replica_groups=mesh['z'=8,'y'=8,'c'=2,'head'=4] {'z','y'}, dimensions={0} | all-to-all | bytes 2097152 | tf_op jit(solution)/shard_map/all_to_all | solution.py:170
  131.2 0.6 fusion.91
  (62 shorter events, 5.0 us)
Async XLA Ops:
  2.9 9.5 %copy-start = (bf16[128,128]{1,0:T(8,128)(2,1)S(1)}, bf16[128,128]{1,0:T(8,128)(2,1)}, u32[]{:S(2)}) copy-start(bf16[128,128]{1,0:T(8,128)(2,1)} %param.14) | copy-start | bytes 98308
  2.9 10.2 %copy-start.1 = (s32[1,128]{1,0:T(1,128)S(1)}, s32[1,128]{1,0:T(1,128)}, u32[]{:S(2)}) copy-start(s32[1,128]{1,0:T(1,128)} %param.15) | copy-start | bytes 1540
  2.9 18.3 %copy-start.2 = (bf16[4096,128]{1,0:T(8,128)(2,1)S(1)}, bf16[4096,128]{1,0:T(8,128)(2,1)}, u32[]{:S(2)}) copy-start(bf16[4096,128]{1,0:T(8,128)(2,1)} %param.13) | copy-start | bytes 3145732
  2.9 18.3 %copy-start.3 = (bf16[4096,128]{1,0:T(8,128)(2,1)S(1)}, bf16[4096,128]{1,0:T(8,128)(2,1)}, u32[]{:S(2)}) copy-start(bf16[4096,128]{1,0:T(8,128)(2,1)} %param.12) | copy-start | bytes 3145732
  2.9 18.3 %all-to-all-start = ((bf16[4,128,1024]{1,2,0:T(8,128)(2,1)}), bf16[4,128,1024]{1,2,0:T(8,128)(2,1)S(1)}, u32[]{:S(2)}, u32[]{:S(2)}) async-start(bf16[4,128,1024]{1,2,0:T(8,128)(2,1)} %broadcast_in_dim.30), calls=%async_computation | async-start | bytes 2097152 | tf_op jit(solution)/shard_map/all_to_all | solution.py:34
  23.0 32.2 %all-to-all-start.1 = ((bf16[128,2,512]{2,1,0:T(2,128)(2,1)}), bf16[128,2,512]{2,1,0:T(2,128)(2,1)S(1)}, u32[]{:S(2)}, u32[]{:S(2)}) async-start(bf16[128,2,512]{2,1,0:T(2,128)(2,1)} %all_to_all.18), calls=%async_computation.1 | async-start | bytes 524288 | tf_op jit(solution)/shard_map/all_to_all | solution.py:69
  41.5 39.6 %collective-permute-start = (bf16[128,2176]{0,1:T(8,128)(2,1)S(1)}, bf16[128,2176]{0,1:T(8,128)(2,1)S(1)}, u32[]{:S(2)}, u32[]{:S(2)}) collective-permute-start(bf16[128,2176]{0,1:T(8,128)(2,1)S(1)} %get-tuple-element.41), channel_id=1, source_target_pairs={{0,4},{4,0},{1,5},{5,1},{2,6},{6,2},{3,7},{7,3},{8,12},{12,8},{9,1... | collective-permute-start | bytes 1671176 | tf_op jit(solution)/shard_map/ppermute | solution.py:21
  56.2 8.6 %collective-permute-start.1 = (bf16[64,256]{1,0:T(8,128)(2,1)S(1)}, bf16[64,256]{1,0:T(8,128)(2,1)S(1)}, u32[]{:S(2)}, u32[]{:S(2)}) collective-permute-start(bf16[64,256]{1,0:T(8,128)(2,1)S(1)} %slice.160), channel_id=1, source_target_pairs={{0,4},{4,8},{8,12},{12,16},{16,20},{20,24},{24,28},{28,32},{32,36}... | collective-permute-start | bytes 98312 | tf_op jit(solution)/shard_map/ppermute | solution.py:21
  66.5 4.4 %collective-permute-start.2 = (f32[64,256]{0,1:T(8,128)S(1)}, f32[64,256]{0,1:T(8,128)S(1)}, u32[]{:S(2)}, u32[]{:S(2)}) collective-permute-start(f32[64,256]{0,1:T(8,128)S(1)} %get-tuple-element.45), channel_id=1, source_target_pairs={{0,508},{4,0},{8,4},{12,8},{16,12},{20,16},{24,20},{28,24},{32,28}... | collective-permute-start | bytes 196616 | tf_op jit(solution)/shard_map/ppermute | solution.py:21
  72.4 23.4 %all-to-all-start.2 = ((bf16[128,2,2,256]{3,2,1,0:T(2,128)(2,1)}), bf16[128,2,2,256]{3,2,1,0:T(2,128)(2,1)S(1)}, u32[]{:S(2)}, u32[]{:S(2)}) async-start(bf16[128,2,2,256]{3,2,1,0:T(2,128)(2,1)} %reshape.305), calls=%async_computation.2 | async-start | bytes 524288 | tf_op jit(solution)/shard_map/all_to_all | solution.py:138
